TPU v7x, 128 devices: a whole 4x4x4 slice. The times are simulated.
128 devices in a mesh: tok: 16 (over y, x), head: 8 (over z, core).
Axes of the slice: x: 4, y: 4, z: 4, core: 2. Of those that a mesh axis runs over, the one named last changes fastest.
Arguments:
- tokens: bfloat16 [8192, 8192], P('tok', 'head'), may hold values from -60 to 60
- gain: bfloat16 [8192], P('head'), may hold values from 0.5 to 2
- w_query: bfloat16 [8192, 8, 512], P(('head', 'tok')), may hold values from -0.125 to 0.125
- w_key: bfloat16 [8192, 8, 128], P(('head', 'tok')), may hold values from -0.0625 to 0.0625
- w_value: bfloat16 [8192, 8, 128], P(('head', 'tok')), may hold values from -0.5 to 0.5
- group_ids: int32 [8192, 1], P('tok'), may hold values from 0 to 15; in each aligned block of 512 rows (0 to 511, 512 to 1023, ...) at most 64 rows name the same one
- key_pages: bfloat16 [1024, 128, 8, 128], P('tok', None, 'head'), may hold values from -42 to 42
- value_pages: bfloat16 [1024, 128, 8, 128], P('tok', None, 'head'), may hold values from -48 to 48
- page_table: int32 [16, 32], P('tok'), may hold values from 0 to 1023, as said below
Outputs:
- attention: bfloat16 [8192, 4096], P('tok', 'head')
Inputs may be any that keep to these rules, and one draw needn't show every extreme that they name: `group_ids`: among the 512 tokens of one index of tok (aligned blocks of rows), no group appears more than 64 times, a bound that some block reaches. `page_table`: row g lists 32 different pages, all in g * 64 to (g + 1) * 64 - 1, among them the first and the last page of that range.
All inputs are finite; a program needn't handle non-finite values.
Results may differ from a plain program's by a relative error of at most 0.0085.
The roundings to bfloat16 on the way count: a program that leaves them out, or rounds other values in their place, can miss the bound.
Values may be sent and summed in bfloat16 or wider, within the bound.
No kernel may reach another device: no remote copies, remote signals or barrier semaphores. Data moves between devices by JAX's collectives and lax.ppermute only.
A program may use at most 128 MiB of HBM per device.

v0:
```python
import math

import jax
import jax.numpy as jnp
from jax import lax
from jax.sharding import PartitionSpec as P

EPS = 1e-05
THETA = 10000.0


def rotate(values, positions):
    halfway = values.shape[-1] // 2
    frequency = jnp.exp(
        -math.log(THETA) * 2.0 * jnp.arange(halfway, dtype=jnp.float32) / values.shape[-1]
    )
    angles = positions.astype(jnp.float32)[:, None] * frequency[None, :]
    cosine = jnp.cos(angles)[:, None, :]
    sine_part = jnp.sin(angles)[:, None, :]
    leading = values[..., :halfway].astype(jnp.float32)
    trailing = values[..., halfway:].astype(jnp.float32)
    return jnp.concatenate(
        [leading * cosine - trailing * sine_part, trailing * cosine + leading * sine_part], axis=-1
    ).astype(jnp.bfloat16)


def attend(
    queries, query_rank, prefix_keys, prefix_values, new_keys, new_values, key_rank, key_live
):
    scaling = 1.0 / math.sqrt(queries.shape[-1])
    before = (
        jnp.einsum("bhd,pd->bhp", queries, prefix_keys, preferred_element_type=jnp.float32)
        * scaling
    )
    inside = (
        jnp.einsum("bhd,sd->bhs", queries, new_keys, preferred_element_type=jnp.float32) * scaling
    )
    allowed = key_live[None, :] & (key_rank[None, :] <= query_rank[:, None])
    inside = jnp.where(allowed[:, None, :], inside, -jnp.inf)
    highest = jnp.maximum(jnp.max(before, axis=-1), jnp.max(inside, axis=-1))
    expo_before = jnp.exp(before - highest[..., None])
    expo_inside = jnp.exp(inside - highest[..., None])
    totals = jnp.sum(expo_before, axis=-1) + jnp.sum(expo_inside, axis=-1)
    mixed = jnp.einsum(
        "bhp,pd->bhd",
        expo_before.astype(jnp.bfloat16),
        prefix_values,
        preferred_element_type=jnp.float32,
    )
    mixed = mixed + jnp.einsum(
        "bhs,sd->bhd",
        expo_inside.astype(jnp.bfloat16),
        new_values,
        preferred_element_type=jnp.float32,
    )
    return (mixed / totals[..., None]).astype(jnp.bfloat16)


def row_norm(tokens, gain, full_width):
    values_wide = tokens.astype(jnp.float32)
    squares = lax.psum(jnp.sum(values_wide * values_wide, axis=1), "head")
    factor = lax.rsqrt(squares / full_width + EPS)
    return (values_wide * factor[:, None] * gain.astype(jnp.float32)[None, :]).astype(jnp.bfloat16)


def body(tokens, gain, w_query, w_key, w_value, group_ids, key_pages, value_pages, page_table):
    row_count = tokens.shape[0]
    n_tok = lax.axis_size("tok")
    n_head = lax.axis_size("head")
    head_size = key_pages.shape[-1]
    query_width = w_query.shape[2]
    group_heads = query_width // head_size
    full_width = tokens.shape[1] * n_head
    capacity = 2 * row_count // n_tok
    normed = row_norm(tokens, gain, full_width)
    gathered = (
        lax.all_gather(w_query, "tok", axis=0, tiled=True),
        lax.all_gather(w_key, "tok", axis=0, tiled=True),
        lax.all_gather(w_value, "tok", axis=0, tiled=True),
    )
    group_count = row_count * lax.axis_size("head") // row_count
    results = []
    for weight in gathered:
        results.append(
            jnp.einsum("rd,dnc->nrc", normed, weight, preferred_element_type=jnp.float32)
        )
    joined = jnp.concatenate(results, axis=2)
    projected = lax.psum_scatter(
        joined.reshape(group_count * row_count, joined.shape[2]),
        "head",
        scatter_dimension=0,
        tiled=True,
    )
    projected_low = projected.astype(jnp.bfloat16)
    width_all = projected_low.shape[1]
    group_of = group_ids[:, 0]
    member = (group_of[:, None] == jnp.arange(n_tok, dtype=jnp.int32)[None, :]).astype(jnp.int32)
    local_rank = jnp.sum((jnp.cumsum(member, axis=0) - member) * member, axis=1)
    slot_index = group_of * capacity + local_rank
    outgoing = (
        jnp.zeros((n_tok * capacity, width_all), jnp.bfloat16).at[slot_index].set(projected_low)
    )
    marker = jnp.zeros((n_tok * capacity,), jnp.bfloat16).at[slot_index].set(1.0)
    arrived, arrived_marker = (
        lax.all_to_all(
            outgoing.reshape(n_tok, capacity, width_all),
            "tok",
            split_axis=0,
            concat_axis=0,
            tiled=True,
        ),
        lax.all_to_all(
            marker.reshape(n_tok, capacity), "tok", split_axis=0, concat_axis=0, tiled=True
        ),
    )
    slot_total = n_tok * capacity
    arrived = arrived.reshape(slot_total, width_all)
    live_count = (arrived_marker.reshape(slot_total) > 0).astype(jnp.int32)
    key_live = live_count > 0
    slot_rank = jnp.cumsum(live_count) - live_count
    prefix_length = page_table.shape[1] * key_pages.shape[1]
    positions = prefix_length + slot_rank
    rotated_queries = rotate(
        arrived[:, :query_width].reshape(slot_total, group_heads, head_size), positions
    )
    rotated_keys = rotate(
        arrived[:, query_width : query_width + head_size].reshape(slot_total, 1, head_size),
        positions,
    )[:, 0, :]
    slot_values = arrived[:, query_width + head_size :]
    local_pages = page_table[0] - lax.axis_index("tok") * key_pages.shape[0]
    prefix_keys = jnp.take(key_pages[:, :, 0, :], local_pages, axis=0).reshape(
        prefix_length, head_size
    )
    prefix_values = jnp.take(value_pages[:, :, 0, :], local_pages, axis=0).reshape(
        prefix_length, head_size
    )
    block_size = min(128, slot_total)

    def one_block(blocked):
        return attend(
            blocked[0],
            blocked[1],
            prefix_keys,
            prefix_values,
            rotated_keys,
            slot_values,
            slot_rank,
            key_live,
        )

    attended = lax.map(
        one_block,
        (
            rotated_queries.reshape(slot_total // block_size, block_size, group_heads, head_size),
            slot_rank.reshape(slot_total // block_size, block_size),
        ),
    )
    returned = lax.all_to_all(
        attended.reshape(n_tok, capacity, query_width),
        "tok",
        split_axis=0,
        concat_axis=0,
        tiled=True,
    )
    return returned.reshape(n_tok * capacity, query_width)[slot_index]


def solution(mesh):
    placed = (
        P("tok", "head"),
        P("head"),
        P(("head", "tok"), None, None),
        P(("head", "tok"), None, None),
        P(("head", "tok"), None, None),
        P("tok", None),
        P("tok", None, "head", None),
        P("tok", None, "head", None),
        P("tok", None),
    )
    return jax.shard_map(
        body, mesh=mesh, in_specs=placed, out_specs=P("tok", "head"), check_vma=False
    )
```

profile of v0, /device:TPU:32, one launch (start us, length us, event | category | flops | bytes accessed | tf_op | source)
XLA Modules:
  0.0 415.2 jit_solution(10881437984728749985)
XLA Ops:
  6.5 1.7 copy.34
  8.3 1.6 copy.33
  10.0 2.0 copy.32
  12.4 12.5 %psum.7 = f32[512]{0:T(512)S(1)} all-reduce(f32[512]{0:T(512)S(1)} %fusion.30), channel_id=1, replica_groups=mesh['tok'=16,'head'=8] {'head'}, use_global_device_ids=true, to_apply=%region_4.5 | all-reduce | flops 512 | bytes 4096 | tf_op jit(solution)/shard_map/psum | solution.py:61
  24.9 31.4 %all-gather.8.cloned.1.call-done = bf16[1024,8,128]{2,0,1:T(8,128)(2,1)} async-done(((bf16[64,8,128]{2,0,1:T(8,128)(2,1)}), bf16[1024,8,128]{2,0,1:T(8,128)(2,1)}) %all-gather.8.cloned.1.call-update) | async-done | bytes 2097168 | tf_op jit(solution)/shard_map/all_gather | solution.py:79
  56.3 4.3 %convolution_bitcast_fusion.1 = f32[8,512,128]{1,2,0:T(8,128)} fusion(bf16[1024,8,128]{2,0,1:T(8,128)(2,1)} %all-gather.8.cloned.1.call-done, bf16[512,1024]{1,0:T(8,128)(2,1)S(1)} %copy-done.4, f32[1024]{0:T(1024)S(1)} %convert_element_type.74, f32[512]{0:T(512)S(1)} %add_rsqrt_fusion), kind=kOutput, calls=%fused_computation.48 | convolution fusion | flops 1075838976 | bytes 5249024 | tf_op jit(solution)/shard_map/rd,dnc->nrc/dot_general | solution.py:85
  60.6 42.0 %all-gather.6.cloned.1.call-done = bf16[1024,8,128]{2,0,1:T(8,128)(2,1)} async-done(((bf16[64,8,128]{2,0,1:T(8,128)(2,1)}), bf16[1024,8,128]{2,0,1:T(8,128)(2,1)}) %all-gather.6.cloned.1.call-update) | async-done | bytes 2097168 | tf_op jit(solution)/shard_map/all_gather | solution.py:78
  102.6 4.3 %convolution_bitcast_fusion.2 = f32[8,512,128]{1,2,0:T(8,128)} fusion(bf16[1024,8,128]{2,0,1:T(8,128)(2,1)} %all-gather.6.cloned.1.call-done, bf16[512,1024]{1,0:T(8,128)(2,1)S(1)} %copy-done.4, f32[1024]{0:T(1024)S(1)} %convert_element_type.74, f32[512]{0:T(512)S(1)} %add_rsqrt_fusion), kind=kOutput, calls=%fused_computation.49 | convolution fusion | flops 1075838976 | bytes 5249024 | tf_op jit(solution)/shard_map/rd,dnc->nrc/dot_general | solution.py:85
  106.9 68.0 %all-gather.4.cloned.1.call-done = bf16[1024,8,512]{2,0,1:T(8,128)(2,1)} async-done(((bf16[64,8,512]{2,0,1:T(8,128)(2,1)}), bf16[1024,8,512]{2,0,1:T(8,128)(2,1)}) %all-gather.4.cloned.1.call-update) | async-done | bytes 8388624 | tf_op jit(solution)/shard_map/all_gather | solution.py:77
  174.9 7.5 %convolution_bitcast_fusion = f32[8,512,512]{1,2,0:T(8,128)S(1)} fusion(bf16[1024,8,512]{2,0,1:T(8,128)(2,1)} %all-gather.4.cloned.1.call-done, bf16[512,1024]{1,0:T(8,128)(2,1)S(1)} %copy-done.4, f32[1024]{0:T(1024)S(1)} %convert_element_type.74, f32[512]{0:T(512)S(1)} %add_rsqrt_fusion), kind=kOutput, calls=%fused_computation.42 | convolution fusion | flops 4297064448 | bytes 17831936 | tf_op jit(solution)/shard_map/rd,dnc->nrc/dot_general | solution.py:85
  182.4 6.9 %pad_maximum_fusion = f32[8,512,768]{1,2,0:T(8,128)} fusion(f32[8,512,128]{1,2,0:T(8,128)S(1)} %copy-done.2, f32[8,512,128]{1,2,0:T(8,128)S(1)} %copy-done.3, f32[8,512,512]{1,2,0:T(8,128)S(1)} %convolution_bitcast_fusion), kind=kLoop, calls=%fused_computation.41 | loop fusion | flops 6291456 | bytes 25165824 | tf_op jit(solution)/shard_map/concatenate | solution.py:87
  189.3 12.6 %copy.35 = f32[8,512,768]{2,1,0:T(8,128)} copy(f32[8,512,768]{1,2,0:T(8,128)} %pad_maximum_fusion) | data formatting | bytes 25165824 | tf_op jit(solution)/shard_map/concatenate | solution.py:87
  204.1 3.8 scatter_custom_fusion.1
  208.5 5.3 %all-to-all-start.1 = ((bf16[16,1,64]{2,1,0:T(2,128)(2,1)}), bf16[16,1,64]{2,1,0:T(2,128)(2,1)S(1)}, u32[]{:S(2)}, u32[]{:S(2)}) async-start(bf16[16,1,64]{2,1,0:T(2,128)(2,1)} %all_to_all.16), calls=%async_computation.2 | async-start | bytes 16384 | tf_op jit(solution)/shard_map/all_to_all | solution.py:112
  214.6 3.3 gather_fusion.2
  217.9 53.8 %reduce-scatter.2.cloned.1.call-done = f32[512,768]{1,0:T(8,128)} async-done(((f32[4096,768]{1,0:T(8,128)}), f32[512,768]{1,0:T(8,128)}) %reduce-scatter.2.cloned.1.call-update) | async-done | bytes 1572880 | tf_op jit(solution)/shard_map/reduce_scatter | solution.py:88
  271.7 4.6 %scatter_custom_fusion = bf16[1024,768]{1,0:T(8,128)(2,1)} fusion(s32[512]{0:T(512)S(1)} %bitcast.131, f32[512,768]{1,0:T(8,128)} %reduce-scatter.2.cloned.1.call-done, bf16[]{:T(256)} %constant.23.clone.1), kind=kCustom, calls=%fused_computation.62 | custom fusion | flops 393216 | bytes 3145730 | tf_op jit(solution)/shard_map/scatter | solution.py:101
  276.3 7.1 %all-to-all-start = ((bf16[16,64,768]{2,1,0:T(8,128)(2,1)}), bf16[16,64,768]{2,1,0:T(8,128)(2,1)}, u32[]{:S(2)}, u32[]{:S(2)}) async-start(bf16[16,64,768]{2,1,0:T(8,128)(2,1)} %bitcast.17), calls=%async_computation.1 | async-start | bytes 3145728 | tf_op jit(solution)/shard_map/all_to_all | solution.py:105
  285.8 1.7 multiply_cosine_fusion.1
  287.5 23.9 %all-to-all-done = bf16[16,64,768]{2,1,0:T(8,128)(2,1)} async-done(((bf16[16,64,768]{2,1,0:T(8,128)(2,1)}), bf16[16,64,768]{2,1,0:T(8,128)(2,1)}, u32[]{:S(2)}, u32[]{:S(2)}) %all-to-all-start) | async-done | bytes 1572896 | tf_op jit(solution)/shard_map/all_to_all | solution.py:105
  311.4 1.8 fusion.61
  314.5 3.1 fusion.50
  318.9 1.6 fusion.34
  321.8 1.7 copy.39
  324.8 57.1 %while.10 = (s32[]{:T(128)}, bf16[8,128,4,128]{3,2,1,0:T(4,128)(2,1)}, bf16[8,128,4,128]{3,1,2,0:T(8,128)(2,1)S(1)}, bf16[4096,128]{1,0:T(8,128)(2,1)S(1)}, pred...) while((s32[]{:T(128)}, ...), condition=%wide.region_15.17_spmd, body=%wide.region_10.16_spmd.sunk | while | flops 1365179392 | bytes 36869268 | solution.py:152
  327.5 1.5 fusion.82
  341.7 1.5 fusion.82
  348.9 1.5 fusion.82
  381.8 2.3 reshape.278
  384.1 3.7 all-to-all-start.2
  387.8 18.2 %all-to-all-done.2 = bf16[16,64,512]{2,1,0:T(8,128)(2,1)S(1)} async-done(((bf16[16,64,512]{2,1,0:T(8,128)(2,1)}), bf16[16,64,512]{2,1,0:T(8,128)(2,1)S(1)}, u32[]{:S(2)}, u32[]{:S(2)}) %all-to-all-start.2) | async-done | bytes 1048608 | tf_op jit(solution)/shard_map/all_to_all | solution.py:159
  406.0 2.6 gather_fusion
  (162 shorter events, 63.7 us)
Async XLA Ops:
  6.5 207.3 %copy-start = (bf16[64,128,1,128]{3,1,2,0:T(8,128)(2,1)S(1)}, bf16[64,128,1,128]{3,1,2,0:T(8,128)(2,1)}, u32[]{:S(2)}) copy-start(bf16[64,128,1,128]{3,1,2,0:T(8,128)(2,1)} %param.19) | copy-start | bytes 6291460
  6.5 5.5 %copy-start.7 = (bf16[1024]{0:T(1024)(128)(2,1)S(1)}, bf16[1024]{0:T(1024)(128)(2,1)}, u32[]{:S(2)}) copy-start(bf16[1024]{0:T(1024)(128)(2,1)} %param.14) | copy-start | bytes 6148
  6.5 5.5 %copy-start.4 = (bf16[512,1024]{1,0:T(8,128)(2,1)S(1)}, bf16[512,1024]{1,0:T(8,128)(2,1)}, u32[]{:S(2)}) copy-start(bf16[512,1024]{1,0:T(8,128)(2,1)} %param.13) | copy-start | bytes 3145732
  6.5 49.7 %all-gather.8.cloned.1.call-start = ((), (), s32[]{:S(2)}) async-start(), calls=%async_computation.6 | async-start | bytes 2228224 | tf_op jit(solution)/shard_map/all_gather | solution.py:79
  8.3 94.3 %all-gather.6.cloned.1.call-start = ((), (), s32[]{:S(2)}) async-start(), calls=%async_computation.5 | async-start | bytes 2228224 | tf_op jit(solution)/shard_map/all_gather | solution.py:78
  9.9 164.9 %all-gather.4.cloned.1.call-start = ((), (), s32[]{:S(2)}) async-start(), calls=%async_computation.4 | async-start | bytes 8912896 | tf_op jit(solution)/shard_map/all_gather | solution.py:77
  12.0 259.7 %reduce-scatter.2.cloned.1.call-start = ((), (), s32[]{:S(2)}) async-start(), calls=%async_computation.7 | async-start | bytes 14155776 | tf_op jit(solution)/shard_map/reduce_scatter | solution.py:88
  174.9 7.5 %copy-start.2 = (f32[8,512,128]{1,2,0:T(8,128)S(1)}, f32[8,512,128]{1,2,0:T(8,128)}, u32[]{:S(2)}) copy-start(f32[8,512,128]{1,2,0:T(8,128)} %convolution_bitcast_fusion.1) | copy-start | bytes 6291460
  174.9 7.6 %copy-start.3 = (f32[8,512,128]{1,2,0:T(8,128)S(1)}, f32[8,512,128]{1,2,0:T(8,128)}, u32[]{:S(2)}) copy-start(f32[8,512,128]{1,2,0:T(8,128)} %convolution_bitcast_fusion.2) | copy-start | bytes 6291460
  201.8 0.7 copy-start.6
  201.8 11.9 %copy-start.8 = (s32[1,32]{1,0:T(1,128)S(1)}, s32[1,32]{1,0:T(1,128)}, u32[]{:S(2)}) copy-start(s32[1,32]{1,0:T(1,128)} %param.21) | copy-start | bytes 388
  208.5 67.8 %all-to-all-start.1 = ((bf16[16,1,64]{2,1,0:T(2,128)(2,1)}), bf16[16,1,64]{2,1,0:T(2,128)(2,1)S(1)}, u32[]{:S(2)}, u32[]{:S(2)}) async-start(bf16[16,1,64]{2,1,0:T(2,128)(2,1)} %all_to_all.16), calls=%async_computation.2 | async-start | bytes 16384 | tf_op jit(solution)/shard_map/all_to_all | solution.py:112
  276.3 35.1 %all-to-all-start = ((bf16[16,64,768]{2,1,0:T(8,128)(2,1)}), bf16[16,64,768]{2,1,0:T(8,128)(2,1)}, u32[]{:S(2)}, u32[]{:S(2)}) async-start(bf16[16,64,768]{2,1,0:T(8,128)(2,1)} %bitcast.17), calls=%async_computation.1 | async-start | bytes 3145728 | tf_op jit(solution)/shard_map/all_to_all | solution.py:105
  329.0 1.5 copy-start.5
  336.1 1.5 copy-start.5
  343.2 1.5 copy-start.5
  350.4 1.5 copy-start.5
  357.5 1.5 copy-start.5
  364.6 1.5 copy-start.5
  371.8 1.5 copy-start.5
  378.9 1.5 copy-start.5
  384.1 21.9 %all-to-all-start.2 = ((bf16[16,64,512]{2,1,0:T(8,128)(2,1)}), bf16[16,64,512]{2,1,0:T(8,128)(2,1)S(1)}, u32[]{:S(2)}, u32[]{:S(2)}) async-start(bf16[16,64,512]{2,1,0:T(8,128)(2,1)} %reshape.278), calls=%async_computation.3 | async-start | bytes 2097152 | tf_op jit(solution)/shard_map/all_to_all | solution.py:159
  406.0 2.6 copy-start.1
Sparse Core Ops, SparseCore 0:
  9.5 46.7 all-gather.7
  58.4 44.1 all-gather.5
  104.8 70.0 all-gather.3
  202.0 69.6 reduce-scatter.1
where the time goes:
time: 416 us; the launch traced here: 415 us
  waiting for transfers between devices  237 us (57%)
  matrix products  48.6 us (12%)
  local copies, waits for them, and re-layouts  44.9 us (11%)
  other arithmetic  42 us (10%)
  starting transfers between devices  16.1 us (4%)
  between operations  13.4 us (3%)
  blocking collectives  12.5 us (3%)
    all_gather x1, waiting for transfers between devices, body(): lax.all_gather(w_query, 'tok', axis=0, tiled=True)  68 us
    reduce_scatter x1, waiting for transfers between devices, body(): lax.psum_scatter(joined.reshape(group_count * row_count, joined.shape[2])...  53.8 us
    all_gather x1, waiting for transfers between devices, body(): lax.all_gather(w_key, 'tok', axis=0, tiled=True)  42 us
    all_gather x1, waiting for transfers between devices, body(): lax.all_gather(w_value, 'tok', axis=0, tiled=True)  31.4 us
    all_to_all x1, waiting for transfers between devices, body(): lax.all_to_all(outgoing.reshape(n_tok, capacity, width_all), 'tok', split...  23.9 us
    all_to_all x1, waiting for transfers between devices, body(): lax.all_to_all(attended.reshape(n_tok, capacity, query_width), 'tok', spl...  18.2 us
    reduce_sum x16, other arithmetic, attend(): totals = jnp.sum(expo_before, axis=-1) + jnp.sum(expo_inside, axis=-1)  16.8 us
    dot_general x3, matrix products, body(): jnp.einsum('rd,dnc->nrc', normed, weight, preferred_element_type=jnp.floa...  16.1 us
  transfers between devices with their start and end apart: 7, of which 6 were waited for; matrix products, arithmetic and copies ran while one was open for 7% of the time, Pallas kernels for 0%

commit v1 on v0

--- a/solution.py
+++ b/solution.py
@@ -73,18 +73,10 @@
     full_width = tokens.shape[1] * n_head
     capacity = 2 * row_count // n_tok
     normed = row_norm(tokens, gain, full_width)
-    gathered = (
-        lax.all_gather(w_query, "tok", axis=0, tiled=True),
-        lax.all_gather(w_key, "tok", axis=0, tiled=True),
-        lax.all_gather(w_value, "tok", axis=0, tiled=True),
-    )
+    weights_local = jnp.concatenate([w_query, w_key, w_value], axis=2)
+    gathered = lax.all_gather(weights_local, "tok", axis=0, tiled=True)
     group_count = row_count * lax.axis_size("head") // row_count
-    results = []
-    for weight in gathered:
-        results.append(
-            jnp.einsum("rd,dnc->nrc", normed, weight, preferred_element_type=jnp.float32)
-        )
-    joined = jnp.concatenate(results, axis=2)
+    joined = jnp.einsum("rd,dnc->nrc", normed, gathered, preferred_element_type=jnp.float32)
     projected = lax.psum_scatter(
         joined.reshape(group_count * row_count, joined.shape[2]),
         "head",
@@ -100,22 +92,22 @@
     outgoing = (
         jnp.zeros((n_tok * capacity, width_all), jnp.bfloat16).at[slot_index].set(projected_low)
     )
-    marker = jnp.zeros((n_tok * capacity,), jnp.bfloat16).at[slot_index].set(1.0)
-    arrived, arrived_marker = (
-        lax.all_to_all(
-            outgoing.reshape(n_tok, capacity, width_all),
-            "tok",
-            split_axis=0,
-            concat_axis=0,
-            tiled=True,
-        ),
-        lax.all_to_all(
-            marker.reshape(n_tok, capacity), "tok", split_axis=0, concat_axis=0, tiled=True
-        ),
+    arrived = lax.all_to_all(
+        outgoing.reshape(n_tok, capacity, width_all),
+        "tok",
+        split_axis=0,
+        concat_axis=0,
+        tiled=True,
+    )
+    all_groups = lax.all_gather(group_of, "tok", axis=0, tiled=True).reshape(n_tok, row_count)
+    block_counts = jnp.sum(
+        (all_groups == lax.axis_index("tok")).astype(jnp.int32), axis=1
     )
     slot_total = n_tok * capacity
     arrived = arrived.reshape(slot_total, width_all)
-    live_count = (arrived_marker.reshape(slot_total) > 0).astype(jnp.int32)
+    live_count = (
+        jnp.arange(capacity, dtype=jnp.int32)[None, :] < block_counts[:, None]
+    ).astype(jnp.int32).reshape(slot_total)
     key_live = live_count > 0
     slot_rank = jnp.cumsum(live_count) - live_count
     prefix_length = page_table.shape[1] * key_pages.shape[1]

time: 416 us -> 351 us (0.84)
  waiting for transfers between devices: 237 us -> 159 us
  blocking collectives: 12.5 us -> 35.5 us
  local copies, waits for them, and re-layouts: 44.9 us -> 30.1 us
  matrix products: 48.6 us -> 62.2 us
  starting transfers between devices: 16.1 us -> 10.9 us
    all_gather x3 -> x1, waiting for transfers between devices: 141 us -> 78.9 us  [body(): gathered = lax.all_gather(weights_local, 'tok', axis=0, tiled=True)]
    all_gather x0 -> x1, blocking collectives: none -> 23 us  [body(): lax.all_gather(group_of, 'tok', axis=0, tiled=True)]
    concatenate x1 -> x0, local copies, waits for them, and re-layouts: 12.6 us -> none  [body(): joined = jnp.concatenate(results, axis=2)]
    reduce_scatter x1, waiting for transfers between devices: 53.8 us -> 43.5 us  [body(): lax.psum_scatter(joined.reshape(group_count * row_count, joined.shape[2])...]
    dot_general x8, matrix products: 4.52 us -> 12.5 us  [attend(): jnp.einsum('bhd,sd->bhs', queries, new_keys, preferred_element_type=jnp.f...]
    dot_general x8, matrix products: 10.7 us -> 18 us  [attend(): jnp.einsum('bhd,pd->bhp', queries, prefix_keys, preferred_element_type=jn...]
    concatenate x1, other arithmetic: 6.86 us -> 0.95 us  [body(): weights_local = jnp.concatenate([w_query, w_key, w_value], axis=2)]
    all_to_all x1, waiting for transfers between devices: 23.9 us -> 18.2 us  [body(): lax.all_to_all(outgoing.reshape(n_tok, capacity, width_all), 'tok', split...]
  transfers between devices with their start and end apart: 7 -> 4, of which waited for: 6 -> 4; matrix products, arithmetic and copies ran while one was open for 7% -> 4% of each run, Pallas kernels for 0% -> 0%
where the time goes in v1:
time: 351 us; the launch traced here: 350 us
  waiting for transfers between devices  159 us (45%)
  matrix products  62.2 us (18%)
  other arithmetic  38.3 us (11%)
  blocking collectives  35.5 us (10%)
  local copies, waits for them, and re-layouts  30.1 us (9%)
  between operations  13.6 us (4%)
  starting transfers between devices  10.9 us (3%)
    all_gather x1, waiting for transfers between devices, body(): gathered = lax.all_gather(weights_local, 'tok', axis=0, tiled=True)  78.9 us
    reduce_scatter x1, waiting for transfers between devices, body(): lax.psum_scatter(joined.reshape(group_count * row_count, joined.shape[2])...  43.5 us
    all_gather x1, blocking collectives, body(): lax.all_gather(group_of, 'tok', axis=0, tiled=True)  23 us
    all_to_all x1, waiting for transfers between devices, body(): lax.all_to_all(attended.reshape(n_tok, capacity, query_width), 'tok', spl...  18.2 us
    all_to_all x1, waiting for transfers between devices, body(): lax.all_to_all(outgoing.reshape(n_tok, capacity, width_all), 'tok', split...  18.2 us
    dot_general x8, matrix products, attend(): jnp.einsum('bhd,pd->bhp', queries, prefix_keys, preferred_element_type=jn...  18 us
    reduce_sum x16, other arithmetic, attend(): totals = jnp.sum(expo_before, axis=-1) + jnp.sum(expo_inside, axis=-1)  16.8 us
    dot_general x1, matrix products, body(): jnp.einsum('rd,dnc->nrc', normed, gathered, preferred_element_type=jnp.fl...  14.4 us
  transfers between devices with their start and end apart: 4, of which 4 were waited for; matrix products, arithmetic and copies ran while one was open for 4% of the time, Pallas kernels for 0%

profile of v1, /device:TPU:32, one launch (start us, length us, event | category | flops | bytes accessed | tf_op | source)
XLA Modules:
  0.0 349.9 jit_solution(17621018906772747158)
XLA Ops:
  11.1 12.5 %psum.7 = f32[512]{0:T(512)S(1)} all-reduce(f32[512]{0:T(512)S(1)} %fusion.33), channel_id=1, replica_groups=mesh['tok'=16,'head'=8] {'head'}, use_global_device_ids=true, to_apply=%region_4.5 | all-reduce | flops 512 | bytes 4096 | tf_op jit(solution)/shard_map/psum | solution.py:61
  23.6 78.9 %all-gather.3.cloned.1.call-done = bf16[1024,8,768]{2,0,1:T(8,128)(2,1)} async-done(((bf16[64,8,768]{2,0,1:T(8,128)(2,1)}), bf16[1024,8,768]{2,0,1:T(8,128)(2,1)}) %all-gather.3.cloned.1.call-update) | async-done | bytes 12582928 | tf_op jit(solution)/shard_map/all_gather | solution.py:77
  102.5 14.4 %fusion.41 = f32[8,768,512]{1,2,0:T(8,128)} fusion(bf16[1024,8,768]{2,0,1:T(8,128)(2,1)} %all-gather.3.cloned.1.call-done, bf16[512,1024]{1,0:T(8,128)(2,1)S(1)} %copy-done.2, f32[1024]{0:T(1024)S(1)} %convert_element_type.78, f32[512]{0:T(512)S(1)} %add_rsqrt_fusion), kind=kOutput, calls=%fused_computation.58 | convolution fusion | flops 6444548096 | bytes 26220544 | tf_op jit(solution)/shard_map/rd,dnc->nrc/dot_general | solution.py:79
  117.6 23.0 %all-gather = s32[8192,1]{0,1:T(1,128)S(1)} all-gather(s32[512,1]{0,1:T(1,128)S(1)} %copy-done.4), channel_id=2, replica_groups=mesh['tok'=16,'head'=8] {'tok'}, dimensions={0}, use_global_device_ids=true | all-gather | bytes 34816 | tf_op jit(solution)/shard_map/all_gather | solution.py:102
  143.2 43.5 %reduce-scatter.2.cloned.1.call-done = f32[512,768]{1,0:T(8,128)} async-done(((f32[4096,768]{1,0:T(8,128)}), f32[512,768]{1,0:T(8,128)}) %reduce-scatter.2.cloned.1.call-update) | async-done | bytes 1572880 | tf_op jit(solution)/shard_map/reduce_scatter | solution.py:80
  186.7 4.6 %scatter_custom_fusion = bf16[1024,768]{1,0:T(8,128)(2,1)} fusion(s32[512]{0:T(512)S(1)} %bitcast.121, f32[512,768]{1,0:T(8,128)} %reduce-scatter.2.cloned.1.call-done, bf16[]{:T(256)} %constant.32.clone.1), kind=kCustom, calls=%fused_computation.65 | custom fusion | flops 393216 | bytes 3145730 | tf_op jit(solution)/shard_map/scatter | solution.py:93
  191.4 7.2 %all-to-all-start = ((bf16[16,64,768]{2,1,0:T(8,128)(2,1)}), bf16[16,64,768]{2,1,0:T(8,128)(2,1)}, u32[]{:S(2)}, u32[]{:S(2)}) async-start(bf16[16,64,768]{2,1,0:T(8,128)(2,1)} %bitcast.112), calls=%async_computation.1 | async-start | bytes 3145728 | tf_op jit(solution)/shard_map/all_to_all | solution.py:95
  198.7 1.7 gather_fusion.1
  200.3 3.2 gather_fusion.2
  203.8 1.7 multiply_cosine_fusion.1
  205.6 2.8 broadcast_select_fusion
  208.4 18.2 %all-to-all-done = bf16[16,64,768]{2,1,0:T(8,128)(2,1)} async-done(((bf16[16,64,768]{2,1,0:T(8,128)(2,1)}), bf16[16,64,768]{2,1,0:T(8,128)(2,1)}, u32[]{:S(2)}, u32[]{:S(2)}) %all-to-all-start) | async-done | bytes 1572896 | tf_op jit(solution)/shard_map/all_to_all | solution.py:95
  226.6 1.8 fusion.64
  228.4 2.3 slice.52
  230.6 3.1 fusion.57
  233.7 2.3 copy.21
  236.0 1.6 fusion.37
  239.0 2.4 copy.19
  242.6 73.7 %while.11 = (s32[]{:T(128)}, bf16[8,128,4,128]{3,2,1,0:T(4,128)(2,1)}, bf16[8,128,4,128]{3,1,2,0:T(8,128)(2,1)}, bf16[4096,128]{1,0:T(8,128)(2,1)}, s32[1024]{0:...) while((s32[]{:T(128)}, ...), condition=%wide.region_15.17_spmd.clone, body=%wide.region_10.16_spmd.clone.sunk | while | flops 1365182464 | bytes 41082088 | solution.py:144
  244.5 2.3 multiply_reduce_fusion.2
  253.7 2.3 multiply_reduce_fusion.2
  262.9 2.3 multiply_reduce_fusion.2
  272.1 2.3 multiply_reduce_fusion.2
  279.8 1.6 fusion.83
  281.3 2.3 multiply_reduce_fusion.2
  290.5 2.3 multiply_reduce_fusion.2
  299.8 2.3 multiply_reduce_fusion.2
  309.0 2.3 multiply_reduce_fusion.2
  316.3 2.3 reshape.284
  318.6 3.7 %all-to-all-start.1 = ((bf16[16,64,512]{2,1,0:T(8,128)(2,1)}), bf16[16,64,512]{2,1,0:T(8,128)(2,1)S(1)}, u32[]{:S(2)}, u32[]{:S(2)}) async-start(bf16[16,64,512]{2,1,0:T(8,128)(2,1)} %reshape.284), calls=%async_computation.2 | async-start | bytes 2097152 | tf_op jit(solution)/shard_map/all_to_all | solution.py:151
  322.2 18.2 %all-to-all-done.1 = bf16[16,64,512]{2,1,0:T(8,128)(2,1)S(1)} async-done(((bf16[16,64,512]{2,1,0:T(8,128)(2,1)}), bf16[16,64,512]{2,1,0:T(8,128)(2,1)S(1)}, u32[]{:S(2)}, u32[]{:S(2)}) %all-to-all-start.1) | async-done | bytes 1048608 | tf_op jit(solution)/shard_map/all_to_all | solution.py:151
  340.5 2.6 gather_fusion
  (189 shorter events, 64.3 us)
Async XLA Ops:
  6.5 192.1 %copy-start = (bf16[64,128,1,128]{3,1,2,0:T(8,128)(2,1)S(1)}, bf16[64,128,1,128]{3,1,2,0:T(8,128)(2,1)}, u32[]{:S(2)}) copy-start(bf16[64,128,1,128]{3,1,2,0:T(8,128)(2,1)} %param.19) | copy-start | bytes 6291460
  6.5 4.2 %copy-start.5 = (bf16[1024]{0:T(1024)(128)(2,1)S(1)}, bf16[1024]{0:T(1024)(128)(2,1)}, u32[]{:S(2)}) copy-start(bf16[1024]{0:T(1024)(128)(2,1)} %param.14) | copy-start | bytes 6148
  6.5 4.3 %copy-start.2 = (bf16[512,1024]{1,0:T(8,128)(2,1)S(1)}, bf16[512,1024]{1,0:T(8,128)(2,1)}, u32[]{:S(2)}) copy-start(bf16[512,1024]{1,0:T(8,128)(2,1)} %param.13) | copy-start | bytes 3145732
  6.5 96.0 %all-gather.3.cloned.1.call-start = ((), (), s32[]{:S(2)}) async-start(), calls=%async_computation.3 | async-start | bytes 13369344 | tf_op jit(solution)/shard_map/all_gather | solution.py:77
  10.7 176.0 %reduce-scatter.2.cloned.1.call-start = ((), (), s32[]{:S(2)}) async-start(), calls=%async_computation.4 | async-start | bytes 14155776 | tf_op jit(solution)/shard_map/reduce_scatter | solution.py:80
  116.9 0.7 copy-start.4
  191.4 7.2 %copy-start.6 = (s32[1,32]{1,0:T(1,128)S(1)}, s32[1,32]{1,0:T(1,128)}, u32[]{:S(2)}) copy-start(s32[1,32]{1,0:T(1,128)} %param.21) | copy-start | bytes 388
  191.4 35.2 %all-to-all-start = ((bf16[16,64,768]{2,1,0:T(8,128)(2,1)}), bf16[16,64,768]{2,1,0:T(8,128)(2,1)}, u32[]{:S(2)}, u32[]{:S(2)}) async-start(bf16[16,64,768]{2,1,0:T(8,128)(2,1)} %bitcast.112), calls=%async_computation.1 | async-start | bytes 3145728 | tf_op jit(solution)/shard_map/all_to_all | solution.py:95
  242.8 1.7 copy-start.1
  248.9 1.5 copy-start.3
  252.0 1.7 copy-start.1
  258.1 1.5 copy-start.3
  261.2 1.7 copy-start.1
  267.3 1.5 copy-start.3
  270.4 1.7 copy-start.1
  276.5 1.5 copy-start.3
  279.6 1.7 copy-start.1
  285.7 1.5 copy-start.3
  288.8 1.7 copy-start.1
  294.9 1.5 copy-start.3
  298.0 1.7 copy-start.1
  304.1 1.5 copy-start.3
  307.2 1.7 copy-start.1
  313.3 1.5 copy-start.3
  318.6 21.9 %all-to-all-start.1 = ((bf16[16,64,512]{2,1,0:T(8,128)(2,1)}), bf16[16,64,512]{2,1,0:T(8,128)(2,1)S(1)}, u32[]{:S(2)}, u32[]{:S(2)}) async-start(bf16[16,64,512]{2,1,0:T(8,128)(2,1)} %reshape.284), calls=%async_computation.2 | async-start | bytes 2097152 | tf_op jit(solution)/shard_map/all_to_all | solution.py:151
Sparse Core Ops, SparseCore 0:
  10.9 91.6 all-gather.2
  117.1 69.6 reduce-scatter.1

commit v2 on v1

--- a/solution.py
+++ b/solution.py
@@ -89,20 +89,17 @@
     member = (group_of[:, None] == jnp.arange(n_tok, dtype=jnp.int32)[None, :]).astype(jnp.int32)
     local_rank = jnp.sum((jnp.cumsum(member, axis=0) - member) * member, axis=1)
     slot_index = group_of * capacity + local_rank
+    counts_local = jnp.sum(member, axis=0).astype(jnp.bfloat16)
     outgoing = (
         jnp.zeros((n_tok * capacity, width_all), jnp.bfloat16).at[slot_index].set(projected_low)
     )
-    arrived = lax.all_to_all(
-        outgoing.reshape(n_tok, capacity, width_all),
-        "tok",
-        split_axis=0,
-        concat_axis=0,
-        tiled=True,
+    count_rows = jnp.broadcast_to(counts_local[:, None, None], (n_tok, 16, width_all))
+    outgoing = jnp.concatenate(
+        [outgoing.reshape(n_tok, capacity, width_all), count_rows], axis=1
     )
-    all_groups = lax.all_gather(group_of, "tok", axis=0, tiled=True).reshape(n_tok, row_count)
-    block_counts = jnp.sum(
-        (all_groups == lax.axis_index("tok")).astype(jnp.int32), axis=1
-    )
+    arrived_all = lax.all_to_all(outgoing, "tok", split_axis=0, concat_axis=0, tiled=True)
+    block_counts = arrived_all[:, capacity, 0].astype(jnp.int32)
+    arrived = arrived_all[:, :capacity, :]
     slot_total = n_tok * capacity
     arrived = arrived.reshape(slot_total, width_all)
     live_count = (

time: 351 us -> 344 us (0.980)
  waiting for transfers between devices: 159 us -> 193 us
  blocking collectives: 35.5 us -> 12.5 us
  matrix products: 62.2 us -> 46.8 us
  local copies, waits for them, and re-layouts: 30.1 us -> 26 us
    reduce_scatter x1, waiting for transfers between devices: 43.5 us -> 67.6 us  [body(): lax.psum_scatter(joined.reshape(group_count * row_count, joined.shape[2])...]
    all_gather x1 -> x0, blocking collectives: 23 us -> none  [body(): lax.all_gather(group_of, 'tok', axis=0, tiled=True)]
    all_to_all x1, waiting for transfers between devices: 18.2 us -> 27.9 us  [body(): lax.all_to_all(outgoing, 'tok', split_axis=0, concat_axis=0, tiled=True)]
    dot_general x8, matrix products: 12.5 us -> 4.52 us  [attend(): jnp.einsum('bhd,sd->bhs', queries, new_keys, preferred_element_type=jnp.f...]
    dot_general x8, matrix products: 18 us -> 10.7 us  [attend(): jnp.einsum('bhd,pd->bhp', queries, prefix_keys, preferred_element_type=jn...]
  transfers between devices with their start and end apart: 4 -> 4, of which waited for: 4 -> 4; matrix products, arithmetic and copies ran while one was open for 4% -> 2% of each run, Pallas kernels for 0% -> 0%
where the time goes in v2:
time: 344 us
  waiting for transfers between devices  193 us (56%)
  matrix products  46.8 us (14%)
  other arithmetic  40.8 us (12%)
  local copies, waits for them, and re-layouts  26 us (8%)
  between operations  13.6 us (4%)
  blocking collectives  12.5 us (4%)
  starting transfers between devices  10.9 us (3%)
    all_gather x1, waiting for transfers between devices, body(): gathered = lax.all_gather(weights_local, 'tok', axis=0, tiled=True)  78.9 us
    reduce_scatter x1, waiting for transfers between devices, body(): lax.psum_scatter(joined.reshape(group_count * row_count, joined.shape[2])...  67.6 us
    all_to_all x1, waiting for transfers between devices, body(): lax.all_to_all(outgoing, 'tok', split_axis=0, concat_axis=0, tiled=True)  27.9 us
    all_to_all x1, waiting for transfers between devices, body(): lax.all_to_all(attended.reshape(n_tok, capacity, query_width), 'tok', spl...  18.2 us
    reduce_sum x16, other arithmetic, attend(): totals = jnp.sum(expo_before, axis=-1) + jnp.sum(expo_inside, axis=-1)  16.8 us
    dot_general x1, matrix products, body(): jnp.einsum('rd,dnc->nrc', normed, gathered, preferred_element_type=jnp.fl...  14.4 us
    psum x1, blocking collectives, row_norm(): squares = lax.psum(jnp.sum(values_wide * values_wide, axis=1), 'head')  12.5 us
    dot_general x8, matrix products, attend(): jnp.einsum('bhp,pd->bhd', expo_before.astype(jnp.bfloat16), prefix_values...  11.8 us
  transfers between devices with their start and end apart: 4, of which 4 were waited for; matrix products, arithmetic and copies ran while one was open for 2% of the time, Pallas kernels for 0%

profile of v2, /device:TPU:32, one launch (start us, length us, event | category | flops | bytes accessed | tf_op | source)
XLA Modules:
  0.0 343.7 jit_solution(11092186876331091009)
XLA Ops:
  11.1 12.5 %psum.7 = f32[512]{0:T(512)S(1)} all-reduce(f32[512]{0:T(512)S(1)} %fusion.33), channel_id=1, replica_groups=mesh['tok'=16,'head'=8] {'head'}, use_global_device_ids=true, to_apply=%region_4.5 | all-reduce | flops 512 | bytes 4096 | tf_op jit(solution)/shard_map/psum | solution.py:61
  23.6 78.9 %all-gather.2.cloned.1.call-done = bf16[1024,8,768]{2,0,1:T(8,128)(2,1)} async-done(((bf16[64,8,768]{2,0,1:T(8,128)(2,1)}), bf16[1024,8,768]{2,0,1:T(8,128)(2,1)}) %all-gather.2.cloned.1.call-update) | async-done | bytes 12582928 | tf_op jit(solution)/shard_map/all_gather | solution.py:77
  102.5 14.4 %fusion.41 = f32[8,768,512]{1,2,0:T(8,128)} fusion(bf16[1024,8,768]{2,0,1:T(8,128)(2,1)} %all-gather.2.cloned.1.call-done, bf16[512,1024]{1,0:T(8,128)(2,1)S(1)} %copy-done.3, f32[1024]{0:T(1024)S(1)} %convert_element_type.95, f32[512]{0:T(512)S(1)} %add_rsqrt_fusion), kind=kOutput, calls=%fused_computation.59 | convolution fusion | flops 6444548096 | bytes 26220544 | tf_op jit(solution)/shard_map/rd,dnc->nrc/dot_general | solution.py:79
  119.2 67.6 %reduce-scatter.2.cloned.1.call-done = f32[512,768]{1,0:T(8,128)} async-done(((f32[4096,768]{1,0:T(8,128)}), f32[512,768]{1,0:T(8,128)}) %reduce-scatter.2.cloned.1.call-update) | async-done | bytes 1572880 | tf_op jit(solution)/shard_map/reduce_scatter | solution.py:80
  186.7 4.6 %scatter_custom_fusion = bf16[1024,768]{1,0:T(8,128)(2,1)} fusion(s32[512]{0:T(512)S(1)} %bitcast.115, f32[512,768]{1,0:T(8,128)} %reduce-scatter.2.cloned.1.call-done, bf16[]{:T(256)} %constant.32.clone.1), kind=kCustom, calls=%fused_computation.66 | custom fusion | flops 393216 | bytes 3145730 | tf_op jit(solution)/shard_map/scatter | solution.py:94
  191.5 2.8 pad_maximum_fusion
  194.3 7.2 %all-to-all-start = ((bf16[16,80,768]{2,1,0:T(8,128)(2,1)}), bf16[16,80,768]{2,1,0:T(8,128)(2,1)}, u32[]{:S(2)}, u32[]{:S(2)}) async-start(bf16[16,80,768]{2,1,0:T(8,128)(2,1)} %pad_maximum_fusion), calls=%async_computation.1 | async-start | bytes 3932160 | tf_op jit(solution)/shard_map/all_to_all | solution.py:100
  202.4 3.3 gather_fusion.2
  207.2 27.9 %all-to-all-done = bf16[16,80,768]{2,1,0:T(8,128)(2,1)} async-done(((bf16[16,80,768]{2,1,0:T(8,128)(2,1)}), bf16[16,80,768]{2,1,0:T(8,128)(2,1)}, u32[]{:S(2)}, u32[]{:S(2)}) %all-to-all-start) | async-done | bytes 1966112 | tf_op jit(solution)/shard_map/all_to_all | solution.py:100
  236.4 1.6 slice.60
  239.6 1.8 multiply_cosine_fusion.1
  241.4 3.1 fusion.57
  245.9 1.6 fusion.37
  248.8 1.7 copy.28
  251.7 58.3 %while.11 = (s32[]{:T(128)}, bf16[8,128,4,128]{3,2,1,0:T(4,128)(2,1)}, bf16[8,128,4,128]{3,1,2,0:T(8,128)(2,1)S(1)}, bf16[4096,128]{1,0:T(8,128)(2,1)S(1)}, s32[...) while((s32[]{:T(128)}, ...), condition=%wide.region_15.17_spmd.clone, body=%wide.region_10.16_spmd.clone.sunk | while | flops 1365182464 | bytes 36886740 | solution.py:141
  254.6 1.5 fusion.84
  256.1 1.5 fusion.83
  261.9 1.5 fusion.84
  263.4 1.5 fusion.83
  269.2 1.5 fusion.84
  270.7 1.5 fusion.83
  276.4 1.5 fusion.84
  283.7 1.5 fusion.84
  285.2 1.5 fusion.83
  291.0 1.5 fusion.84
  298.3 1.5 fusion.84
  299.8 1.5 fusion.83
  305.6 1.5 fusion.84
  310.0 2.3 reshape.292
  312.3 3.7 %all-to-all-start.1 = ((bf16[16,64,512]{2,1,0:T(8,128)(2,1)}), bf16[16,64,512]{2,1,0:T(8,128)(2,1)S(1)}, u32[]{:S(2)}, u32[]{:S(2)}) async-start(bf16[16,64,512]{2,1,0:T(8,128)(2,1)} %reshape.292), calls=%async_computation.2 | async-start | bytes 2097152 | tf_op jit(solution)/shard_map/all_to_all | solution.py:148
  316.0 18.2 %all-to-all-done.1 = bf16[16,64,512]{2,1,0:T(8,128)(2,1)S(1)} async-done(((bf16[16,64,512]{2,1,0:T(8,128)(2,1)}), bf16[16,64,512]{2,1,0:T(8,128)(2,1)S(1)}, u32[]{:S(2)}, u32[]{:S(2)}) %all-to-all-start.1) | async-done | bytes 1048608 | tf_op jit(solution)/shard_map/all_to_all | solution.py:148
  334.2 2.6 gather_fusion
  (178 shorter events, 54.5 us)
Async XLA Ops:
  6.5 195.1 %copy-start = (bf16[64,128,1,128]{3,1,2,0:T(8,128)(2,1)S(1)}, bf16[64,128,1,128]{3,1,2,0:T(8,128)(2,1)}, u32[]{:S(2)}) copy-start(bf16[64,128,1,128]{3,1,2,0:T(8,128)(2,1)} %param.19) | copy-start | bytes 6291460
  6.5 4.2 %copy-start.6 = (bf16[1024]{0:T(1024)(128)(2,1)S(1)}, bf16[1024]{0:T(1024)(128)(2,1)}, u32[]{:S(2)}) copy-start(bf16[1024]{0:T(1024)(128)(2,1)} %param.14) | copy-start | bytes 6148
  6.5 4.3 %copy-start.3 = (bf16[512,1024]{1,0:T(8,128)(2,1)S(1)}, bf16[512,1024]{1,0:T(8,128)(2,1)}, u32[]{:S(2)}) copy-start(bf16[512,1024]{1,0:T(8,128)(2,1)} %param.13) | copy-start | bytes 3145732
  6.5 96.0 %all-gather.2.cloned.1.call-start = ((), (), s32[]{:S(2)}) async-start(), calls=%async_computation.3 | async-start | bytes 13369344 | tf_op jit(solution)/shard_map/all_gather | solution.py:77
  10.7 176.0 %reduce-scatter.2.cloned.1.call-start = ((), (), s32[]{:S(2)}) async-start(), calls=%async_computation.4 | async-start | bytes 14155776 | tf_op jit(solution)/shard_map/reduce_scatter | solution.py:80
  116.9 0.7 copy-start.5
  194.3 7.3 %copy-start.7 = (s32[1,32]{1,0:T(1,128)S(1)}, s32[1,32]{1,0:T(1,128)}, u32[]{:S(2)}) copy-start(s32[1,32]{1,0:T(1,128)} %param.21) | copy-start | bytes 388
  194.3 40.8 %all-to-all-start = ((bf16[16,80,768]{2,1,0:T(8,128)(2,1)}), bf16[16,80,768]{2,1,0:T(8,128)(2,1)}, u32[]{:S(2)}, u32[]{:S(2)}) async-start(bf16[16,80,768]{2,1,0:T(8,128)(2,1)} %pad_maximum_fusion), calls=%async_computation.1 | async-start | bytes 3932160 | tf_op jit(solution)/shard_map/all_to_all | solution.py:100
  244.6 1.3 copy-start.2
  256.1 1.5 copy-start.4
  263.4 1.5 copy-start.4
  270.7 1.5 copy-start.4
  277.9 1.5 copy-start.4
  285.2 1.5 copy-start.4
  292.5 1.5 copy-start.4
  299.8 1.5 copy-start.4
  307.1 1.5 copy-start.4
  312.3 21.9 %all-to-all-start.1 = ((bf16[16,64,512]{2,1,0:T(8,128)(2,1)}), bf16[16,64,512]{2,1,0:T(8,128)(2,1)S(1)}, u32[]{:S(2)}, u32[]{:S(2)}) async-start(bf16[16,64,512]{2,1,0:T(8,128)(2,1)} %reshape.292), calls=%async_computation.2 | async-start | bytes 2097152 | tf_op jit(solution)/shard_map/all_to_all | solution.py:148
  334.2 2.6 copy-start.1
Sparse Core Ops, SparseCore 0:
  10.9 91.6 all-gather.1
  117.1 69.6 reduce-scatter.1

commit v3 on v2

--- a/solution.py
+++ b/solution.py
@@ -3,6 +3,8 @@
 import jax
 import jax.numpy as jnp
 from jax import lax
+from jax.experimental import pallas as pl
+from jax.experimental.pallas import tpu as pltpu
 from jax.sharding import PartitionSpec as P
 
 EPS = 1e-05
@@ -54,6 +56,63 @@
         preferred_element_type=jnp.float32,
     )
     return (mixed / totals[..., None]).astype(jnp.bfloat16)
+
+
+def attention_kernel(q_ref, qr_ref, kp_ref, vp_ref, kn_ref, vn_ref, kr_ref, o_ref):
+    scaling = 1.0 / math.sqrt(q_ref.shape[-1])
+    q = q_ref[...]
+    before = lax.dot_general(
+        q, kp_ref[...], (((1,), (1,)), ((), ())), preferred_element_type=jnp.float32
+    ) * scaling
+    inside = lax.dot_general(
+        q, kn_ref[...], (((1,), (1,)), ((), ())), preferred_element_type=jnp.float32
+    ) * scaling
+    allowed = kr_ref[...] <= qr_ref[...]
+    inside = jnp.where(allowed, inside, -jnp.inf)
+    highest = jnp.maximum(
+        jnp.max(before, axis=1, keepdims=True), jnp.max(inside, axis=1, keepdims=True)
+    )
+    expo_before = jnp.exp(before - highest)
+    expo_inside = jnp.exp(inside - highest)
+    totals = jnp.sum(expo_before, axis=1, keepdims=True) + jnp.sum(
+        expo_inside, axis=1, keepdims=True
+    )
+    mixed = jnp.dot(
+        expo_before.astype(jnp.bfloat16), vp_ref[...], preferred_element_type=jnp.float32
+    ) + jnp.dot(
+        expo_inside.astype(jnp.bfloat16), vn_ref[...], preferred_element_type=jnp.float32
+    )
+    o_ref[...] = (mixed / totals).astype(o_ref.dtype)
+
+
+def attend_all(queries, query_rank, prefix_keys, prefix_values, new_keys, new_values,
+               key_rank, key_live, block_rows=256):
+    slots, heads, size = queries.shape
+    rows = slots * heads
+    q = queries.reshape(rows, size)
+    q_rank = jnp.repeat(query_rank, heads).reshape(rows, 1)
+    big = jnp.iinfo(jnp.int32).max
+    k_rank = jnp.where(key_live, key_rank, big).reshape(1, -1)
+    prefix_len = prefix_keys.shape[0]
+    new_len = new_keys.shape[0]
+    full = lambda i: (0, 0)
+    out = pl.pallas_call(
+        attention_kernel,
+        grid=(rows // block_rows,),
+        in_specs=[
+            pl.BlockSpec((block_rows, size), lambda i: (i, 0)),
+            pl.BlockSpec((block_rows, 1), lambda i: (i, 0)),
+            pl.BlockSpec((prefix_len, size), full),
+            pl.BlockSpec((prefix_len, size), full),
+            pl.BlockSpec((new_len, size), full),
+            pl.BlockSpec((new_len, size), full),
+            pl.BlockSpec((1, new_len), full),
+        ],
+        out_specs=pl.BlockSpec((block_rows, size), lambda i: (i, 0)),
+        out_shape=jax.ShapeDtypeStruct((rows, size), jnp.bfloat16),
+        compiler_params=pltpu.CompilerParams(vmem_limit_bytes=48 * 1024 * 1024),
+    )(q, q_rank, prefix_keys, prefix_values, new_keys, new_values, k_rank)
+    return out.reshape(slots, heads, size)
 
 
 def row_norm(tokens, gain, full_width):
@@ -124,26 +183,15 @@
     prefix_values = jnp.take(value_pages[:, :, 0, :], local_pages, axis=0).reshape(
         prefix_length, head_size
     )
-    block_size = min(128, slot_total)
-
-    def one_block(blocked):
-        return attend(
-            blocked[0],
-            blocked[1],
-            prefix_keys,
-            prefix_values,
-            rotated_keys,
-            slot_values,
-            slot_rank,
-            key_live,
-        )
-
-    attended = lax.map(
-        one_block,
-        (
-            rotated_queries.reshape(slot_total // block_size, block_size, group_heads, head_size),
-            slot_rank.reshape(slot_total // block_size, block_size),
-        ),
+    attended = attend_all(
+        rotated_queries,
+        slot_rank,
+        prefix_keys,
+        prefix_values,
+        rotated_keys,
+        slot_values,
+        slot_rank,
+        key_live,
     )
     returned = lax.all_to_all(
         attended.reshape(n_tok, capacity, query_width),

time: 344 us -> 339 us (0.985)
  Pallas kernels: 0 us -> 45 us
  matrix products: 46.8 us -> 14.3 us
  other arithmetic: 40.8 us -> 26 us
    pallas_call x0 -> x1, Pallas kernels: none -> 45 us  [attend_all(): pl.pallas_call(attention_kernel, grid=(rows // block_rows,), in_specs=[pl...]
    dot_general x32 -> x0, matrix products: 32.5 us -> none  [the longest x8 11.8 us: attend(): jnp.einsum('bhp,pd->bhd', expo_before.astype(jnp.bfloat16), prefix_values...]
    reduce_sum x16 -> x0, other arithmetic: 16.8 us -> none  [attend(): totals = jnp.sum(expo_before, axis=-1) + jnp.sum(expo_inside, axis=-1)]
    dynamic_update_slice x8 -> x0, local copies, waits for them, and re-layouts: 6.05 us -> none  [body(): lax.map(one_block, (rotated_queries.reshape(slot_total // block_size, blo...]
    another operation x3 -> x5, local copies, waits for them, and re-layouts: 0.2 us -> 5.45 us  [the longest x1 2.76 us: attend_all(): q_rank = jnp.repeat(query_rank, heads).reshape(rows, 1)]
  transfers between devices with their start and end apart: 4 -> 4, of which waited for: 4 -> 4; matrix products, arithmetic and copies ran while one was open for 2% -> 3% of each run, Pallas kernels for 0% -> 0%
where the time goes in v3:
time: 339 us
  waiting for transfers between devices  190 us (56%)
  Pallas kernels  45 us (13%)
  other arithmetic  26 us (8%)
  local copies, waits for them, and re-layouts  25.8 us (8%)
  matrix products  14.3 us (4%)
  between operations  13.6 us (4%)
  blocking collectives  12.5 us (4%)
  starting transfers between devices  10.9 us (3%)
    all_gather x1, waiting for transfers between devices, body(): gathered = lax.all_gather(weights_local, 'tok', axis=0, tiled=True)  78.9 us
    reduce_scatter x1, waiting for transfers between devices, body(): lax.psum_scatter(joined.reshape(group_count * row_count, joined.shape[2])...  67.6 us
    pallas_call x1, Pallas kernels, attend_all(): pl.pallas_call(attention_kernel, grid=(rows // block_rows,), in_specs=[pl...  45 us
    all_to_all x1, waiting for transfers between devices, body(): lax.all_to_all(outgoing, 'tok', split_axis=0, concat_axis=0, tiled=True)  25.7 us
    all_to_all x1, waiting for transfers between devices, body(): lax.all_to_all(attended.reshape(n_tok, capacity, query_width), 'tok', spl...  18.2 us
    dot_general x1, matrix products, body(): jnp.einsum('rd,dnc->nrc', normed, gathered, preferred_element_type=jnp.fl...  14.3 us
    psum x1, blocking collectives, row_norm(): squares = lax.psum(jnp.sum(values_wide * values_wide, axis=1), 'head')  12.5 us
    all_to_all x1, starting transfers between devices, body(): lax.all_to_all(outgoing, 'tok', split_axis=0, concat_axis=0, tiled=True)  7.2 us
  transfers between devices with their start and end apart: 4, of which 4 were waited for; matrix products, arithmetic and copies ran while one was open for 3% of the time, Pallas kernels for 0%

profile of v3, /device:TPU:32, one launch (start us, length us, event | category | flops | bytes accessed | tf_op | source)
XLA Modules:
  0.0 338.6 jit_solution(3097574167521157957)
XLA Ops:
  6.5 1.3 copy.20
  7.9 0.9 copy.21
  8.8 0.9 copy.22
  9.8 1.0 pad_maximum_fusion.2
  11.1 12.5 %psum.7 = f32[512]{0:T(512)S(1)} all-reduce(f32[512]{0:T(512)S(1)} %fusion), channel_id=1, replica_groups=mesh['tok'=16,'head'=8] {'head'}, use_global_device_ids=true, to_apply=%region_4.5 | all-reduce | flops 512 | bytes 4096 | tf_op jit(solution)/shard_map/psum | solution.py:120
  23.7 78.9 %all-gather.2.cloned.1.call-done = bf16[1024,8,768]{2,0,1:T(8,128)(2,1)} async-done(((bf16[64,8,768]{2,0,1:T(8,128)(2,1)}), bf16[1024,8,768]{2,0,1:T(8,128)(2,1)}) %all-gather.2.cloned.1.call-update) | async-done | bytes 12582928 | tf_op jit(solution)/shard_map/all_gather | solution.py:136
  102.6 14.3 %fusion.8 = f32[8,768,512]{1,2,0:T(8,128)} fusion(bf16[1024,8,768]{2,0,1:T(8,128)(2,1)} %all-gather.2.cloned.1.call-done, bf16[512,1024]{1,0:T(8,128)(2,1)S(1)} %copy-done.3, f32[1024]{0:T(1024)S(1)} %convert_element_type.97, f32[512]{0:T(512)S(1)} %add_rsqrt_fusion), kind=kOutput, calls=%fused_computation.19 | convolution fusion | flops 6444548096 | bytes 26220544 | tf_op jit(solution)/shard_map/rd,dnc->nrc/dot_general | solution.py:138
  117.6 1.1 reduce-window.15
  119.2 67.6 %reduce-scatter.2.cloned.1.call-done = f32[512,768]{1,0:T(8,128)} async-done(((f32[4096,768]{1,0:T(8,128)}), f32[512,768]{1,0:T(8,128)}) %reduce-scatter.2.cloned.1.call-update) | async-done | bytes 1572880 | tf_op jit(solution)/shard_map/reduce_scatter | solution.py:139
  186.7 4.6 %scatter_custom_fusion = bf16[1024,768]{1,0:T(8,128)(2,1)} fusion(s32[512]{0:T(512)S(1)} %bitcast.58, f32[512,768]{1,0:T(8,128)} %reduce-scatter.2.cloned.1.call-done, bf16[]{:T(256)} %constant.20.clone.1), kind=kCustom, calls=%fused_computation.26 | custom fusion | flops 393216 | bytes 3145730 | tf_op jit(solution)/shard_map/scatter | solution.py:153
  191.5 2.8 pad_maximum_fusion
  194.3 7.2 %all-to-all-start = ((bf16[16,80,768]{2,1,0:T(8,128)(2,1)}), bf16[16,80,768]{2,1,0:T(8,128)(2,1)}, u32[]{:S(2)}, u32[]{:S(2)}) async-start(bf16[16,80,768]{2,1,0:T(8,128)(2,1)} %pad_maximum_fusion), calls=%async_computation.1 | async-start | bytes 3932160 | tf_op jit(solution)/shard_map/all_to_all | solution.py:159
  201.6 1.7 gather_fusion.1
  203.3 3.3 gather_fusion.2
  206.6 2.8 broadcast_select_fusion
  209.4 25.7 %all-to-all-done = bf16[16,80,768]{2,1,0:T(8,128)(2,1)} async-done(((bf16[16,80,768]{2,1,0:T(8,128)(2,1)}), bf16[16,80,768]{2,1,0:T(8,128)(2,1)}, u32[]{:S(2)}, u32[]{:S(2)}) %all-to-all-start) | async-done | bytes 1966112 | tf_op jit(solution)/shard_map/all_to_all | solution.py:159
  235.1 1.1 fusion.28
  236.3 1.6 slice.60
  237.9 1.1 slice.61
  239.0 0.7 fusion.30
  240.5 2.2 reshape.279
  242.8 3.0 multiply_cosine_fusion.1
  245.8 4.3 %fusion.24 = (bf16[1024,64]{1,0:T(8,128)(2,1)}, bf16[1024,64]{1,0:T(8,128)(2,1)}) fusion(f32[64]{0:T(128)S(1)} %multiply_exponential_fusion, f32[1024]{0:T(1024)S(1)} %get-tuple-element.10, bf16[1024,1,128]{2,0,1:T(8,128)(2,1)} %get-tuple-element.16), kind=kLoop, calls=%fused_computation.42 | loop fusion | flops 720896 | bytes 528640 | tf_op jit(solution)/shard_map/concatenate | solution.py:24
  250.1 1.0 broadcast_in_dim.17
  251.1 2.8 reshape_reshape.8.qr_ref
  253.9 3.4 %fusion.4 = (bf16[1024,4,64]{2,1,0:T(4,128)(2,1)S(1)}, bf16[1024,4,64]{2,1,0:T(4,128)(2,1)S(1)}) fusion(f32[1024,64]{1,0:T(8,128)} %get-tuple-element.20, f32[1024,64]{1,0:T(8,128)} %get-tuple-element.19, bf16[1024,4,128]{2,1,0:T(4,128)(2,1)} %reshape.279), kind=kLoop, calls=%fused_computation.14 | loop fusion | flops 2621440 | bytes 2621440 | tf_op jit(solution)/shard_map/convert.11
  258.7 45.0 %shard_map.91 = bf16[4096,128]{1,0:T(8,128)(2,1)S(1)} custom-call(bf16[4096,128]{1,0:T(8,128)(2,1)S(1)} %pad_maximum_fusion.1.q_ref, s32[4096,1]{1,0:T(8,128)} %reshape_reshape.8.qr_ref, bf16[4096,128]{1,0:T(8,128)(2,1)S(1)} %bitcast.46, bf16[4096,128]{1,0:T(8,128)(2,1)S(1)} %bitcast.45, bf16[1024,128]{1,0:T(8,128)(2,1)S(1)} %pad_maximum_fusion.3.kn_ref, ...), custom_call_target="tpu_custom_call" | custom-call | tf_op jit(solution)/shard_map/pallas_call | solution.py:99
  303.7 1.0 copy-done.2
  304.7 2.5 reshape_reshape.7
  307.2 3.7 %all-to-all-start.1 = ((bf16[16,64,512]{2,1,0:T(8,128)(2,1)}), bf16[16,64,512]{2,1,0:T(8,128)(2,1)S(1)}, u32[]{:S(2)}, u32[]{:S(2)}) async-start(bf16[16,64,512]{2,1,0:T(8,128)(2,1)} %reshape_reshape.7), calls=%async_computation.2 | async-start | bytes 2097152 | tf_op jit(solution)/shard_map/all_to_all | solution.py:196
  310.9 18.2 %all-to-all-done.1 = bf16[16,64,512]{2,1,0:T(8,128)(2,1)S(1)} async-done(((bf16[16,64,512]{2,1,0:T(8,128)(2,1)}), bf16[16,64,512]{2,1,0:T(8,128)(2,1)S(1)}, u32[]{:S(2)}, u32[]{:S(2)}) %all-to-all-start.1) | async-done | bytes 1048608 | tf_op jit(solution)/shard_map/all_to_all | solution.py:196
  329.1 2.6 gather_fusion
  (53 shorter events, 4.1 us)
Async XLA Ops:
  6.5 195.1 %copy-start = (bf16[64,128,1,128]{3,1,2,0:T(8,128)(2,1)S(1)}, bf16[64,128,1,128]{3,1,2,0:T(8,128)(2,1)}, u32[]{:S(2)}) copy-start(bf16[64,128,1,128]{3,1,2,0:T(8,128)(2,1)} %param.17) | copy-start | bytes 6291460
  6.5 4.3 %copy-start.7 = (bf16[1024]{0:T(1024)(128)(2,1)S(1)}, bf16[1024]{0:T(1024)(128)(2,1)}, u32[]{:S(2)}) copy-start(bf16[1024]{0:T(1024)(128)(2,1)} %param.12) | copy-start | bytes 6148
  6.5 4.3 %copy-start.3 = (bf16[512,1024]{1,0:T(8,128)(2,1)S(1)}, bf16[512,1024]{1,0:T(8,128)(2,1)}, u32[]{:S(2)}) copy-start(bf16[512,1024]{1,0:T(8,128)(2,1)} %param.11) | copy-start | bytes 3145732
  6.5 96.1 %all-gather.2.cloned.1.call-start = ((), (), s32[]{:S(2)}) async-start(), calls=%async_computation.3 | async-start | bytes 13369344 | tf_op jit(solution)/shard_map/all_gather | solution.py:136
  10.8 176.0 %reduce-scatter.2.cloned.1.call-start = ((), (), s32[]{:S(2)}) async-start(), calls=%async_computation.4 | async-start | bytes 14155776 | tf_op jit(solution)/shard_map/reduce_scatter | solution.py:139
  116.9 0.7 copy-start.6
  194.3 7.3 %copy-start.8 = (s32[1,32]{1,0:T(1,128)S(1)}, s32[1,32]{1,0:T(1,128)}, u32[]{:S(2)}) copy-start(s32[1,32]{1,0:T(1,128)} %param.19) | copy-start | bytes 388
  194.3 40.8 %all-to-all-start = ((bf16[16,80,768]{2,1,0:T(8,128)(2,1)}), bf16[16,80,768]{2,1,0:T(8,128)(2,1)}, u32[]{:S(2)}, u32[]{:S(2)}) async-start(bf16[16,80,768]{2,1,0:T(8,128)(2,1)} %pad_maximum_fusion), calls=%async_computation.1 | async-start | bytes 3932160 | tf_op jit(solution)/shard_map/all_to_all | solution.py:159
  257.3 1.0 copy-start.4
  257.3 1.0 copy-start.5
  257.4 1.4 copy-start.1
  303.7 1.0 copy-start.2
  307.2 21.9 %all-to-all-start.1 = ((bf16[16,64,512]{2,1,0:T(8,128)(2,1)}), bf16[16,64,512]{2,1,0:T(8,128)(2,1)S(1)}, u32[]{:S(2)}, u32[]{:S(2)}) async-start(bf16[16,64,512]{2,1,0:T(8,128)(2,1)} %reshape_reshape.7), calls=%async_computation.2 | async-start | bytes 2097152 | tf_op jit(solution)/shard_map/all_to_all | solution.py:196
Sparse Core Ops, SparseCore 0:
  10.9 91.6 all-gather.1
  117.0 69.6 reduce-scatter.1

commit v4 on v3

--- a/solution.py
+++ b/solution.py
@@ -122,61 +122,96 @@
     return (values_wide * factor[:, None] * gain.astype(jnp.float32)[None, :]).astype(jnp.bfloat16)
 
 
+def pair_order(own, other, parity):
+    stacked = jnp.stack([own, other])
+    return jnp.take(stacked, jnp.stack([parity, 1 - parity]), axis=0)
+
+
 def body(tokens, gain, w_query, w_key, w_value, group_ids, key_pages, value_pages, page_table):
     row_count = tokens.shape[0]
-    n_tok = lax.axis_size("tok")
+    n_pair = lax.axis_size("tp")
+    n_tok = n_pair * 2
     n_head = lax.axis_size("head")
     head_size = key_pages.shape[-1]
     query_width = w_query.shape[2]
     group_heads = query_width // head_size
+    half_heads = group_heads // 2
     full_width = tokens.shape[1] * n_head
     capacity = 2 * row_count // n_tok
+    pair_capacity = 2 * capacity
+    parity = lax.axis_index("tq")
+    tok_index = lax.axis_index("tp") * 2 + parity
+    swap = [(0, 1), (1, 0)]
     normed = row_norm(tokens, gain, full_width)
     weights_local = jnp.concatenate([w_query, w_key, w_value], axis=2)
-    gathered = lax.all_gather(weights_local, "tok", axis=0, tiled=True)
-    group_count = row_count * lax.axis_size("head") // row_count
-    joined = jnp.einsum("rd,dnc->nrc", normed, gathered, preferred_element_type=jnp.float32)
+    split_q = half_heads * head_size
+    first_half = jnp.concatenate(
+        [weights_local[:, :, :split_q], weights_local[:, :, query_width : query_width + head_size]],
+        axis=2,
+    )
+    second_half = jnp.concatenate(
+        [weights_local[:, :, split_q:query_width], weights_local[:, :, query_width + head_size :]],
+        axis=2,
+    )
+    keep = jnp.where(parity == 0, first_half, second_half)
+    send = jnp.where(parity == 0, second_half, first_half)
+    received = lax.ppermute(send, "tq", swap)
+    pair_weights = pair_order(keep, received, parity)
+    pair_weights = pair_weights.reshape((-1,) + pair_weights.shape[2:])
+    gathered = lax.all_gather(pair_weights, "tp", axis=0, tiled=True)
+    partner_normed = lax.ppermute(normed, "tq", swap)
+    pair_normed = pair_order(normed, partner_normed, parity).reshape(2 * row_count, -1)
+    group_own = group_ids[:, 0]
+    group_partner = lax.ppermute(group_own, "tq", swap)
+    group_pair = pair_order(group_own, group_partner, parity).reshape(2 * row_count)
+    joined = jnp.einsum("rd,dnc->nrc", pair_normed, gathered, preferred_element_type=jnp.float32)
     projected = lax.psum_scatter(
-        joined.reshape(group_count * row_count, joined.shape[2]),
+        joined.reshape(n_head * 2 * row_count, joined.shape[2]),
         "head",
         scatter_dimension=0,
         tiled=True,
     )
     projected_low = projected.astype(jnp.bfloat16)
-    width_all = projected_low.shape[1]
-    group_of = group_ids[:, 0]
-    member = (group_of[:, None] == jnp.arange(n_tok, dtype=jnp.int32)[None, :]).astype(jnp.int32)
-    local_rank = jnp.sum((jnp.cumsum(member, axis=0) - member) * member, axis=1)
-    slot_index = group_of * capacity + local_rank
-    counts_local = jnp.sum(member, axis=0).astype(jnp.bfloat16)
+    width_half = projected_low.shape[1]
+    member = (group_pair[:, None] == jnp.arange(n_tok, dtype=jnp.int32)[None, :]).astype(jnp.int32)
+    pair_rank = jnp.sum((jnp.cumsum(member, axis=0) - member) * member, axis=1)
+    slot_index = group_pair * pair_capacity + pair_rank
+    counts_first = jnp.sum(member[:row_count], axis=0).astype(jnp.bfloat16)
+    counts_second = jnp.sum(member[row_count:], axis=0).astype(jnp.bfloat16)
     outgoing = (
-        jnp.zeros((n_tok * capacity, width_all), jnp.bfloat16).at[slot_index].set(projected_low)
-    )
-    count_rows = jnp.broadcast_to(counts_local[:, None, None], (n_tok, 16, width_all))
+        jnp.zeros((n_tok * pair_capacity, width_half), jnp.bfloat16)
+        .at[slot_index]
+        .set(projected_low)
+    )
+    count_rows = jnp.zeros((n_tok, 16, width_half), jnp.bfloat16)
+    count_rows = count_rows.at[:, 0, :].set(counts_first[:, None])
+    count_rows = count_rows.at[:, 1, :].set(counts_second[:, None])
     outgoing = jnp.concatenate(
-        [outgoing.reshape(n_tok, capacity, width_all), count_rows], axis=1
-    )
-    arrived_all = lax.all_to_all(outgoing, "tok", split_axis=0, concat_axis=0, tiled=True)
-    block_counts = arrived_all[:, capacity, 0].astype(jnp.int32)
-    arrived = arrived_all[:, :capacity, :]
-    slot_total = n_tok * capacity
-    arrived = arrived.reshape(slot_total, width_all)
+        [outgoing.reshape(n_tok, pair_capacity, width_half), count_rows], axis=1
+    )
+    arrived_all = lax.all_to_all(outgoing, ("tp", "tq"), 0, 0, tiled=True)
+    arrived_all = arrived_all.reshape(n_pair, 2, pair_capacity + 16, width_half)
+    count_first = arrived_all[:, 0, pair_capacity, 0].astype(jnp.int32)
+    count_second = arrived_all[:, 0, pair_capacity + 1, 0].astype(jnp.int32)
+    part_one = arrived_all[:, 0, :pair_capacity, :]
+    part_two = arrived_all[:, 1, :pair_capacity, :]
+    slot_total = n_pair * pair_capacity
+    slot_queries = jnp.concatenate(
+        [part_one[..., :split_q], part_two[..., :split_q]], axis=-1
+    ).reshape(slot_total, group_heads, head_size)
+    slot_keys = part_one[..., split_q:].reshape(slot_total, 1, head_size)
+    slot_values = part_two[..., split_q:].reshape(slot_total, head_size)
     live_count = (
-        jnp.arange(capacity, dtype=jnp.int32)[None, :] < block_counts[:, None]
+        jnp.arange(pair_capacity, dtype=jnp.int32)[None, :]
+        < (count_first + count_second)[:, None]
     ).astype(jnp.int32).reshape(slot_total)
     key_live = live_count > 0
     slot_rank = jnp.cumsum(live_count) - live_count
     prefix_length = page_table.shape[1] * key_pages.shape[1]
     positions = prefix_length + slot_rank
-    rotated_queries = rotate(
-        arrived[:, :query_width].reshape(slot_total, group_heads, head_size), positions
-    )
-    rotated_keys = rotate(
-        arrived[:, query_width : query_width + head_size].reshape(slot_total, 1, head_size),
-        positions,
-    )[:, 0, :]
-    slot_values = arrived[:, query_width + head_size :]
-    local_pages = page_table[0] - lax.axis_index("tok") * key_pages.shape[0]
+    rotated_queries = rotate(slot_queries, positions)
+    rotated_keys = rotate(slot_keys, positions)[:, 0, :]
+    local_pages = page_table[0] - tok_index * key_pages.shape[0]
     prefix_keys = jnp.take(key_pages[:, :, 0, :], local_pages, axis=0).reshape(
         prefix_length, head_size
     )
@@ -192,29 +227,42 @@
         slot_values,
         slot_rank,
         key_live,
+    ).reshape(n_pair, pair_capacity, query_width)
+    later = jnp.clip(
+        count_first[:, None] + jnp.arange(capacity, dtype=jnp.int32)[None, :],
+        0,
+        pair_capacity - 1,
+    )
+    back = jnp.stack(
+        [attended[:, :capacity, :], jnp.take_along_axis(attended, later[:, :, None], axis=1)],
+        axis=1,
     )
     returned = lax.all_to_all(
-        attended.reshape(n_tok, capacity, query_width),
-        "tok",
-        split_axis=0,
-        concat_axis=0,
-        tiled=True,
-    )
-    return returned.reshape(n_tok * capacity, query_width)[slot_index]
+        back.reshape(n_tok, capacity, query_width), ("tp", "tq"), 0, 0, tiled=True
+    )
+    member_own = member[:row_count] * (1 - parity) + member[row_count:] * parity
+    group_of = group_own
+    local_rank = jnp.sum((jnp.cumsum(member_own, axis=0) - member_own) * member_own, axis=1)
+    return returned.reshape(n_tok * capacity, query_width)[group_of * capacity + local_rank]
 
 
 def solution(mesh):
+    n_tok, n_head = mesh.devices.shape
+    paired = jax.sharding.Mesh(
+        mesh.devices.reshape(n_tok // 2, 2, n_head), ("tp", "tq", "head")
+    )
+    tok = ("tp", "tq")
     placed = (
-        P("tok", "head"),
+        P(tok, "head"),
         P("head"),
-        P(("head", "tok"), None, None),
-        P(("head", "tok"), None, None),
-        P(("head", "tok"), None, None),
-        P("tok", None),
-        P("tok", None, "head", None),
-        P("tok", None, "head", None),
-        P("tok", None),
+        P(("head",) + tok, None, None),
+        P(("head",) + tok, None, None),
+        P(("head",) + tok, None, None),
+        P(tok, None),
+        P(tok, None, "head", None),
+        P(tok, None, "head", None),
+        P(tok, None),
     )
     return jax.shard_map(
-        body, mesh=mesh, in_specs=placed, out_specs=P("tok", "head"), check_vma=False
-    )
+        body, mesh=paired, in_specs=placed, out_specs=P(tok, "head"), check_vma=False
+    )

time: 339 us -> 399 us (1.18)
  local copies, waits for them, and re-layouts: 25.8 us -> 64 us
  other arithmetic: 26 us -> 48.1 us
    ppermute x0 -> x3, waiting for transfers between devices: none -> 42.3 us  [the longest x1 30.4 us: body(): partner_normed = lax.ppermute(normed, 'tq', swap)]
    all_gather x1, waiting for transfers between devices: 78.9 us -> 47.8 us  [body(): gathered = lax.all_gather(pair_weights, 'tp', axis=0, tiled=True)]
    gather x1 -> x8, local copies, waits for them, and re-layouts: 2.62 us -> 17.3 us  [the longest x5 8.17 us: pair_order(): return jnp.take(stacked, jnp.stack([parity, 1 - parity]), axis=0)]
    transpose x0 -> x1, local copies, waits for them, and re-layouts: none -> 12.6 us  [body(): jnp.einsum('rd,dnc->nrc', pair_normed, gathered, preferred_element_type=j...]
    reduce_scatter x1, waiting for transfers between devices: 67.6 us -> 56.1 us  [body(): lax.psum_scatter(joined.reshape(n_head * 2 * row_count, joined.shape[2]),...]
    another operation x5 -> x14, other arithmetic: 4.92 us -> 14.1 us
    select_n x1 -> x10, other arithmetic: 0.01 us -> 8.52 us  [the longest x5 5.4 us: pair_order(): return jnp.take(stacked, jnp.stack([parity, 1 - parity]), axis=0)]
    another operation x4 -> x15, local copies, waits for them, and re-layouts: 2.69 us -> 9.13 us  [the longest x1 2.5 us: body(): attended.reshape(n_tok, capacity, query_width)]
  transfers between devices with their start and end apart: 4 -> 7, of which waited for: 4 -> 7; matrix products, arithmetic and copies ran while one was open for 3% -> 7% of each run, Pallas kernels for 0% -> 0%
where the time goes in v4:
time: 399 us; the launch traced here: 397 us
  waiting for transfers between devices  187 us (47%)
  local copies, waits for them, and re-layouts  64 us (16%)
  other arithmetic  48.1 us (12%)
  Pallas kernels  45.1 us (11%)
  starting transfers between devices  14.5 us (4%)
  between operations  13.8 us (3%)
  matrix products  12.8 us (3%)
  blocking collectives  11.7 us (3%)
    reduce_scatter x1, waiting for transfers between devices, body(): lax.psum_scatter(joined.reshape(n_head * 2 * row_count, joined.shape[2]),...  56.1 us
    all_gather x1, waiting for transfers between devices, body(): gathered = lax.all_gather(pair_weights, 'tp', axis=0, tiled=True)  47.8 us
    pallas_call x1, Pallas kernels, attend_all(): pl.pallas_call(attention_kernel, grid=(rows // block_rows,), in_specs=[pl...  45.1 us
    ppermute x1, waiting for transfers between devices, body(): partner_normed = lax.ppermute(normed, 'tq', swap)  30.4 us
    all_to_all x1, waiting for transfers between devices, body(): arrived_all = lax.all_to_all(outgoing, ('tp', 'tq'), 0, 0, tiled=True)  23.1 us
    all_to_all x1, waiting for transfers between devices, body(): lax.all_to_all(back.reshape(n_tok, capacity, query_width), ('tp', 'tq'),...  18 us
    dot_general x1, matrix products, body(): jnp.einsum('rd,dnc->nrc', pair_normed, gathered, preferred_element_type=j...  12.8 us
    transpose x1, local copies, waits for them, and re-layouts, body(): jnp.einsum('rd,dnc->nrc', pair_normed, gathered, preferred_element_type=j...  12.6 us
  transfers between devices with their start and end apart: 7, of which 7 were waited for; matrix products, arithmetic and copies ran while one was open for 7% of the time, Pallas kernels for 0%

profile of v4, /device:TPU:32, one launch (start us, length us, event | category | flops | bytes accessed | tf_op | source)
XLA Modules:
  0.0 397.4 jit_solution(10417114167246725764)
XLA Ops:
  11.6 9.1 %collective-permute-done.1 = bf16[64,8,384]{2,1,0:T(8,128)(2,1)S(1)} collective-permute-done((bf16[64,8,384]{2,1,0:T(8,128)(2,1)}, bf16[64,8,384]{2,1,0:T(8,128)(2,1)S(1)}, u32[]{:S(2)}, u32[]{:S(2)}) %collective-permute-start.1) | collective-permute-done | bytes 393248 | tf_op jit(solution)/shard_map/ppermute | solution.py:158
  24.1 2.5 copy.29
  29.0 11.7 %psum.7 = f32[512]{0:T(512)S(1)} all-reduce(f32[512]{0:T(512)S(1)} %fusion), channel_id=1, replica_groups=mesh['tp'=8,'tq'=2,'head'=8] {'head'}, use_global_device_ids=true, to_apply=%region_4.5 | all-reduce | flops 512 | bytes 4096 | tf_op jit(solution)/shard_map/psum | solution.py:120
  43.9 30.4 %collective-permute-done.2 = bf16[512,1024]{1,0:T(8,128)(2,1)} collective-permute-done((bf16[512,1024]{1,0:T(8,128)(2,1)}, bf16[512,1024]{1,0:T(8,128)(2,1)}, u32[]{:S(2)}, u32[]{:S(2)}) %collective-permute-start.2) | collective-permute-done | bytes 1048608 | tf_op jit(solution)/shard_map/ppermute | solution.py:162
  74.3 2.8 pad_maximum_fusion
  77.1 3.6 gather_fusion.2
  80.6 3.2 bitcast_select_fusion
  83.8 47.8 %all-gather.2.cloned.1.call-done = bf16[1024,8,384]{0,2,1:T(8,128)(2,1)} async-done(((bf16[128,8,384]{0,2,1:T(8,128)(2,1)}), bf16[1024,8,384]{0,2,1:T(8,128)(2,1)}) %all-gather.2.cloned.1.call-update) | async-done | bytes 6291472 | tf_op jit(solution)/shard_map/all_gather | solution.py:161
  131.6 12.8 %convolution_bitcast_fusion = f32[8,1024,384]{1,2,0:T(8,128)} fusion(bf16[1024,8,384]{0,2,1:T(8,128)(2,1)} %all-gather.2.cloned.1.call-done, bf16[1024,1024]{1,0:T(8,128)(2,1)} %bitcast_select_fusion), kind=kOutput, calls=%fused_computation.8 | convolution fusion | flops 6442450944 | bytes 20971520 | tf_op jit(solution)/shard_map/rd,dnc->nrc/dot_general | solution.py:167
  144.4 12.6 %copy.30 = f32[8,1024,384]{2,1,0:T(8,128)} copy(f32[8,1024,384]{1,2,0:T(8,128)} %convolution_bitcast_fusion) | data formatting | bytes 25165824 | tf_op jit(solution)/shard_map/rd,dnc->nrc/transpose | solution.py:167
  158.4 2.9 collective-permute-done
  161.9 4.5 %reduce-window.21 = s32[16,8,128]{2,1,0:T(8,128)S(1)} reduce-window(s32[16,8,128]{2,1,0:T(8,128)S(1)} %fusion.25, s32[]{:T(128)} %constant.152.clone.1), window={size=1x1x128 pad=0_0x0_0x127_0}, to_apply=%region_0.0 | reduce-window | flops 2080768 | bytes 131076 | tf_op jit(solution)/shard_map/reduce-window
  168.9 56.1 %reduce-scatter.2.cloned.1.call-done = f32[1024,384]{1,0:T(8,128)} async-done(((f32[8192,384]{1,0:T(8,128)}), f32[1024,384]{1,0:T(8,128)}) %reduce-scatter.2.cloned.1.call-update) | async-done | bytes 1572880 | tf_op jit(solution)/shard_map/reduce_scatter | solution.py:168
  225.1 6.9 %scatter_custom_fusion = bf16[2048,384]{1,0:T(8,128)(2,1)} fusion(s32[1024]{0:T(1024)S(1)} %bitcast.137, f32[1024,384]{1,0:T(8,128)} %reduce-scatter.2.cloned.1.call-done, bf16[]{:T(256)} %constant.148.clone.1), kind=kCustom, calls=%fused_computation.34 | custom fusion | flops 393216 | bytes 3145730 | tf_op jit(solution)/shard_map/scatter | solution.py:184
  232.0 2.8 pad_maximum_fusion.1
  234.8 7.2 %all-to-all-start = ((bf16[16,144,384]{2,1,0:T(8,128)(2,1)}), bf16[16,144,384]{2,1,0:T(8,128)(2,1)}, u32[]{:S(2)}, u32[]{:S(2)}) async-start(bf16[16,144,384]{2,1,0:T(8,128)(2,1)} %pad_maximum_fusion.1), calls=%async_computation.1 | async-start | bytes 3538944 | tf_op jit(solution)/shard_map/all_to_all | solution.py:192
  243.7 3.3 gather_fusion.6
  247.0 2.8 broadcast_select_fusion
  249.8 23.1 %all-to-all-done = bf16[16,144,384]{2,1,0:T(8,128)(2,1)} async-done(((bf16[16,144,384]{2,1,0:T(8,128)(2,1)}), bf16[16,144,384]{2,1,0:T(8,128)(2,1)}, u32[]{:S(2)}, u32[]{:S(2)}) %all-to-all-start) | async-done | bytes 1769504 | tf_op jit(solution)/shard_map/all_to_all | solution.py:192
  278.5 3.1 fusion.20
  284.9 3.8 fusion.40
  288.6 2.3 copy.41
  290.9 2.3 copy.42
  293.2 2.7 fusion.5
  295.8 2.3 copy.33
  298.2 2.3 copy.34
  301.5 2.8 reshape_reshape.8.qr_ref
  307.6 45.1 %shard_map.91 = bf16[4096,128]{1,0:T(8,128)(2,1)S(1)} custom-call(bf16[4096,128]{1,0:T(8,128)(2,1)S(1)} %pad_maximum_fusion.3.q_ref, s32[4096,1]{1,0:T(8,128)} %reshape_reshape.8.qr_ref, bf16[4096,128]{1,0:T(8,128)(2,1)S(1)} %bitcast.111, bf16[4096,128]{1,0:T(8,128)(2,1)S(1)} %bitcast.110, bf16[1024,128]{1,0:T(8,128)(2,1)S(1)} %pad_maximum_fusion.6.kn_ref, ...), custom_call_target="tpu_custom_call" | custom-call | tf_op jit(solution)/shard_map/pallas_call | solution.py:99
  356.4 6.4 %gather_fusion.4 = bf16[512,512]{1,0:T(8,128)(2,1)} fusion(bf16[8,128,512]{2,1,0:T(8,128)(2,1)S(1)} %reshape_reshape.7, s32[512]{0:T(512)S(1)} %reshape.722), kind=kCustom, calls=%fused_computation.6 | custom fusion | bytes 1052672 | tf_op jit(solution)/shard_map/jit(take_along_axis)/gather | solution.py:237
  366.2 3.7 all-to-all-start.1
  369.9 18.0 %all-to-all-done.1 = bf16[16,64,512]{2,1,0:T(8,128)(2,1)S(1)} async-done(((bf16[16,64,512]{2,1,0:T(8,128)(2,1)}), bf16[16,64,512]{2,1,0:T(8,128)(2,1)S(1)}, u32[]{:S(2)}, u32[]{:S(2)}) %all-to-all-start.1) | async-done | bytes 1048608 | tf_op jit(solution)/shard_map/all_to_all | solution.py:240
  388.0 2.6 gather_fusion.3
  (111 shorter events, 40.4 us)
Async XLA Ops:
  6.5 235.5 %copy-start = (bf16[64,128,1,128]{3,1,2,0:T(8,128)(2,1)S(1)}, bf16[64,128,1,128]{3,1,2,0:T(8,128)(2,1)}, u32[]{:S(2)}) copy-start(bf16[64,128,1,128]{3,1,2,0:T(8,128)(2,1)} %param.21) | copy-start | bytes 6291460
  6.5 4.9 %copy-start.5 = (bf16[64,8,128]{2,1,0:T(8,128)(2,1)S(1)}, bf16[64,8,128]{2,1,0:T(8,128)(2,1)}, u32[]{:S(2)}) copy-start(bf16[64,8,128]{2,1,0:T(8,128)(2,1)} %param.18) | copy-start | bytes 393220
  6.5 4.9 %copy-start.4 = (bf16[64,8,128]{2,1,0:T(8,128)(2,1)S(1)}, bf16[64,8,128]{2,1,0:T(8,128)(2,1)}, u32[]{:S(2)}) copy-start(bf16[64,8,128]{2,1,0:T(8,128)(2,1)} %param.19) | copy-start | bytes 393220
  6.5 125.1 %all-gather.2.cloned.1.call-start = ((), (), s32[]{:S(2)}) async-start(), calls=%async_computation.3 | async-start | bytes 7077888 | tf_op jit(solution)/shard_map/all_gather | solution.py:161
  9.6 11.1 %collective-permute-start.1 = (bf16[64,8,384]{2,1,0:T(8,128)(2,1)}, bf16[64,8,384]{2,1,0:T(8,128)(2,1)S(1)}, u32[]{:S(2)}, u32[]{:S(2)}) collective-permute-start(bf16[64,8,384]{2,1,0:T(8,128)(2,1)} %maximum_select_fusion.1), channel_id=1, source_target_pairs={{0,8},{8,0},{1,9},{9,1},{2,10},{10,2},{3,11},{11,3},{4,12},{12,4},... | collective-permute-start | bytes 1179656 | tf_op jit(solution)/shard_map/ppermute | solution.py:158
  20.7 0.7 copy-start.6
  24.1 4.7 %copy-start.8 = (bf16[1024]{0:T(1024)(128)(2,1)S(1)}, bf16[1024]{0:T(1024)(128)(2,1)}, u32[]{:S(2)}) copy-start(bf16[1024]{0:T(1024)(128)(2,1)} %param.16) | copy-start | bytes 6148
  24.1 4.7 %copy-start.3 = (bf16[512,1024]{1,0:T(8,128)(2,1)S(1)}, bf16[512,1024]{1,0:T(8,128)(2,1)}, u32[]{:S(2)}) copy-start(bf16[512,1024]{1,0:T(8,128)(2,1)} %param.15) | copy-start | bytes 3145732
  28.7 196.4 %reduce-scatter.2.cloned.1.call-start = ((), (), s32[]{:S(2)}) async-start(), calls=%async_computation.4 | async-start | bytes 14155776 | tf_op jit(solution)/shard_map/reduce_scatter | solution.py:168
  42.0 32.3 %collective-permute-start.2 = (bf16[512,1024]{1,0:T(8,128)(2,1)}, bf16[512,1024]{1,0:T(8,128)(2,1)}, u32[]{:S(2)}, u32[]{:S(2)}) collective-permute-start(bf16[512,1024]{1,0:T(8,128)(2,1)} %fusion.2), channel_id=1, source_target_pairs={{0,8},{8,0},{1,9},{9,1},{2,10},{10,2},{3,11},{11,3},{4,12},{12,4},... | collective-permute-start | bytes 3145736 | tf_op jit(solution)/shard_map/ppermute | solution.py:162
  157.0 0.7 copy-start.7
  157.6 3.6 collective-permute-start
  234.8 7.2 %copy-start.9 = (s32[1,32]{1,0:T(1,128)S(1)}, s32[1,32]{1,0:T(1,128)}, u32[]{:S(2)}) copy-start(s32[1,32]{1,0:T(1,128)} %param.23) | copy-start | bytes 388
  234.8 38.0 %all-to-all-start = ((bf16[16,144,384]{2,1,0:T(8,128)(2,1)}), bf16[16,144,384]{2,1,0:T(8,128)(2,1)}, u32[]{:S(2)}, u32[]{:S(2)}) async-start(bf16[16,144,384]{2,1,0:T(8,128)(2,1)} %pad_maximum_fusion.1), calls=%async_computation.1 | async-start | bytes 3538944 | tf_op jit(solution)/shard_map/all_to_all | solution.py:192
  304.2 3.4 copy-start.1
  352.8 1.0 copy-start.2
  366.2 21.7 %all-to-all-start.1 = ((bf16[16,64,512]{2,1,0:T(8,128)(2,1)}), bf16[16,64,512]{2,1,0:T(8,128)(2,1)S(1)}, u32[]{:S(2)}, u32[]{:S(2)}) async-start(bf16[16,64,512]{2,1,0:T(8,128)(2,1)} %bitcast.119), calls=%async_computation.2 | async-start | bytes 2097152 | tf_op jit(solution)/shard_map/all_to_all | solution.py:240
Sparse Core Ops, SparseCore 0:
  28.8 102.7 all-gather.1
  157.1 67.9 reduce-scatter.1

commit v5 on v3

--- a/solution.py
+++ b/solution.py
@@ -58,17 +58,26 @@
     return (mixed / totals[..., None]).astype(jnp.bfloat16)
 
 
-def attention_kernel(q_ref, qr_ref, kp_ref, vp_ref, kn_ref, vn_ref, kr_ref, o_ref):
-    scaling = 1.0 / math.sqrt(q_ref.shape[-1])
-    q = q_ref[...]
+def attention_kernel(q_ref, cos_ref, sin_ref, qr_ref, kp_ref, vp_ref, kn_ref, vn_ref, kr_ref, o_ref):
+    size = kp_ref.shape[-1]
+    heads = q_ref.shape[-1] // size
+    scaling = 1.0 / math.sqrt(size)
+    cosine = cos_ref[...]
+    sine = sin_ref[...]
+    parts = []
+    for head in range(heads):
+        wide = q_ref[:, head * size : (head + 1) * size].astype(jnp.float32)
+        turned = pltpu.roll(wide, size // 2, 1)
+        parts.append((wide * cosine + turned * sine).astype(jnp.bfloat16))
+    q = jnp.concatenate(parts, axis=0)
+    q_rank = jnp.concatenate([qr_ref[...]] * heads, axis=0)
     before = lax.dot_general(
         q, kp_ref[...], (((1,), (1,)), ((), ())), preferred_element_type=jnp.float32
     ) * scaling
     inside = lax.dot_general(
         q, kn_ref[...], (((1,), (1,)), ((), ())), preferred_element_type=jnp.float32
     ) * scaling
-    allowed = kr_ref[...] <= qr_ref[...]
-    inside = jnp.where(allowed, inside, -jnp.inf)
+    inside = jnp.where(kr_ref[...] <= q_rank, inside, -jnp.inf)
     highest = jnp.maximum(
         jnp.max(before, axis=1, keepdims=True), jnp.max(inside, axis=1, keepdims=True)
     )
@@ -82,37 +91,50 @@
     ) + jnp.dot(
         expo_inside.astype(jnp.bfloat16), vn_ref[...], preferred_element_type=jnp.float32
     )
-    o_ref[...] = (mixed / totals).astype(o_ref.dtype)
-
-
-def attend_all(queries, query_rank, prefix_keys, prefix_values, new_keys, new_values,
-               key_rank, key_live, block_rows=256):
-    slots, heads, size = queries.shape
-    rows = slots * heads
-    q = queries.reshape(rows, size)
-    q_rank = jnp.repeat(query_rank, heads).reshape(rows, 1)
+    result = (mixed / totals).astype(o_ref.dtype)
+    rows = q_ref.shape[0]
+    for head in range(heads):
+        o_ref[:, head * size : (head + 1) * size] = result[head * rows : (head + 1) * rows]
+
+
+def attend_rotating(queries, positions, query_rank, prefix_keys, prefix_values, new_keys,
+                    new_values, key_rank, key_live, block_slots=64):
+    slots, width = queries.shape
+    size = prefix_keys.shape[-1]
+    halfway = size // 2
+    frequency = jnp.exp(
+        -math.log(10000.0) * 2.0 * jnp.arange(halfway, dtype=jnp.float32) / size
+    )
+    angles = positions.astype(jnp.float32)[:, None] * frequency[None, :]
+    cosine = jnp.cos(angles)
+    sine = jnp.sin(angles)
+    cos_table = jnp.concatenate([cosine, cosine], axis=1)
+    sin_table = jnp.concatenate([-sine, sine], axis=1)
     big = jnp.iinfo(jnp.int32).max
     k_rank = jnp.where(key_live, key_rank, big).reshape(1, -1)
     prefix_len = prefix_keys.shape[0]
     new_len = new_keys.shape[0]
     full = lambda i: (0, 0)
-    out = pl.pallas_call(
+    by_slot = lambda i: (i, 0)
+    return pl.pallas_call(
         attention_kernel,
-        grid=(rows // block_rows,),
+        grid=(slots // block_slots,),
         in_specs=[
-            pl.BlockSpec((block_rows, size), lambda i: (i, 0)),
-            pl.BlockSpec((block_rows, 1), lambda i: (i, 0)),
+            pl.BlockSpec((block_slots, width), by_slot),
+            pl.BlockSpec((block_slots, size), by_slot),
+            pl.BlockSpec((block_slots, size), by_slot),
+            pl.BlockSpec((block_slots, 1), by_slot),
             pl.BlockSpec((prefix_len, size), full),
             pl.BlockSpec((prefix_len, size), full),
             pl.BlockSpec((new_len, size), full),
             pl.BlockSpec((new_len, size), full),
             pl.BlockSpec((1, new_len), full),
         ],
-        out_specs=pl.BlockSpec((block_rows, size), lambda i: (i, 0)),
-        out_shape=jax.ShapeDtypeStruct((rows, size), jnp.bfloat16),
+        out_specs=pl.BlockSpec((block_slots, width), by_slot),
+        out_shape=jax.ShapeDtypeStruct((slots, width), jnp.bfloat16),
         compiler_params=pltpu.CompilerParams(vmem_limit_bytes=48 * 1024 * 1024),
-    )(q, q_rank, prefix_keys, prefix_values, new_keys, new_values, k_rank)
-    return out.reshape(slots, heads, size)
+    )(queries, cos_table, sin_table, query_rank.reshape(slots, 1), prefix_keys, prefix_values,
+      new_keys, new_values, k_rank)
 
 
 def row_norm(tokens, gain, full_width):
@@ -168,9 +190,6 @@
     slot_rank = jnp.cumsum(live_count) - live_count
     prefix_length = page_table.shape[1] * key_pages.shape[1]
     positions = prefix_length + slot_rank
-    rotated_queries = rotate(
-        arrived[:, :query_width].reshape(slot_total, group_heads, head_size), positions
-    )
     rotated_keys = rotate(
         arrived[:, query_width : query_width + head_size].reshape(slot_total, 1, head_size),
         positions,
@@ -183,8 +202,9 @@
     prefix_values = jnp.take(value_pages[:, :, 0, :], local_pages, axis=0).reshape(
         prefix_length, head_size
     )
-    attended = attend_all(
-        rotated_queries,
+    attended = attend_rotating(
+        arrived[:, :query_width],
+        positions,
         slot_rank,
         prefix_keys,
         prefix_values,

time: 339 us -> 332 us (0.979)
  local copies, waits for them, and re-layouts: 25.8 us -> 17.9 us
    another operation x5 -> x3, local copies, waits for them, and re-layouts: 5.45 us -> 0.2 us  [the longest x1 2.76 us: attend_all(): q_rank = jnp.repeat(query_rank, heads).reshape(rows, 1)]
    another operation x5 -> x4, other arithmetic: 4.92 us -> 1.48 us
where the time goes in v5:
time: 332 us; the launch traced here: 331 us
  waiting for transfers between devices  191 us (58%)
  Pallas kernels  45.9 us (14%)
  other arithmetic  25.2 us (8%)
  local copies, waits for them, and re-layouts  17.9 us (5%)
  matrix products  14.3 us (4%)
  between operations  13.6 us (4%)
  blocking collectives  12.5 us (4%)
  starting transfers between devices  10.9 us (3%)
    all_gather x1, waiting for transfers between devices, body(): gathered = lax.all_gather(weights_local, 'tok', axis=0, tiled=True)  78.9 us
    reduce_scatter x1, waiting for transfers between devices, body(): lax.psum_scatter(joined.reshape(group_count * row_count, joined.shape[2])...  67.6 us
    pallas_call x1, Pallas kernels, attend_rotating(): pl.pallas_call(attention_kernel, grid=(slots // block_slots,), in_specs=[...  45.9 us
    all_to_all x1, waiting for transfers between devices, body(): lax.all_to_all(outgoing, 'tok', split_axis=0, concat_axis=0, tiled=True)  25.7 us
    all_to_all x1, waiting for transfers between devices, body(): lax.all_to_all(attended.reshape(n_tok, capacity, query_width), 'tok', spl...  18.6 us
    dot_general x1, matrix products, body(): jnp.einsum('rd,dnc->nrc', normed, gathered, preferred_element_type=jnp.fl...  14.3 us
    psum x1, blocking collectives, row_norm(): squares = lax.psum(jnp.sum(values_wide * values_wide, axis=1), 'head')  12.5 us
    all_to_all x1, starting transfers between devices, body(): lax.all_to_all(outgoing, 'tok', split_axis=0, concat_axis=0, tiled=True)  7.2 us
  transfers between devices with their start and end apart: 4, of which 4 were waited for; matrix products, arithmetic and copies ran while one was open for 3% of the time, Pallas kernels for 0%

profile of v5, /device:TPU:32, one launch (start us, length us, event | category | flops | bytes accessed | tf_op | source)
XLA Modules:
  0.0 331.0 jit_solution(5376733197192347668)
XLA Ops:
  6.5 1.3 copy.27
  7.9 0.9 copy.28
  8.8 0.9 copy.29
  9.8 1.0 pad_maximum_fusion.1
  11.1 12.5 %psum.7 = f32[512]{0:T(512)S(1)} all-reduce(f32[512]{0:T(512)S(1)} %fusion), channel_id=1, replica_groups=mesh['tok'=16,'head'=8] {'head'}, use_global_device_ids=true, to_apply=%region_4.5 | all-reduce | flops 512 | bytes 4096 | tf_op jit(solution)/shard_map/psum | solution.py:142
  23.7 78.9 %all-gather.2.cloned.1.call-done = bf16[1024,8,768]{2,0,1:T(8,128)(2,1)} async-done(((bf16[64,8,768]{2,0,1:T(8,128)(2,1)}), bf16[1024,8,768]{2,0,1:T(8,128)(2,1)}) %all-gather.2.cloned.1.call-update) | async-done | bytes 12582928 | tf_op jit(solution)/shard_map/all_gather | solution.py:158
  102.6 14.3 %fusion.4 = f32[8,768,512]{1,2,0:T(8,128)} fusion(bf16[1024,8,768]{2,0,1:T(8,128)(2,1)} %all-gather.2.cloned.1.call-done, bf16[512,1024]{1,0:T(8,128)(2,1)S(1)} %copy-done.4, f32[1024]{0:T(1024)S(1)} %convert_element_type.100, f32[512]{0:T(512)S(1)} %add_rsqrt_fusion), kind=kOutput, calls=%fused_computation.11 | convolution fusion | flops 6444548096 | bytes 26220544 | tf_op jit(solution)/shard_map/rd,dnc->nrc/dot_general | solution.py:160
  116.9 0.7 copy-done.5
  117.6 1.1 reduce-window.15
  119.2 67.6 %reduce-scatter.2.cloned.1.call-done = f32[512,768]{1,0:T(8,128)} async-done(((f32[4096,768]{1,0:T(8,128)}), f32[512,768]{1,0:T(8,128)}) %reduce-scatter.2.cloned.1.call-update) | async-done | bytes 1572880 | tf_op jit(solution)/shard_map/reduce_scatter | solution.py:161
  186.7 4.6 %scatter_custom_fusion = bf16[1024,768]{1,0:T(8,128)(2,1)} fusion(s32[512]{0:T(512)S(1)} %bitcast.61, f32[512,768]{1,0:T(8,128)} %reduce-scatter.2.cloned.1.call-done, bf16[]{:T(256)} %constant.20.clone.1), kind=kCustom, calls=%fused_computation.17 | custom fusion | flops 393216 | bytes 3145730 | tf_op jit(solution)/shard_map/scatter | solution.py:175
  191.5 2.8 pad_maximum_fusion
  194.3 7.2 %all-to-all-start = ((bf16[16,80,768]{2,1,0:T(8,128)(2,1)}), bf16[16,80,768]{2,1,0:T(8,128)(2,1)}, u32[]{:S(2)}, u32[]{:S(2)}) async-start(bf16[16,80,768]{2,1,0:T(8,128)(2,1)} %pad_maximum_fusion), calls=%async_computation.1 | async-start | bytes 3932160 | tf_op jit(solution)/shard_map/all_to_all | solution.py:181
  201.6 1.7 gather_fusion.1
  203.3 3.3 gather_fusion.2
  206.6 2.8 broadcast_select_fusion
  209.4 25.7 %all-to-all-done = bf16[16,80,768]{2,1,0:T(8,128)(2,1)} async-done(((bf16[16,80,768]{2,1,0:T(8,128)(2,1)}), bf16[16,80,768]{2,1,0:T(8,128)(2,1)}, u32[]{:S(2)}, u32[]{:S(2)}) %all-to-all-start) | async-done | bytes 1966112 | tf_op jit(solution)/shard_map/all_to_all | solution.py:181
  235.1 1.1 fusion.25
  236.6 1.6 slice.52
  238.1 0.8 fusion.29
  238.9 1.1 slice.53.q_ref
  240.1 0.3 reduce-window.19
  240.7 3.1 fusion.21
  243.8 4.3 %fusion.20 = (bf16[1024,64]{1,0:T(8,128)(2,1)}, bf16[1024,64]{1,0:T(8,128)(2,1)}) fusion(f32[64]{0:T(128)S(1)} %multiply_exponential_fusion, f32[1024]{0:T(1024)S(1)} %get-tuple-element.10, bf16[1024,1,128]{2,0,1:T(8,128)(2,1)} %get-tuple-element.13), kind=kLoop, calls=%fused_computation.35 | loop fusion | flops 720896 | bytes 528640 | tf_op jit(solution)/shard_map/concatenate | solution.py:24
  248.2 1.0 copy.30.qr_ref
  249.2 1.3 pad_maximum_fusion.4.kn_ref
  250.5 1.9 pad_maximum_fusion.2
  252.4 45.9 %shard_map.91 = bf16[1024,512]{1,0:T(8,128)(2,1)S(1)} custom-call(bf16[1024,512]{1,0:T(8,128)(2,1)S(1)} %copy-done.1, f32[1024,128]{1,0:T(8,128)S(1)} %get-tuple-element.21.cos_ref, f32[1024,128]{1,0:T(8,128)S(1)} %get-tuple-element.22.sin_ref, s32[1024,1]{1,0:T(8,128)S(1)} %copy-done.3, bf16[4096,128]{1,0:T(8,128)(2,1)S(1)} %bitcast.48, ...), custom_call_target="tpu_custom_call" | custom-call | tf_op jit(solution)/shard_map/pallas_call | solution.py:119
  298.3 1.0 copy-done.2
  299.3 3.7 %all-to-all-start.1 = ((bf16[16,64,512]{2,1,0:T(8,128)(2,1)}), bf16[16,64,512]{2,1,0:T(8,128)(2,1)S(1)}, u32[]{:S(2)}, u32[]{:S(2)}) async-start(bf16[16,64,512]{2,1,0:T(8,128)(2,1)} %bitcast.49), calls=%async_computation.2 | async-start | bytes 2097152 | tf_op jit(solution)/shard_map/all_to_all | solution.py:216
  303.0 18.6 %all-to-all-done.1 = bf16[16,64,512]{2,1,0:T(8,128)(2,1)S(1)} async-done(((bf16[16,64,512]{2,1,0:T(8,128)(2,1)}), bf16[16,64,512]{2,1,0:T(8,128)(2,1)S(1)}, u32[]{:S(2)}, u32[]{:S(2)}) %all-to-all-start.1) | async-done | bytes 1048608 | tf_op jit(solution)/shard_map/all_to_all | solution.py:216
  321.5 2.6 gather_fusion
  (49 shorter events, 1.9 us)
Async XLA Ops:
  6.5 195.1 %copy-start = (bf16[64,128,1,128]{3,1,2,0:T(8,128)(2,1)S(1)}, bf16[64,128,1,128]{3,1,2,0:T(8,128)(2,1)}, u32[]{:S(2)}) copy-start(bf16[64,128,1,128]{3,1,2,0:T(8,128)(2,1)} %param.17) | copy-start | bytes 6291460
  6.5 4.3 %copy-start.6 = (bf16[1024]{0:T(1024)(128)(2,1)S(1)}, bf16[1024]{0:T(1024)(128)(2,1)}, u32[]{:S(2)}) copy-start(bf16[1024]{0:T(1024)(128)(2,1)} %param.12) | copy-start | bytes 6148
  6.5 4.3 %copy-start.4 = (bf16[512,1024]{1,0:T(8,128)(2,1)S(1)}, bf16[512,1024]{1,0:T(8,128)(2,1)}, u32[]{:S(2)}) copy-start(bf16[512,1024]{1,0:T(8,128)(2,1)} %param.11) | copy-start | bytes 3145732
  6.5 96.1 %all-gather.2.cloned.1.call-start = ((), (), s32[]{:S(2)}) async-start(), calls=%async_computation.3 | async-start | bytes 13369344 | tf_op jit(solution)/shard_map/all_gather | solution.py:158
  10.8 176.0 %reduce-scatter.2.cloned.1.call-start = ((), (), s32[]{:S(2)}) async-start(), calls=%async_computation.4 | async-start | bytes 14155776 | tf_op jit(solution)/shard_map/reduce_scatter | solution.py:161
  116.9 0.7 copy-start.5
  194.3 7.3 %copy-start.7 = (s32[1,32]{1,0:T(1,128)S(1)}, s32[1,32]{1,0:T(1,128)}, u32[]{:S(2)}) copy-start(s32[1,32]{1,0:T(1,128)} %param.19) | copy-start | bytes 388
  194.3 40.8 %all-to-all-start = ((bf16[16,80,768]{2,1,0:T(8,128)(2,1)}), bf16[16,80,768]{2,1,0:T(8,128)(2,1)}, u32[]{:S(2)}, u32[]{:S(2)}) async-start(bf16[16,80,768]{2,1,0:T(8,128)(2,1)} %pad_maximum_fusion), calls=%async_computation.1 | async-start | bytes 3932160 | tf_op jit(solution)/shard_map/all_to_all | solution.py:181
  249.2 3.2 copy-start.1
  249.2 3.2 copy-start.3
  298.3 1.0 copy-start.2
  299.3 22.2 %all-to-all-start.1 = ((bf16[16,64,512]{2,1,0:T(8,128)(2,1)}), bf16[16,64,512]{2,1,0:T(8,128)(2,1)S(1)}, u32[]{:S(2)}, u32[]{:S(2)}) async-start(bf16[16,64,512]{2,1,0:T(8,128)(2,1)} %bitcast.49), calls=%async_computation.2 | async-start | bytes 2097152 | tf_op jit(solution)/shard_map/all_to_all | solution.py:216
Sparse Core Ops, SparseCore 0:
  10.9 91.6 all-gather.1
  117.0 69.6 reduce-scatter.1

commit v6 on v5

--- a/solution.py
+++ b/solution.py
@@ -97,9 +97,9 @@
         o_ref[:, head * size : (head + 1) * size] = result[head * rows : (head + 1) * rows]
 
 
-def attend_rotating(queries, positions, query_rank, prefix_keys, prefix_values, new_keys,
-                    new_values, key_rank, key_live, block_slots=64):
-    slots, width = queries.shape
+def attend_rotating(arrived, width, positions, query_rank, prefix_keys, prefix_values, new_keys,
+                    key_rank, key_live, block_slots=64):
+    slots = arrived.shape[0]
     size = prefix_keys.shape[-1]
     halfway = size // 2
     frequency = jnp.exp(
@@ -127,14 +127,14 @@
             pl.BlockSpec((prefix_len, size), full),
             pl.BlockSpec((prefix_len, size), full),
             pl.BlockSpec((new_len, size), full),
-            pl.BlockSpec((new_len, size), full),
+            pl.BlockSpec((new_len, size), lambda i: (0, width // size + 1)),
             pl.BlockSpec((1, new_len), full),
         ],
         out_specs=pl.BlockSpec((block_slots, width), by_slot),
         out_shape=jax.ShapeDtypeStruct((slots, width), jnp.bfloat16),
         compiler_params=pltpu.CompilerParams(vmem_limit_bytes=48 * 1024 * 1024),
-    )(queries, cos_table, sin_table, query_rank.reshape(slots, 1), prefix_keys, prefix_values,
-      new_keys, new_values, k_rank)
+    )(arrived, cos_table, sin_table, query_rank.reshape(slots, 1), prefix_keys, prefix_values,
+      new_keys, arrived, k_rank)
 
 
 def row_norm(tokens, gain, full_width):
@@ -170,17 +170,14 @@
     member = (group_of[:, None] == jnp.arange(n_tok, dtype=jnp.int32)[None, :]).astype(jnp.int32)
     local_rank = jnp.sum((jnp.cumsum(member, axis=0) - member) * member, axis=1)
     slot_index = group_of * capacity + local_rank
-    counts_local = jnp.sum(member, axis=0).astype(jnp.bfloat16)
+    counts_local = jnp.sum(member, axis=0).reshape(n_tok, 1)
+    block_counts = lax.all_to_all(counts_local, "tok", 0, 0, tiled=True).reshape(n_tok)
     outgoing = (
         jnp.zeros((n_tok * capacity, width_all), jnp.bfloat16).at[slot_index].set(projected_low)
     )
-    count_rows = jnp.broadcast_to(counts_local[:, None, None], (n_tok, 16, width_all))
-    outgoing = jnp.concatenate(
-        [outgoing.reshape(n_tok, capacity, width_all), count_rows], axis=1
-    )
-    arrived_all = lax.all_to_all(outgoing, "tok", split_axis=0, concat_axis=0, tiled=True)
-    block_counts = arrived_all[:, capacity, 0].astype(jnp.int32)
-    arrived = arrived_all[:, :capacity, :]
+    arrived = lax.all_to_all(
+        outgoing.reshape(n_tok, capacity, width_all), "tok", 0, 0, tiled=True
+    )
     slot_total = n_tok * capacity
     arrived = arrived.reshape(slot_total, width_all)
     live_count = (
@@ -194,7 +191,6 @@
         arrived[:, query_width : query_width + head_size].reshape(slot_total, 1, head_size),
         positions,
     )[:, 0, :]
-    slot_values = arrived[:, query_width + head_size :]
     local_pages = page_table[0] - lax.axis_index("tok") * key_pages.shape[0]
     prefix_keys = jnp.take(key_pages[:, :, 0, :], local_pages, axis=0).reshape(
         prefix_length, head_size
@@ -203,13 +199,13 @@
         prefix_length, head_size
     )
     attended = attend_rotating(
-        arrived[:, :query_width],
+        arrived,
+        query_width,
         positions,
         slot_rank,
         prefix_keys,
         prefix_values,
         rotated_keys,
-        slot_values,
         slot_rank,
         key_live,
     )

time: 332 us -> 310 us (0.934)
  waiting for transfers between devices: 191 us -> 173 us
  other arithmetic: 25.2 us -> 16.8 us
  starting transfers between devices: 10.9 us -> 16 us
    reduce_scatter x1, waiting for transfers between devices: 67.6 us -> 53.7 us  [body(): lax.psum_scatter(joined.reshape(group_count * row_count, joined.shape[2])...]
    all_to_all x1 -> x2, starting transfers between devices: 7.2 us -> 12.3 us  [the longest x1 7.08 us: body(): lax.all_to_all(outgoing.reshape(n_tok, capacity, width_all), 'tok', 0, 0,...]
    all_to_all x1 -> x2, waiting for transfers between devices: 25.7 us -> 22.2 us  [the longest x1 22.2 us: body(): lax.all_to_all(outgoing.reshape(n_tok, capacity, width_all), 'tok', 0, 0,...]
    slice x4 -> x1, local copies, waits for them, and re-layouts: 3.61 us -> 0.22 us  [the longest x1 1.56 us: body(): arrived = arrived_all[:, :capacity, :]]
  transfers between devices with their start and end apart: 4 -> 5, of which waited for: 4 -> 4; matrix products, arithmetic and copies ran while one was open for 3% -> 7% of each run, Pallas kernels for 0% -> 0%
where the time goes in v6:
time: 310 us; the launch traced here: 309 us
  waiting for transfers between devices  173 us (56%)
  Pallas kernels  45.7 us (15%)
  local copies, waits for them, and re-layouts  17.3 us (6%)
  other arithmetic  16.8 us (5%)
  starting transfers between devices  16 us (5%)
  matrix products  14.4 us (5%)
  between operations  13.6 us (4%)
  blocking collectives  12.5 us (4%)
    all_gather x1, waiting for transfers between devices, body(): gathered = lax.all_gather(weights_local, 'tok', axis=0, tiled=True)  78.9 us
    reduce_scatter x1, waiting for transfers between devices, body(): lax.psum_scatter(joined.reshape(group_count * row_count, joined.shape[2])...  53.7 us
    pallas_call x1, Pallas kernels, attend_rotating(): pl.pallas_call(attention_kernel, grid=(slots // block_slots,), in_specs=[...  45.7 us
    all_to_all x1, waiting for transfers between devices, body(): lax.all_to_all(outgoing.reshape(n_tok, capacity, width_all), 'tok', 0, 0,...  22.2 us
    all_to_all x1, waiting for transfers between devices, body(): lax.all_to_all(attended.reshape(n_tok, capacity, query_width), 'tok', spl...  18.2 us
    dot_general x1, matrix products, body(): jnp.einsum('rd,dnc->nrc', normed, gathered, preferred_element_type=jnp.fl...  14.4 us
    psum x1, blocking collectives, row_norm(): squares = lax.psum(jnp.sum(values_wide * values_wide, axis=1), 'head')  12.5 us
    all_to_all x1, starting transfers between devices, body(): lax.all_to_all(outgoing.reshape(n_tok, capacity, width_all), 'tok', 0, 0,...  7.08 us
  transfers between devices with their start and end apart: 5, of which 4 were waited for; matrix products, arithmetic and copies ran while one was open for 7% of the time, Pallas kernels for 0%

profile of v6, /device:TPU:32, one launch (start us, length us, event | category | flops | bytes accessed | tf_op | source)
XLA Modules:
  0.0 309.4 jit_solution(12866041901267580659)
XLA Ops:
  6.5 1.1 copy.36
  7.6 0.9 copy.35
  8.6 1.2 copy.34
  9.8 1.0 pad_maximum_fusion
  10.8 0.3 fusion
  11.1 12.5 %psum.7 = f32[512]{0:T(512)S(1)} all-reduce(f32[512]{0:T(512)S(1)} %fusion), channel_id=1, replica_groups=mesh['tok'=16,'head'=8] {'head'}, use_global_device_ids=true, to_apply=%region_4.5 | all-reduce | flops 512 | bytes 4096 | tf_op jit(solution)/shard_map/psum | solution.py:142
  23.6 78.9 %all-gather.2.cloned.1.call-done = bf16[1024,8,768]{2,0,1:T(8,128)(2,1)} async-done(((bf16[64,8,768]{2,0,1:T(8,128)(2,1)}), bf16[1024,8,768]{2,0,1:T(8,128)(2,1)}) %all-gather.2.cloned.1.call-update) | async-done | bytes 12582928 | tf_op jit(solution)/shard_map/all_gather | solution.py:158
  102.5 14.4 %fusion.4 = f32[8,768,512]{1,2,0:T(8,128)} fusion(bf16[1024,8,768]{2,0,1:T(8,128)(2,1)} %all-gather.2.cloned.1.call-done, bf16[512,1024]{1,0:T(8,128)(2,1)S(1)} %copy-done.6, f32[1024]{0:T(1024)S(1)} %convert_element_type.77, f32[512]{0:T(512)S(1)} %add_rsqrt_fusion), kind=kOutput, calls=%fused_computation.10 | convolution fusion | flops 6444548096 | bytes 26220544 | tf_op jit(solution)/shard_map/rd,dnc->nrc/dot_general | solution.py:160
  116.9 0.7 copy-done.7
  117.6 1.1 reduce-window.15
  119.1 0.7 copy.37
  119.8 5.3 %all-to-all-start.1 = ((s32[16,1,1]{2,1,0:T(1,128)}), s32[16,1,1]{2,1,0:T(1,128)S(1)}, u32[]{:S(2)}, u32[]{:S(2)}) async-start(s32[16,1,1]{2,1,0:T(1,128)} %copy.37), calls=%async_computation.2 | async-start | bytes 16384 | tf_op jit(solution)/shard_map/all_to_all | solution.py:174
  125.2 1.7 gather_fusion.2
  126.9 3.3 %gather_fusion.1 = bf16[32,128,128]{2,1,0:T(8,128)(2,1)} fusion(bf16[64,128,128]{2,1,0:T(8,128)(2,1)} %bitcast.55, s32[1024]{0:T(1024)S(1)} %pad_clamp_fusion.1), kind=kCustom, calls=%fused_computation.clone | custom fusion | bytes 2097280 | tf_op jit(solution)/shard_map/jit(_take)/gather | solution.py:195
  130.2 2.8 broadcast_select_fusion
  133.0 53.7 %reduce-scatter.2.cloned.1.call-done = f32[512,768]{1,0:T(8,128)} async-done(((f32[4096,768]{1,0:T(8,128)}), f32[512,768]{1,0:T(8,128)}) %reduce-scatter.2.cloned.1.call-update) | async-done | bytes 1572880 | tf_op jit(solution)/shard_map/reduce_scatter | solution.py:161
  186.7 4.6 %scatter_custom_fusion = bf16[1024,768]{1,0:T(8,128)(2,1)} fusion(s32[512]{0:T(512)S(1)} %bitcast.60, f32[512,768]{1,0:T(8,128)} %reduce-scatter.2.cloned.1.call-done, bf16[]{:T(256)} %constant.20.clone.1), kind=kCustom, calls=%fused_computation.16 | custom fusion | flops 393216 | bytes 3145730 | tf_op jit(solution)/shard_map/scatter | solution.py:176
  191.4 7.1 %all-to-all-start = ((bf16[16,64,768]{2,1,0:T(8,128)(2,1)}), bf16[16,64,768]{2,1,0:T(8,128)(2,1)}, u32[]{:S(2)}, u32[]{:S(2)}) async-start(bf16[16,64,768]{2,1,0:T(8,128)(2,1)} %bitcast.54), calls=%async_computation.1 | async-start | bytes 3145728 | tf_op jit(solution)/shard_map/all_to_all | solution.py:178
  198.5 0.4 reduce.1
  199.4 0.3 reduce-window.19
  200.0 1.0 copy.38.qr_ref
  201.0 1.9 fusion.21
  202.9 1.3 pad_maximum_fusion.1
  204.3 22.2 %all-to-all-done = bf16[16,64,768]{2,1,0:T(8,128)(2,1)} async-done(((bf16[16,64,768]{2,1,0:T(8,128)(2,1)}), bf16[16,64,768]{2,1,0:T(8,128)(2,1)}, u32[]{:S(2)}, u32[]{:S(2)}) %all-to-all-start) | async-done | bytes 1572896 | tf_op jit(solution)/shard_map/all_to_all | solution.py:178
  226.5 1.1 slice_bitcast_fusion
  227.6 2.5 fusion.20
  230.3 1.0 copy-done.5
  231.3 45.7 %shard_map.91 = bf16[1024,512]{1,0:T(8,128)(2,1)S(1)} custom-call(bf16[1024,768]{1,0:T(8,128)(2,1)} %bitcast.9.q_ref.vn_ref, f32[1024,128]{1,0:T(8,128)S(1)} %copy-done.3, f32[1024,128]{1,0:T(8,128)S(1)} %copy-done.4, s32[1024,1]{1,0:T(8,128)S(1)} %copy-done.5, bf16[4096,128]{1,0:T(8,128)(2,1)S(1)} %bitcast.50, bf16[4096,128]{1,0:T(8,128)(2,1)S(1)} %bitcast.49, ...), custom_call_target="tpu_custom_call" | custom-call | tf_op jit(solution)/shard_map/pallas_call | solution.py:119
  277.0 1.0 copy-done.2
  278.0 3.7 %all-to-all-start.2 = ((bf16[16,64,512]{2,1,0:T(8,128)(2,1)}), bf16[16,64,512]{2,1,0:T(8,128)(2,1)S(1)}, u32[]{:S(2)}, u32[]{:S(2)}) async-start(bf16[16,64,512]{2,1,0:T(8,128)(2,1)} %bitcast.51), calls=%async_computation.3 | async-start | bytes 2097152 | tf_op jit(solution)/shard_map/all_to_all | solution.py:212
  281.7 18.2 %all-to-all-done.2 = bf16[16,64,512]{2,1,0:T(8,128)(2,1)S(1)} async-done(((bf16[16,64,512]{2,1,0:T(8,128)(2,1)}), bf16[16,64,512]{2,1,0:T(8,128)(2,1)S(1)}, u32[]{:S(2)}, u32[]{:S(2)}) %all-to-all-start.2) | async-done | bytes 1048608 | tf_op jit(solution)/shard_map/all_to_all | solution.py:212
  299.9 2.6 gather_fusion
  (51 shorter events, 1.7 us)
Async XLA Ops:
  6.5 118.7 %copy-start = (bf16[64,128,1,128]{3,1,2,0:T(8,128)(2,1)S(1)}, bf16[64,128,1,128]{3,1,2,0:T(8,128)(2,1)}, u32[]{:S(2)}) copy-start(bf16[64,128,1,128]{3,1,2,0:T(8,128)(2,1)} %param.18) | copy-start | bytes 6291460
  6.5 4.2 %copy-start.8 = (bf16[1024]{0:T(1024)(128)(2,1)S(1)}, bf16[1024]{0:T(1024)(128)(2,1)}, u32[]{:S(2)}) copy-start(bf16[1024]{0:T(1024)(128)(2,1)} %param.12) | copy-start | bytes 6148
  6.5 4.3 %copy-start.6 = (bf16[512,1024]{1,0:T(8,128)(2,1)S(1)}, bf16[512,1024]{1,0:T(8,128)(2,1)}, u32[]{:S(2)}) copy-start(bf16[512,1024]{1,0:T(8,128)(2,1)} %param.11) | copy-start | bytes 3145732
  6.5 96.0 %all-gather.2.cloned.1.call-start = ((), (), s32[]{:S(2)}) async-start(), calls=%async_computation.4 | async-start | bytes 13369344 | tf_op jit(solution)/shard_map/all_gather | solution.py:158
  10.7 176.0 %reduce-scatter.2.cloned.1.call-start = ((), (), s32[]{:S(2)}) async-start(), calls=%async_computation.5 | async-start | bytes 14155776 | tf_op jit(solution)/shard_map/reduce_scatter | solution.py:161
  116.9 0.7 copy-start.7
  116.9 8.3 %copy-start.9 = (s32[1,32]{1,0:T(1,128)S(1)}, s32[1,32]{1,0:T(1,128)}, u32[]{:S(2)}) copy-start(s32[1,32]{1,0:T(1,128)} %param.19) | copy-start | bytes 388
  119.8 71.6 %all-to-all-start.1 = ((s32[16,1,1]{2,1,0:T(1,128)}), s32[16,1,1]{2,1,0:T(1,128)S(1)}, u32[]{:S(2)}, u32[]{:S(2)}) async-start(s32[16,1,1]{2,1,0:T(1,128)} %copy.37), calls=%async_computation.2 | async-start | bytes 16384 | tf_op jit(solution)/shard_map/all_to_all | solution.py:174
  191.4 35.1 %all-to-all-start = ((bf16[16,64,768]{2,1,0:T(8,128)(2,1)}), bf16[16,64,768]{2,1,0:T(8,128)(2,1)}, u32[]{:S(2)}, u32[]{:S(2)}) async-start(bf16[16,64,768]{2,1,0:T(8,128)(2,1)} %bitcast.54), calls=%async_computation.1 | async-start | bytes 3145728 | tf_op jit(solution)/shard_map/all_to_all | solution.py:178
  226.5 3.8 %copy-start.1 = (bf16[32,128,128]{2,1,0:T(8,128)(2,1)S(1)}, bf16[32,128,128]{2,1,0:T(8,128)(2,1)}, u32[]{:S(2)}) copy-start(bf16[32,128,128]{2,1,0:T(8,128)(2,1)} %get-tuple-element.18) | copy-start | bytes 3145732
  226.5 3.8 %copy-start.3 = (f32[1024,128]{1,0:T(8,128)S(1)}, f32[1024,128]{1,0:T(8,128)}, u32[]{:S(2)}) copy-start(f32[1024,128]{1,0:T(8,128)} %get-tuple-element.19.cos_ref) | copy-start | bytes 1572868
  226.5 3.8 %copy-start.4 = (f32[1024,128]{1,0:T(8,128)S(1)}, f32[1024,128]{1,0:T(8,128)}, u32[]{:S(2)}) copy-start(f32[1024,128]{1,0:T(8,128)} %get-tuple-element.20.sin_ref) | copy-start | bytes 1572868
  230.3 1.0 copy-start.5
  277.0 1.0 copy-start.2
  278.0 21.9 %all-to-all-start.2 = ((bf16[16,64,512]{2,1,0:T(8,128)(2,1)}), bf16[16,64,512]{2,1,0:T(8,128)(2,1)S(1)}, u32[]{:S(2)}, u32[]{:S(2)}) async-start(bf16[16,64,512]{2,1,0:T(8,128)(2,1)} %bitcast.51), calls=%async_computation.3 | async-start | bytes 2097152 | tf_op jit(solution)/shard_map/all_to_all | solution.py:212
Sparse Core Ops, SparseCore 0:
  10.9 91.6 all-gather.1
  117.1 69.6 reduce-scatter.1

commit v7 on v6

--- a/solution.py
+++ b/solution.py
@@ -153,17 +153,24 @@
     group_heads = query_width // head_size
     full_width = tokens.shape[1] * n_head
     capacity = 2 * row_count // n_tok
-    normed = row_norm(tokens, gain, full_width)
     weights_local = jnp.concatenate([w_query, w_key, w_value], axis=2)
-    gathered = lax.all_gather(weights_local, "tok", axis=0, tiled=True)
-    group_count = row_count * lax.axis_size("head") // row_count
-    joined = jnp.einsum("rd,dnc->nrc", normed, gathered, preferred_element_type=jnp.float32)
-    projected = lax.psum_scatter(
-        joined.reshape(group_count * row_count, joined.shape[2]),
-        "head",
-        scatter_dimension=0,
-        tiled=True,
-    )
+    weights_head = lax.all_to_all(weights_local, "head", 1, 0, tiled=True)
+    weights_head = weights_head.reshape(n_head, -1, weights_head.shape[-1])
+    gathered = lax.all_gather(weights_head, "tok", axis=1, tiled=True)
+    gathered = gathered.reshape(-1, gathered.shape[-1])
+    gain_rows = jnp.broadcast_to(gain[None, :], (16, gain.shape[0]))
+    stacked = lax.all_gather(
+        jnp.concatenate([tokens, gain_rows], axis=0), "head", axis=1, tiled=True
+    )
+    tokens_full = stacked[:row_count]
+    gain_full = stacked[row_count]
+    values_wide = tokens_full.astype(jnp.float32)
+    squares = jnp.sum(values_wide * values_wide, axis=1)
+    factor = lax.rsqrt(squares / full_width + EPS)
+    normed = (values_wide * factor[:, None] * gain_full.astype(jnp.float32)[None, :]).astype(
+        jnp.bfloat16
+    )
+    projected = jnp.dot(normed, gathered, preferred_element_type=jnp.float32)
     projected_low = projected.astype(jnp.bfloat16)
     width_all = projected_low.shape[1]
     group_of = group_ids[:, 0]

time: 310 us -> 286 us (0.923)
  waiting for transfers between devices: 173 us -> 139 us
  blocking collectives: 12.5 us -> 18.4 us
    reduce_scatter x1 -> x0, waiting for transfers between devices: 53.7 us -> none  [body(): lax.psum_scatter(joined.reshape(group_count * row_count, joined.shape[2])...]
    all_gather x1 -> x2, waiting for transfers between devices: 78.9 us -> 104 us  [the longest x1 86.8 us: body(): gathered = lax.all_gather(weights_head, 'tok', axis=1, tiled=True)]
    all_to_all x0 -> x1, blocking collectives: none -> 18.4 us  [body(): weights_head = lax.all_to_all(weights_local, 'head', 1, 0, tiled=True)]
    psum x1 -> x0, blocking collectives: 12.5 us -> none  [row_norm(): squares = lax.psum(jnp.sum(values_wide * values_wide, axis=1), 'head')]
    reduce_sum x1, other arithmetic: 0.28 us -> 5.1 us  [body(): squares = jnp.sum(values_wide * values_wide, axis=1)]
    scatter x1 -> x0, other arithmetic: 4.65 us -> none  [body(): jnp.zeros((n_tok * capacity, width_all), jnp.bfloat16).at[slot_index]]
    scatter x0 -> x1, local copies, waits for them, and re-layouts: none -> 4.37 us  [body(): jnp.zeros((n_tok * capacity, width_all), jnp.bfloat16).at[slot_index]]
    all_to_all x1, waiting for transfers between devices: 22.2 us -> 18.5 us  [body(): lax.all_to_all(outgoing.reshape(n_tok, capacity, width_all), 'tok', 0, 0,...]
  transfers between devices with their start and end apart: 5 -> 5, of which waited for: 4 -> 4; matrix products, arithmetic and copies ran while one was open for 7% -> 14% of each run, Pallas kernels for 0% -> 0%
where the time goes in v7:
time: 286 us; the launch traced here: 285 us
  waiting for transfers between devices  139 us (49%)
  Pallas kernels  45.7 us (16%)
  other arithmetic  19.4 us (7%)
  local copies, waits for them, and re-layouts  18.9 us (7%)
  blocking collectives  18.4 us (6%)
  starting transfers between devices  16.3 us (6%)
  matrix products  13.7 us (5%)
  between operations  13.7 us (5%)
    all_gather x1, waiting for transfers between devices, body(): gathered = lax.all_gather(weights_head, 'tok', axis=1, tiled=True)  86.8 us
    pallas_call x1, Pallas kernels, attend_rotating(): pl.pallas_call(attention_kernel, grid=(slots // block_slots,), in_specs=[...  45.7 us
    all_to_all x1, waiting for transfers between devices, body(): lax.all_to_all(outgoing.reshape(n_tok, capacity, width_all), 'tok', 0, 0,...  18.5 us
    all_to_all x1, blocking collectives, body(): weights_head = lax.all_to_all(weights_local, 'head', 1, 0, tiled=True)  18.4 us
    all_gather x1, waiting for transfers between devices, body(): lax.all_gather(jnp.concatenate([tokens, gain_rows], axis=0), 'head', axis...  16.8 us
    all_to_all x1, waiting for transfers between devices, body(): lax.all_to_all(attended.reshape(n_tok, capacity, query_width), 'tok', spl...  16.8 us
    dot_general x1, matrix products, body(): projected = jnp.dot(normed, gathered, preferred_element_type=jnp.float32)  13.7 us
    all_to_all x1, starting transfers between devices, body(): lax.all_to_all(counts_local, 'tok', 0, 0, tiled=True).reshape(n_tok)  7.26 us
  transfers between devices with their start and end apart: 5, of which 4 were waited for; matrix products, arithmetic and copies ran while one was open for 14% of the time, Pallas kernels for 0%

profile of v7, /device:TPU:32, one launch (start us, length us, event | category | flops | bytes accessed | tf_op | source)
XLA Modules:
  0.0 285.0 jit_solution(9652371199040019829)
XLA Ops:
  6.6 0.8 broadcast_in_dim.14
  7.4 2.3 pad_maximum_fusion
  9.9 0.2 copy.31
  10.2 18.4 %all_to_all.34 = bf16[64,8,768]{2,0,1:T(8,128)(2,1)} all-to-all(bf16[64,8,768]{2,0,1:T(8,128)(2,1)S(1)} %pad_maximum_fusion.1), channel_id=1, replica_groups=mesh['tok'=16,'head'=8] {'head'}, dimensions={1} | all-to-all | bytes 1572864 | tf_op jit(solution)/shard_map/all_to_all | solution.py:157
  28.7 1.2 reduce-window.15
  29.8 0.2 slice_reduce_fusion
  30.2 0.7 copy.34
  30.9 7.3 %all-to-all-start.2 = ((s32[16,1,1]{2,1,0:T(1,128)}), s32[16,1,1]{2,1,0:T(1,128)S(1)}, u32[]{:S(2)}, u32[]{:S(2)}) async-start(s32[16,1,1]{2,1,0:T(1,128)} %copy.34), calls=%async_computation.2 | async-start | bytes 16384 | tf_op jit(solution)/shard_map/all_to_all | solution.py:181
  38.3 1.7 gather_fusion.2
  40.0 3.4 %gather_fusion.1 = bf16[32,128,128]{2,1,0:T(8,128)(2,1)} fusion(bf16[64,128,128]{2,1,0:T(8,128)(2,1)} %bitcast.54, s32[1024]{0:T(1024)S(1)} %pad_clamp_fusion.1), kind=kCustom, calls=%fused_computation.clone | custom fusion | bytes 2097280 | tf_op jit(solution)/shard_map/jit(_take)/gather | solution.py:202
  43.4 2.9 %broadcast_select_fusion = (bf16[32,128,128]{2,1,0:T(8,128)(2,1)S(1)}, bf16[32,128,128]{2,1,0:T(8,128)(2,1)}) fusion(bf16[32,128,128]{2,1,0:T(8,128)(2,1)} %gather_fusion.2, pred[32]{0:T(512)(128)(4,1)S(1)} %get-tuple-element.8, bf16[32,128,128]{2,1,0:T(8,128)(2,1)} %gather_fusion.1), kind=kLoop, calls=%fused_computation.15 | loop fusion | flops 1048576 | bytes 4194336 | tf_op jit(solution)/shard_map/jit(_take)/select_n | solution.py:205
  46.2 16.8 %all-gather.4.cloned.1.call-done = bf16[528,8192]{1,0:T(8,128)(2,1)} async-done(((bf16[528,1024]{1,0:T(8,128)(2,1)}), bf16[528,8192]{1,0:T(8,128)(2,1)}) %all-gather.4.cloned.1.call-update) | async-done | bytes 8650768 | tf_op jit(solution)/shard_map/all_gather | solution.py:162
  63.0 5.1 %fusion = f32[512]{0:T(512)S(1)} fusion(bf16[528,8192]{1,0:T(8,128)(2,1)} %all-gather.4.cloned.1.call-done), kind=kLoop, calls=%fused_computation.6 | loop fusion | flops 12582400 | bytes 8390656 | tf_op jit(solution)/shard_map/reduce_sum | solution.py:168
  68.1 0.9 slice_convert_fusion
  69.1 86.8 %all-gather.6.cloned.1.call-done = bf16[8,1024,1,768]{3,1,0,2:T(8,128)(2,1)} async-done(((bf16[8,64,1,768]{3,1,0,2:T(8,128)(2,1)}), bf16[8,1024,1,768]{3,1,0,2:T(8,128)(2,1)}) %all-gather.6.cloned.1.call-update) | async-done | bytes 12582928 | tf_op jit(solution)/shard_map/all_gather | solution.py:159
  155.8 13.7 %fusion.8 = bf16[512,768]{1,0:T(8,128)(2,1)} fusion(bf16[8192,768]{1,0:T(8,128)(2,1)} %bitcast.64, f32[8192]{0:T(1024)S(1)} %bitcast.57, f32[512]{0:T(512)S(1)} %add_rsqrt_fusion, bf16[528,8192]{1,0:T(8,128)(2,1)} %all-gather.4.cloned.1.call-done), kind=kOutput, calls=%fused_computation.13 | convolution fusion | flops 6459621376 | bytes 21792768 | tf_op jit(solution)/shard_map/dot_general | solution.py:173
  169.5 4.4 %scatter_custom_fusion = bf16[1024,768]{1,0:T(8,128)(2,1)} fusion(s32[512]{0:T(512)S(1)} %bitcast.60, bf16[512,768]{1,0:T(8,128)(2,1)} %fusion.8, bf16[]{:T(256)} %constant.20.clone.1), kind=kCustom, calls=%fused_computation.18 | custom fusion | bytes 1573376 | tf_op jit(solution)/shard_map/scatter | solution.py:183
  173.9 5.3 %all-to-all-start.1 = ((bf16[16,64,768]{2,1,0:T(8,128)(2,1)}), bf16[16,64,768]{2,1,0:T(8,128)(2,1)}, u32[]{:S(2)}, u32[]{:S(2)}) async-start(bf16[16,64,768]{2,1,0:T(8,128)(2,1)} %bitcast.52), calls=%async_computation.1 | async-start | bytes 3145728 | tf_op jit(solution)/shard_map/all_to_all | solution.py:185
  179.2 0.4 reduce.1
  180.2 0.3 reduce-window.19
  180.8 1.0 copy.35.qr_ref
  181.8 1.9 fusion.23
  183.7 1.3 pad_maximum_fusion.2
  185.0 18.5 %all-to-all-done.1 = bf16[16,64,768]{2,1,0:T(8,128)(2,1)} async-done(((bf16[16,64,768]{2,1,0:T(8,128)(2,1)}), bf16[16,64,768]{2,1,0:T(8,128)(2,1)}, u32[]{:S(2)}, u32[]{:S(2)}) %all-to-all-start.1) | async-done | bytes 1572896 | tf_op jit(solution)/shard_map/all_to_all | solution.py:185
  203.5 1.1 slice_bitcast_fusion
  204.6 2.5 fusion.22
  207.3 1.0 copy-done.5
  208.4 45.7 %shard_map.91 = bf16[1024,512]{1,0:T(8,128)(2,1)S(1)} custom-call(bf16[1024,768]{1,0:T(8,128)(2,1)} %bitcast.10.q_ref.vn_ref, f32[1024,128]{1,0:T(8,128)S(1)} %copy-done.3, f32[1024,128]{1,0:T(8,128)S(1)} %copy-done.4, s32[1024,1]{1,0:T(8,128)S(1)} %copy-done.5, bf16[4096,128]{1,0:T(8,128)(2,1)S(1)} %bitcast.49, bf16[4096,128]{1,0:T(8,128)(2,1)S(1)} %bitcast.48, ...), custom_call_target="tpu_custom_call" | custom-call | tf_op jit(solution)/shard_map/pallas_call | solution.py:119
  254.1 1.0 copy-done.2
  255.1 3.7 %all-to-all-start.3 = ((bf16[16,64,512]{2,1,0:T(8,128)(2,1)}), bf16[16,64,512]{2,1,0:T(8,128)(2,1)S(1)}, u32[]{:S(2)}, u32[]{:S(2)}) async-start(bf16[16,64,512]{2,1,0:T(8,128)(2,1)} %bitcast.50), calls=%async_computation.3 | async-start | bytes 2097152 | tf_op jit(solution)/shard_map/all_to_all | solution.py:219
  258.8 16.8 %all-to-all-done.3 = bf16[16,64,512]{2,1,0:T(8,128)(2,1)S(1)} async-done(((bf16[16,64,512]{2,1,0:T(8,128)(2,1)}), bf16[16,64,512]{2,1,0:T(8,128)(2,1)S(1)}, u32[]{:S(2)}, u32[]{:S(2)}) %all-to-all-start.3) | async-done | bytes 1048608 | tf_op jit(solution)/shard_map/all_to_all | solution.py:219
  275.6 2.6 gather_fusion
  (55 shorter events, 1.6 us)
Async XLA Ops:
  6.5 31.8 %copy-start = (bf16[64,128,1,128]{3,1,2,0:T(8,128)(2,1)S(1)}, bf16[64,128,1,128]{3,1,2,0:T(8,128)(2,1)}, u32[]{:S(2)}) copy-start(bf16[64,128,1,128]{3,1,2,0:T(8,128)(2,1)} %param.18) | copy-start | bytes 6291460
  6.5 3.3 %copy-start.7 = (bf16[64,8,128]{2,1,0:T(8,128)(2,1)S(1)}, bf16[64,8,128]{2,1,0:T(8,128)(2,1)}, u32[]{:S(2)}) copy-start(bf16[64,8,128]{2,1,0:T(8,128)(2,1)} %param.15) | copy-start | bytes 393220
  6.5 3.3 %copy-start.8 = (bf16[64,8,128]{2,1,0:T(8,128)(2,1)S(1)}, bf16[64,8,128]{2,1,0:T(8,128)(2,1)}, u32[]{:S(2)}) copy-start(bf16[64,8,128]{2,1,0:T(8,128)(2,1)} %param.14) | copy-start | bytes 393220
  6.5 3.4 %copy-start.6 = (bf16[64,8,512]{2,1,0:T(8,128)(2,1)S(1)}, bf16[64,8,512]{2,1,0:T(8,128)(2,1)}, u32[]{:S(2)}) copy-start(bf16[64,8,512]{2,1,0:T(8,128)(2,1)} %param.13) | copy-start | bytes 1572868
  6.5 56.5 %all-gather.4.cloned.1.call-start = ((), (), s32[]{:S(2)}) async-start(), calls=%async_computation.4 | async-start | bytes 9732096 | tf_op jit(solution)/shard_map/all_gather | solution.py:162
  9.8 146.1 %all-gather.6.cloned.1.call-start = ((), (), s32[]{:S(2)}) async-start(), calls=%async_computation.5 | async-start | bytes 13369344 | tf_op jit(solution)/shard_map/all_gather | solution.py:159
  10.1 18.6 %copy-start.9 = (s32[512,1]{0,1:T(1,128)S(1)}, s32[512,1]{0,1:T(1,128)}, u32[]{:S(2)}) copy-start(s32[512,1]{0,1:T(1,128)} %param.16) | copy-start | bytes 6148
  10.1 28.2 %copy-start.10 = (s32[1,32]{1,0:T(1,128)S(1)}, s32[1,32]{1,0:T(1,128)}, u32[]{:S(2)}) copy-start(s32[1,32]{1,0:T(1,128)} %param.19) | copy-start | bytes 388
  30.9 143.0 %all-to-all-start.2 = ((s32[16,1,1]{2,1,0:T(1,128)}), s32[16,1,1]{2,1,0:T(1,128)S(1)}, u32[]{:S(2)}, u32[]{:S(2)}) async-start(s32[16,1,1]{2,1,0:T(1,128)} %copy.34), calls=%async_computation.2 | async-start | bytes 16384 | tf_op jit(solution)/shard_map/all_to_all | solution.py:181
  173.9 29.6 %all-to-all-start.1 = ((bf16[16,64,768]{2,1,0:T(8,128)(2,1)}), bf16[16,64,768]{2,1,0:T(8,128)(2,1)}, u32[]{:S(2)}, u32[]{:S(2)}) async-start(bf16[16,64,768]{2,1,0:T(8,128)(2,1)} %bitcast.52), calls=%async_computation.1 | async-start | bytes 3145728 | tf_op jit(solution)/shard_map/all_to_all | solution.py:185
  203.5 3.8 %copy-start.1 = (bf16[32,128,128]{2,1,0:T(8,128)(2,1)S(1)}, bf16[32,128,128]{2,1,0:T(8,128)(2,1)}, u32[]{:S(2)}) copy-start(bf16[32,128,128]{2,1,0:T(8,128)(2,1)} %get-tuple-element.18) | copy-start | bytes 3145732
  203.5 3.8 %copy-start.3 = (f32[1024,128]{1,0:T(8,128)S(1)}, f32[1024,128]{1,0:T(8,128)}, u32[]{:S(2)}) copy-start(f32[1024,128]{1,0:T(8,128)} %get-tuple-element.19.cos_ref) | copy-start | bytes 1572868
  203.5 3.8 %copy-start.4 = (f32[1024,128]{1,0:T(8,128)S(1)}, f32[1024,128]{1,0:T(8,128)}, u32[]{:S(2)}) copy-start(f32[1024,128]{1,0:T(8,128)} %get-tuple-element.20.sin_ref) | copy-start | bytes 1572868
  207.3 1.0 copy-start.5
  254.1 1.0 copy-start.2
  255.1 20.5 %all-to-all-start.3 = ((bf16[16,64,512]{2,1,0:T(8,128)(2,1)}), bf16[16,64,512]{2,1,0:T(8,128)(2,1)S(1)}, u32[]{:S(2)}, u32[]{:S(2)}) async-start(bf16[16,64,512]{2,1,0:T(8,128)(2,1)} %bitcast.50), calls=%async_computation.3 | async-start | bytes 2097152 | tf_op jit(solution)/shard_map/all_to_all | solution.py:219
Sparse Core Ops, SparseCore 0:
  9.9 53.0 all-gather.3
  65.2 90.6 all-gather.5

commit v8 on v7

--- a/solution.py
+++ b/solution.py
@@ -159,8 +159,12 @@
     gathered = lax.all_gather(weights_head, "tok", axis=1, tiled=True)
     gathered = gathered.reshape(-1, gathered.shape[-1])
     gain_rows = jnp.broadcast_to(gain[None, :], (16, gain.shape[0]))
-    stacked = lax.all_gather(
-        jnp.concatenate([tokens, gain_rows], axis=0), "head", axis=1, tiled=True
+    stacked = lax.all_to_all(
+        jnp.tile(jnp.concatenate([tokens, gain_rows], axis=0), (1, n_head)),
+        "head",
+        1,
+        1,
+        tiled=True,
     )
     tokens_full = stacked[:row_count]
     gain_full = stacked[row_count]

time: 286 us -> 279 us (0.976)
  waiting for transfers between devices: 139 us -> 120 us
  starting transfers between devices: 16.3 us -> 24.4 us
  local copies, waits for them, and re-layouts: 18.9 us -> 25.5 us
    all_gather x1, waiting for transfers between devices: 86.8 us -> 0.02 us  [body(): gathered = lax.all_gather(weights_head, 'tok', axis=1, tiled=True)]
    all_to_all x0 -> x1, waiting for transfers between devices: none -> 85.9 us  [body(): lax.all_to_all(jnp.tile(jnp.concatenate([tokens, gain_rows], axis=0), (1,...]
    all_gather x1 -> x0, waiting for transfers between devices: 16.8 us -> none  [body(): lax.all_gather(jnp.concatenate([tokens, gain_rows], axis=0), 'head', axis...]
    all_to_all x0 -> x1, starting transfers between devices: none -> 6.47 us  [body(): lax.all_to_all(jnp.tile(jnp.concatenate([tokens, gain_rows], axis=0), (1,...]
    another operation x3 -> x4, local copies, waits for them, and re-layouts: 0.2 us -> 4.63 us  [the longest x1 4.43 us: body(): jnp.tile(jnp.concatenate([tokens, gain_rows], axis=0), (1, n_head))]
    unnamed x25 -> x24, local copies, waits for them, and re-layouts: 2.25 us -> 5.35 us
  transfers between devices with their start and end apart: 5 -> 5, of which waited for: 4 -> 3; matrix products, arithmetic and copies ran while one was open for 14% -> 16% of each run, Pallas kernels for 0% -> 0%
where the time goes in v8:
time: 279 us; the launch traced here: 277 us
  waiting for transfers between devices  120 us (43%)
  Pallas kernels  45.7 us (16%)
  local copies, waits for them, and re-layouts  25.5 us (9%)
  starting transfers between devices  24.4 us (9%)
  other arithmetic  17.1 us (6%)
  blocking collectives  17.1 us (6%)
  matrix products  13.7 us (5%)
  between operations  13.6 us (5%)
    all_to_all x1, waiting for transfers between devices, body(): lax.all_to_all(jnp.tile(jnp.concatenate([tokens, gain_rows], axis=0), (1,...  85.9 us
    pallas_call x1, Pallas kernels, attend_rotating(): pl.pallas_call(attention_kernel, grid=(slots // block_slots,), in_specs=[...  45.7 us
    all_to_all x1, blocking collectives, body(): weights_head = lax.all_to_all(weights_local, 'head', 1, 0, tiled=True)  17.1 us
    all_to_all x1, waiting for transfers between devices, body(): lax.all_to_all(attended.reshape(n_tok, capacity, query_width), 'tok', spl...  17 us
    all_to_all x1, waiting for transfers between devices, body(): lax.all_to_all(outgoing.reshape(n_tok, capacity, width_all), 'tok', 0, 0,...  17 us
    dot_general x1, matrix products, body(): projected = jnp.dot(normed, gathered, preferred_element_type=jnp.float32)  13.7 us
    all_to_all x1, starting transfers between devices, body(): lax.all_to_all(outgoing.reshape(n_tok, capacity, width_all), 'tok', 0, 0,...  7.27 us
    all_to_all x1, starting transfers between devices, body(): lax.all_to_all(counts_local, 'tok', 0, 0, tiled=True).reshape(n_tok)  7.04 us
  transfers between devices with their start and end apart: 5, of which 3 were waited for; matrix products, arithmetic and copies ran while one was open for 16% of the time, Pallas kernels for 0%

profile of v8, /device:TPU:32, one launch (start us, length us, event | category | flops | bytes accessed | tf_op | source)
XLA Modules:
  0.0 277.1 jit_solution(1847601762712897037)
XLA Ops:
  6.5 1.3 copy.34
  7.9 0.9 copy.35
  8.8 1.0 copy.36
  9.9 17.1 %all_to_all.40 = bf16[64,8,768]{2,0,1:T(8,128)(2,1)} all-to-all(bf16[64,8,768]{2,0,1:T(8,128)(2,1)S(1)} %pad_maximum_fusion.1), channel_id=1, replica_groups=mesh['tok'=16,'head'=8] {'head'}, dimensions={1} | all-to-all | bytes 1572864 | tf_op jit(solution)/shard_map/all_to_all | solution.py:157
  27.1 4.4 %tile.2 = bf16[528,8,1024]{2,0,1:T(8,128)(2,1)} broadcast(bf16[528,1024]{1,0:T(8,128)(2,1)S(1)} %pad_maximum_fusion), dimensions={0,2} | broadcast | bytes 9732096 | tf_op jit(solution)/shard_map/tile | solution.py:163
  31.6 6.5 %all-to-all-start = ((bf16[528,8,1024]{2,0,1:T(8,128)(2,1)}), bf16[528,8,1024]{2,0,1:T(8,128)(2,1)}, u32[]{:S(2)}, u32[]{:S(2)}) async-start(bf16[528,8,1024]{2,0,1:T(8,128)(2,1)} %tile.2), calls=%async_computation | async-start | bytes 17301504 | tf_op jit(solution)/shard_map/all_to_all | solution.py:162
  38.1 1.2 reduce-window.15
  39.6 0.7 copy.37
  40.4 1.7 gather_fusion.1
  42.1 3.2 %gather_fusion.2 = bf16[32,128,128]{2,1,0:T(8,128)(2,1)} fusion(bf16[64,128,128]{2,1,0:T(8,128)(2,1)} %bitcast.61, s32[1024]{0:T(1024)S(1)} %pad_clamp_fusion.1), kind=kCustom, calls=%fused_computation.1.clone | custom fusion | bytes 2097280 | tf_op jit(solution)/shard_map/jit(_take)/gather | solution.py:209
  45.4 2.8 %broadcast_select_fusion = (bf16[32,128,128]{2,1,0:T(8,128)(2,1)S(1)}, bf16[32,128,128]{2,1,0:T(8,128)(2,1)}) fusion(bf16[32,128,128]{2,1,0:T(8,128)(2,1)} %gather_fusion.2, pred[32]{0:T(512)(128)(4,1)S(1)} %get-tuple-element.8, bf16[32,128,128]{2,1,0:T(8,128)(2,1)} %gather_fusion.1), kind=kLoop, calls=%fused_computation.16 | loop fusion | flops 1048576 | bytes 4194336 | tf_op jit(solution)/shard_map/jit(_take)/select_n | solution.py:209
  48.2 85.9 %all-to-all-done = bf16[528,8,1024]{2,0,1:T(8,128)(2,1)} async-done(((bf16[528,8,1024]{2,0,1:T(8,128)(2,1)}), bf16[528,8,1024]{2,0,1:T(8,128)(2,1)}, u32[]{:S(2)}, u32[]{:S(2)}) %all-to-all-start) | async-done | bytes 8650784 | tf_op jit(solution)/shard_map/all_to_all | solution.py:162
  134.1 7.0 %all-to-all-start.3 = ((s32[16,1,1]{2,1,0:T(1,128)}), s32[16,1,1]{2,1,0:T(1,128)S(1)}, u32[]{:S(2)}, u32[]{:S(2)}) async-start(s32[16,1,1]{2,1,0:T(1,128)} %copy.37), calls=%async_computation.3 | async-start | bytes 16384 | tf_op jit(solution)/shard_map/all_to_all | solution.py:185
  141.2 0.9 slice_convert_fusion
  142.1 5.1 %fusion = f32[512]{0:T(512)S(1)} fusion(bf16[528,8,1024]{2,0,1:T(8,128)(2,1)} %all-to-all-done), kind=kLoop, calls=%fused_computation.6 | loop fusion | flops 12582400 | bytes 8390656 | tf_op jit(solution)/shard_map/reduce_sum | solution.py:172
  147.3 13.7 %bitcast_convert_fusion = bf16[512,768]{1,0:T(8,128)(2,1)} fusion(bf16[8,1024,1,768]{3,1,0,2:T(8,128)(2,1)} %all-gather.3.cloned.1.call-done, f32[8,1024]{1,0:T(8,128)S(1)} %bitcast.64, f32[512]{0:T(512)S(1)} %add_rsqrt_fusion, bf16[528,8,1024]{2,0,1:T(8,128)(2,1)} %all-to-all-done), kind=kOutput, calls=%fused_computation.14 | convolution fusion | flops 6459621376 | bytes 21792768 | tf_op jit(solution)/shard_map/dot_general | solution.py:177
  161.0 4.4 %scatter_custom_fusion = bf16[1024,768]{1,0:T(8,128)(2,1)} fusion(s32[512]{0:T(512)S(1)} %bitcast.67, bf16[512,768]{1,0:T(8,128)(2,1)} %bitcast_convert_fusion, bf16[]{:T(256)} %constant.20.clone.1), kind=kCustom, calls=%fused_computation.19 | custom fusion | bytes 1573376 | tf_op jit(solution)/shard_map/scatter | solution.py:187
  165.3 7.3 %all-to-all-start.2 = ((bf16[16,64,768]{2,1,0:T(8,128)(2,1)}), bf16[16,64,768]{2,1,0:T(8,128)(2,1)}, u32[]{:S(2)}, u32[]{:S(2)}) async-start(bf16[16,64,768]{2,1,0:T(8,128)(2,1)} %bitcast.59), calls=%async_computation.2 | async-start | bytes 3145728 | tf_op jit(solution)/shard_map/all_to_all | solution.py:189
  172.6 0.4 reduce.2
  173.6 0.3 reduce-window.19
  174.2 1.0 copy.38.qr_ref
  175.2 1.9 fusion.25
  177.1 1.3 pad_maximum_fusion.2
  178.4 17.0 %all-to-all-done.2 = bf16[16,64,768]{2,1,0:T(8,128)(2,1)} async-done(((bf16[16,64,768]{2,1,0:T(8,128)(2,1)}), bf16[16,64,768]{2,1,0:T(8,128)(2,1)}, u32[]{:S(2)}, u32[]{:S(2)}) %all-to-all-start.2) | async-done | bytes 1572896 | tf_op jit(solution)/shard_map/all_to_all | solution.py:189
  195.4 1.1 slice_bitcast_fusion
  196.5 2.5 fusion.24
  199.2 1.0 copy-done.5
  200.3 45.7 %shard_map.91 = bf16[1024,512]{1,0:T(8,128)(2,1)S(1)} custom-call(bf16[1024,768]{1,0:T(8,128)(2,1)} %bitcast.10.q_ref.vn_ref, f32[1024,128]{1,0:T(8,128)S(1)} %copy-done.3, f32[1024,128]{1,0:T(8,128)S(1)} %copy-done.4, s32[1024,1]{1,0:T(8,128)S(1)} %copy-done.5, bf16[4096,128]{1,0:T(8,128)(2,1)S(1)} %bitcast.56, bf16[4096,128]{1,0:T(8,128)(2,1)S(1)} %bitcast.55, ...), custom_call_target="tpu_custom_call" | custom-call | tf_op jit(solution)/shard_map/pallas_call | solution.py:119
  246.0 1.0 copy-done.2
  247.0 3.7 %all-to-all-start.4 = ((bf16[16,64,512]{2,1,0:T(8,128)(2,1)}), bf16[16,64,512]{2,1,0:T(8,128)(2,1)S(1)}, u32[]{:S(2)}, u32[]{:S(2)}) async-start(bf16[16,64,512]{2,1,0:T(8,128)(2,1)} %bitcast.57), calls=%async_computation.4 | async-start | bytes 2097152 | tf_op jit(solution)/shard_map/all_to_all | solution.py:223
  250.7 17.0 %all-to-all-done.4 = bf16[16,64,512]{2,1,0:T(8,128)(2,1)S(1)} async-done(((bf16[16,64,512]{2,1,0:T(8,128)(2,1)}), bf16[16,64,512]{2,1,0:T(8,128)(2,1)S(1)}, u32[]{:S(2)}, u32[]{:S(2)}) %all-to-all-start.4) | async-done | bytes 1048608 | tf_op jit(solution)/shard_map/all_to_all | solution.py:223
  267.7 2.6 gather_fusion
  (54 shorter events, 1.8 us)
Async XLA Ops:
  6.5 33.9 %copy-start = (bf16[64,128,1,128]{3,1,2,0:T(8,128)(2,1)S(1)}, bf16[64,128,1,128]{3,1,2,0:T(8,128)(2,1)}, u32[]{:S(2)}) copy-start(bf16[64,128,1,128]{3,1,2,0:T(8,128)(2,1)} %param.17) | copy-start | bytes 6291460
  6.5 140.7 %all-gather.3.cloned.1.call-start = ((), (), s32[]{:S(2)}) async-start(), calls=%async_computation.5 | async-start | bytes 13369344 | tf_op jit(solution)/shard_map/all_gather | solution.py:159
  8.8 18.2 %copy-start.8 = (bf16[1024]{0:T(1024)(128)(2,1)S(1)}, bf16[1024]{0:T(1024)(128)(2,1)}, u32[]{:S(2)}) copy-start(bf16[1024]{0:T(1024)(128)(2,1)} %param.12) | copy-start | bytes 6148
  8.8 18.2 %copy-start.6 = (bf16[512,1024]{1,0:T(8,128)(2,1)S(1)}, bf16[512,1024]{1,0:T(8,128)(2,1)}, u32[]{:S(2)}) copy-start(bf16[512,1024]{1,0:T(8,128)(2,1)} %param.11) | copy-start | bytes 3145732
  31.6 6.5 %copy-start.7 = (s32[512,1]{0,1:T(1,128)S(1)}, s32[512,1]{0,1:T(1,128)}, u32[]{:S(2)}) copy-start(s32[512,1]{0,1:T(1,128)} %param.16) | copy-start | bytes 6148
  31.6 8.8 %copy-start.9 = (s32[1,32]{1,0:T(1,128)S(1)}, s32[1,32]{1,0:T(1,128)}, u32[]{:S(2)}) copy-start(s32[1,32]{1,0:T(1,128)} %param.19) | copy-start | bytes 388
  31.6 102.5 %all-to-all-start = ((bf16[528,8,1024]{2,0,1:T(8,128)(2,1)}), bf16[528,8,1024]{2,0,1:T(8,128)(2,1)}, u32[]{:S(2)}, u32[]{:S(2)}) async-start(bf16[528,8,1024]{2,0,1:T(8,128)(2,1)} %tile.2), calls=%async_computation | async-start | bytes 17301504 | tf_op jit(solution)/shard_map/all_to_all | solution.py:162
  134.1 31.2 %all-to-all-start.3 = ((s32[16,1,1]{2,1,0:T(1,128)}), s32[16,1,1]{2,1,0:T(1,128)S(1)}, u32[]{:S(2)}, u32[]{:S(2)}) async-start(s32[16,1,1]{2,1,0:T(1,128)} %copy.37), calls=%async_computation.3 | async-start | bytes 16384 | tf_op jit(solution)/shard_map/all_to_all | solution.py:185
  165.3 30.1 %all-to-all-start.2 = ((bf16[16,64,768]{2,1,0:T(8,128)(2,1)}), bf16[16,64,768]{2,1,0:T(8,128)(2,1)}, u32[]{:S(2)}, u32[]{:S(2)}) async-start(bf16[16,64,768]{2,1,0:T(8,128)(2,1)} %bitcast.59), calls=%async_computation.2 | async-start | bytes 3145728 | tf_op jit(solution)/shard_map/all_to_all | solution.py:189
  195.4 3.8 %copy-start.1 = (bf16[32,128,128]{2,1,0:T(8,128)(2,1)S(1)}, bf16[32,128,128]{2,1,0:T(8,128)(2,1)}, u32[]{:S(2)}) copy-start(bf16[32,128,128]{2,1,0:T(8,128)(2,1)} %get-tuple-element.18) | copy-start | bytes 3145732
  195.4 3.8 %copy-start.3 = (f32[1024,128]{1,0:T(8,128)S(1)}, f32[1024,128]{1,0:T(8,128)}, u32[]{:S(2)}) copy-start(f32[1024,128]{1,0:T(8,128)} %get-tuple-element.19.cos_ref) | copy-start | bytes 1572868
  195.4 3.8 %copy-start.4 = (f32[1024,128]{1,0:T(8,128)S(1)}, f32[1024,128]{1,0:T(8,128)}, u32[]{:S(2)}) copy-start(f32[1024,128]{1,0:T(8,128)} %get-tuple-element.20.sin_ref) | copy-start | bytes 1572868
  199.2 1.0 copy-start.5
  246.0 1.0 copy-start.2
  247.0 20.7 %all-to-all-start.4 = ((bf16[16,64,512]{2,1,0:T(8,128)(2,1)}), bf16[16,64,512]{2,1,0:T(8,128)(2,1)S(1)}, u32[]{:S(2)}, u32[]{:S(2)}) async-start(bf16[16,64,512]{2,1,0:T(8,128)(2,1)} %bitcast.57), calls=%async_computation.4 | async-start | bytes 2097152 | tf_op jit(solution)/shard_map/all_to_all | solution.py:223
Sparse Core Ops, SparseCore 0:
  27.2 90.1 all-gather.2

commit v9 on v7

--- a/solution.py
+++ b/solution.py
@@ -147,20 +147,28 @@
 def body(tokens, gain, w_query, w_key, w_value, group_ids, key_pages, value_pages, page_table):
     row_count = tokens.shape[0]
     n_tok = lax.axis_size("tok")
-    n_head = lax.axis_size("head")
+    n_head = lax.axis_size(("hz", "hc"))
     head_size = key_pages.shape[-1]
     query_width = w_query.shape[2]
     group_heads = query_width // head_size
     full_width = tokens.shape[1] * n_head
     capacity = 2 * row_count // n_tok
     weights_local = jnp.concatenate([w_query, w_key, w_value], axis=2)
-    weights_head = lax.all_to_all(weights_local, "head", 1, 0, tiled=True)
+    weights_head = lax.all_to_all(weights_local, ("hz", "hc"), 1, 0, tiled=True)
     weights_head = weights_head.reshape(n_head, -1, weights_head.shape[-1])
     gathered = lax.all_gather(weights_head, "tok", axis=1, tiled=True)
     gathered = gathered.reshape(-1, gathered.shape[-1])
     gain_rows = jnp.broadcast_to(gain[None, :], (16, gain.shape[0]))
-    stacked = lax.all_gather(
-        jnp.concatenate([tokens, gain_rows], axis=0), "head", axis=1, tiled=True
+    local_block = jnp.concatenate([tokens, gain_rows], axis=0)
+    ring_size = lax.axis_size("hz")
+    across_ring = lax.all_to_all(
+        jnp.tile(local_block, (1, ring_size)), "hz", 1, 1, tiled=True
+    )
+    across_chip = lax.all_to_all(jnp.tile(across_ring, (1, 2)), "hc", 1, 1, tiled=True)
+    stacked = (
+        across_chip.reshape(local_block.shape[0], 2, ring_size, local_block.shape[1])
+        .transpose(0, 2, 1, 3)
+        .reshape(local_block.shape[0], -1)
     )
     tokens_full = stacked[:row_count]
     gain_full = stacked[row_count]
@@ -227,17 +235,20 @@
 
 
 def solution(mesh):
+    n_tok, n_head = mesh.devices.shape
+    split = jax.sharding.Mesh(mesh.devices.reshape(n_tok, n_head // 2, 2), ("tok", "hz", "hc"))
+    head = ("hz", "hc")
     placed = (
-        P("tok", "head"),
-        P("head"),
-        P(("head", "tok"), None, None),
-        P(("head", "tok"), None, None),
-        P(("head", "tok"), None, None),
+        P("tok", head),
+        P(head),
+        P(head + ("tok",), None, None),
+        P(head + ("tok",), None, None),
+        P(head + ("tok",), None, None),
         P("tok", None),
-        P("tok", None, "head", None),
-        P("tok", None, "head", None),
+        P("tok", None, head, None),
+        P("tok", None, head, None),
         P("tok", None),
     )
     return jax.shard_map(
-        body, mesh=mesh, in_specs=placed, out_specs=P("tok", "head"), check_vma=False
-    )
+        body, mesh=split, in_specs=placed, out_specs=P("tok", head), check_vma=False
+    )

time: 286 us -> 308 us (1.077)
  waiting for transfers between devices: 139 us -> 75.1 us
  local copies, waits for them, and re-layouts: 18.9 us -> 68.6 us
  blocking collectives: 18.4 us -> 36 us
  other arithmetic: 19.4 us -> 28.1 us
  starting transfers between devices: 16.3 us -> 24.4 us
    all_gather x1, waiting for transfers between devices: 86.8 us -> 0.01 us  [body(): gathered = lax.all_gather(weights_head, 'tok', axis=1, tiled=True)]
    all_to_all x0 -> x1, waiting for transfers between devices: none -> 39.9 us  [body(): lax.all_to_all(jnp.tile(local_block, (1, ring_size)), 'hz', 1, 1, tiled=T...]
    reshape x0 -> x1, local copies, waits for them, and re-layouts: none -> 18.6 us  [body(): across_chip.reshape(local_block.shape[0], 2, ring_size, local_block.shape...]
    all_to_all x1 -> x2, blocking collectives: 18.4 us -> 36 us  [the longest x1 19 us: body(): lax.all_to_all(jnp.tile(across_ring, (1, 2)), 'hc', 1, 1, tiled=True)]
    all_gather x1 -> x0, waiting for transfers between devices: 16.8 us -> none  [body(): lax.all_gather(jnp.concatenate([tokens, gain_rows], axis=0), 'head', axis...]
    another operation x3 -> x6, local copies, waits for them, and re-layouts: 0.2 us -> 14.5 us  [the longest x2 11.7 us: body(): jnp.tile(across_ring, (1, 2))]
    convert_element_type x0 -> x1, local copies, waits for them, and re-layouts: none -> 13.8 us  [body(): (values_wide * factor[:, None] * gain_full.astype(jnp.float32)[None, :])....]
    convert_element_type x0 -> x2, other arithmetic: none -> 9.12 us  [the longest x1 8.39 us: body(): (values_wide * factor[:, None] * gain_full.astype(jnp.float32)[None, :])....]
  transfers between devices with their start and end apart: 5 -> 5, of which waited for: 4 -> 3; matrix products, arithmetic and copies ran while one was open for 14% -> 31% of each run, Pallas kernels for 0% -> 0%
where the time goes in v9:
time: 308 us; the launch traced here: 304 us
  waiting for transfers between devices  75.1 us (24%)
  local copies, waits for them, and re-layouts  68.6 us (22%)
  Pallas kernels  45.9 us (15%)
  blocking collectives  36 us (12%)
  other arithmetic  28.1 us (9%)
  starting transfers between devices  24.4 us (8%)
  between operations  13.6 us (4%)
  matrix products  12.8 us (4%)
    pallas_call x1, Pallas kernels, attend_rotating(): pl.pallas_call(attention_kernel, grid=(slots // block_slots,), in_specs=[...  45.9 us
    all_to_all x1, waiting for transfers between devices, body(): lax.all_to_all(jnp.tile(local_block, (1, ring_size)), 'hz', 1, 1, tiled=T...  39.9 us
    all_to_all x1, blocking collectives, body(): lax.all_to_all(jnp.tile(across_ring, (1, 2)), 'hc', 1, 1, tiled=True)  19 us
    reshape x1, local copies, waits for them, and re-layouts, body(): across_chip.reshape(local_block.shape[0], 2, ring_size, local_block.shape...  18.6 us
    all_to_all x1, waiting for transfers between devices, body(): lax.all_to_all(outgoing.reshape(n_tok, capacity, width_all), 'tok', 0, 0,...  18.3 us
    all_to_all x1, blocking collectives, body(): weights_head = lax.all_to_all(weights_local, ('hz', 'hc'), 1, 0, tiled=True)  17.1 us
    all_to_all x1, waiting for transfers between devices, body(): lax.all_to_all(attended.reshape(n_tok, capacity, query_width), 'tok', spl...  16.9 us
    convert_element_type x1, local copies, waits for them, and re-layouts, body(): (values_wide * factor[:, None] * gain_full.astype(jnp.float32)[None, :])....  13.8 us
  transfers between devices with their start and end apart: 5, of which 3 were waited for; matrix products, arithmetic and copies ran while one was open for 31% of the time, Pallas kernels for 0%

profile of v9, /device:TPU:32, one launch (start us, length us, event | category | flops | bytes accessed | tf_op | source)
XLA Modules:
  0.0 304.4 jit_solution(13378710365103515081)
XLA Ops:
  6.5 1.1 copy.53
  8.6 1.2 copy.51
  9.8 17.1 %all_to_all.46 = bf16[64,8,768]{2,0,1:T(8,128)(2,1)} all-to-all(bf16[64,8,768]{2,0,1:T(8,128)(2,1)S(1)} %pad_maximum_fusion.1), channel_id=1, replica_groups=mesh['tok'=16,'hz'=4,'hc'=2] {'hz','hc'}, dimensions={1} | all-to-all | bytes 1572864 | tf_op jit(solution)/shard_map/all_to_all | solution.py:157
  27.0 2.6 tile.6
  29.7 6.4 %all-to-all-start = ((bf16[528,4,1024]{2,0,1:T(8,128)(2,1)}), bf16[528,4,1024]{2,0,1:T(8,128)(2,1)}, u32[]{:S(2)}, u32[]{:S(2)}) async-start(bf16[528,4,1024]{2,0,1:T(8,128)(2,1)} %tile.6), calls=%async_computation | async-start | bytes 8650752 | tf_op jit(solution)/shard_map/all_to_all | solution.py:164
  36.1 1.2 reduce-window.15
  38.5 1.7 gather_fusion.2
  40.2 2.3 gather_fusion.1
  42.6 2.5 broadcast_select_fusion
  45.0 39.9 %all-to-all-done = bf16[528,4,1024]{2,0,1:T(8,128)(2,1)} async-done(((bf16[528,4,1024]{2,0,1:T(8,128)(2,1)}), bf16[528,4,1024]{2,0,1:T(8,128)(2,1)}, u32[]{:S(2)}, u32[]{:S(2)}) %all-to-all-start) | async-done | bytes 4325408 | tf_op jit(solution)/shard_map/all_to_all | solution.py:164
  84.9 5.1 %copy.58 = bf16[4,66,8,1024]{3,2,0,1:T(8,128)(2,1)} copy(bf16[4,66,8,1024]{3,2,1,0:T(8,128)(2,1)} %bitcast.31) | data formatting | bytes 8650752 | tf_op jit(solution)/shard_map/tile | solution.py:167
  90.0 6.6 %tile.8 = bf16[528,2,4096]{2,0,1:T(8,128)(2,1)} broadcast(bf16[528,4096]{1,0:T(8,128)(2,1)} %bitcast.66), dimensions={0,2} | broadcast | bytes 12976128 | tf_op jit(solution)/shard_map/tile | solution.py:167
  96.6 19.0 %all_to_all.47 = bf16[528,2,4096]{2,0,1:T(8,128)(2,1)} all-to-all(bf16[528,2,4096]{2,0,1:T(8,128)(2,1)} %tile.8), channel_id=1, replica_groups=mesh['tok'=16,'hz'=4,'hc'=2] {'hc'}, dimensions={1} | all-to-all | bytes 17301504 | tf_op jit(solution)/shard_map/all_to_all | solution.py:167
  115.6 7.0 %all-to-all-start.4 = ((s32[16,1,1]{2,1,0:T(1,128)}), s32[16,1,1]{2,1,0:T(1,128)S(1)}, u32[]{:S(2)}, u32[]{:S(2)}) async-start(s32[16,1,1]{2,1,0:T(1,128)} %copy.54), calls=%async_computation.4 | async-start | bytes 16384 | tf_op jit(solution)/shard_map/all_to_all | solution.py:189
  122.6 18.6 %reshape.337 = bf16[528,2,4,1024]{3,2,0,1:T(4,128)(2,1)} reshape(bf16[528,2,4096]{2,0,1:T(8,128)(2,1)} %all_to_all.47) | data formatting | bytes 17301504 | tf_op jit(solution)/shard_map/reshape | solution.py:169
  141.2 8.3 %fusion = f32[512]{0:T(512)S(1)} fusion(bf16[528,4,2,1024]{3,1,0,2:T(4,128)(2,1)} %bitcast.62), kind=kLoop, calls=%fused_computation.6 | loop fusion | flops 12582400 | bytes 8390656 | tf_op jit(solution)/shard_map/reduce_sum | solution.py:176
  150.2 8.4 %fusion.2 = bf16[512,4,2,1024]{3,1,0,2:T(4,128)(2,1)} fusion(f32[4,2,1024]{2,0,1:T(4,128)S(1)} %fusion.19, f32[512]{0:T(512)S(1)} %add_rsqrt_fusion, bf16[528,4,2,1024]{3,1,0,2:T(4,128)(2,1)} %bitcast.64), kind=kLoop, calls=%fused_computation.8 | loop fusion | flops 16777216 | bytes 16812032 | tf_op jit(solution)/shard_map/convert_element_type | solution.py:178
  158.6 13.8 %copy.50 = bf16[512,4,2,1024]{0,3,2,1:T(8,128)(2,1)} copy(bf16[512,4,2,1024]{3,1,0,2:T(4,128)(2,1)} %fusion.2) | data formatting | bytes 16777216 | tf_op jit(solution)/shard_map/convert_element_type | solution.py:178
  172.4 12.8 %convolution_convert_fusion = bf16[512,768]{1,0:T(8,128)(2,1)S(1)} fusion(bf16[512,8192]{0,1:T(8,128)(2,1)} %bitcast.70, bf16[8192,768]{1,0:T(8,128)(2,1)} %bitcast.82), kind=kOutput, calls=%fused_computation.9 | convolution fusion | flops 6442844160 | bytes 21757952 | tf_op jit(solution)/shard_map/dot_general | solution.py:181
  185.1 4.0 %scatter_custom_fusion = bf16[1024,768]{1,0:T(8,128)(2,1)} fusion(s32[512]{0:T(512)S(1)} %bitcast.78, bf16[512,768]{1,0:T(8,128)(2,1)S(1)} %convolution_convert_fusion, bf16[]{:T(256)} %constant.20.clone.1), kind=kCustom, calls=%fused_computation.14 | custom fusion | bytes 1572866 | tf_op jit(solution)/shard_map/scatter | solution.py:191
  189.2 7.2 %all-to-all-start.3 = ((bf16[16,64,768]{2,1,0:T(8,128)(2,1)}), bf16[16,64,768]{2,1,0:T(8,128)(2,1)S(1)}, u32[]{:S(2)}, u32[]{:S(2)}) async-start(bf16[16,64,768]{2,1,0:T(8,128)(2,1)} %bitcast.71), calls=%async_computation.3 | async-start | bytes 3145728 | tf_op jit(solution)/shard_map/all_to_all | solution.py:193
  197.9 1.1 copy.55.qr_ref
  199.0 1.9 fusion.15
  200.9 1.3 pad_maximum_fusion.2
  202.2 18.3 %all-to-all-done.3 = bf16[16,64,768]{2,1,0:T(8,128)(2,1)S(1)} async-done(((bf16[16,64,768]{2,1,0:T(8,128)(2,1)}), bf16[16,64,768]{2,1,0:T(8,128)(2,1)S(1)}, u32[]{:S(2)}, u32[]{:S(2)}) %all-to-all-start.3) | async-done | bytes 1572896 | tf_op jit(solution)/shard_map/all_to_all | solution.py:193
  220.5 2.5 fusion.14
  223.2 1.2 copy-done.2
  224.4 1.0 copy-done.4
  227.5 45.9 %shard_map.91 = bf16[1024,512]{1,0:T(8,128)(2,1)S(1)} custom-call(bf16[1024,768]{1,0:T(8,128)(2,1)} %bitcast.68, f32[1024,128]{1,0:T(8,128)S(1)} %copy-done.4, f32[1024,128]{1,0:T(8,128)S(1)} %copy-done.5, s32[1024,1]{1,0:T(8,128)S(1)} %copy-done.6, bf16[4096,128]{1,0:T(8,128)(2,1)S(1)} %bitcast.60, bf16[4096,128]{1,0:T(8,128)(2,1)S(1)} %bitcast.59, ...), custom_call_target="tpu_custom_call" | custom-call | tf_op jit(solution)/shard_map/pallas_call | solution.py:119
  274.4 3.7 %all-to-all-start.5 = ((bf16[16,64,512]{2,1,0:T(8,128)(2,1)}), bf16[16,64,512]{2,1,0:T(8,128)(2,1)S(1)}, u32[]{:S(2)}, u32[]{:S(2)}) async-start(bf16[16,64,512]{2,1,0:T(8,128)(2,1)} %bitcast.61), calls=%async_computation.5 | async-start | bytes 2097152 | tf_op jit(solution)/shard_map/all_to_all | solution.py:227
  278.1 16.9 %all-to-all-done.5 = bf16[16,64,512]{2,1,0:T(8,128)(2,1)S(1)} async-done(((bf16[16,64,512]{2,1,0:T(8,128)(2,1)}), bf16[16,64,512]{2,1,0:T(8,128)(2,1)S(1)}, u32[]{:S(2)}, u32[]{:S(2)}) %all-to-all-start.5) | async-done | bytes 1048608 | tf_op jit(solution)/shard_map/all_to_all | solution.py:227
  294.9 2.6 gather_fusion
  (63 shorter events, 7.8 us)
Async XLA Ops:
  6.5 32.0 %copy-start = (bf16[64,128,1,128]{3,1,2,0:T(8,128)(2,1)S(1)}, bf16[64,128,1,128]{3,1,2,0:T(8,128)(2,1)}, u32[]{:S(2)}) copy-start(bf16[64,128,1,128]{3,1,2,0:T(8,128)(2,1)} %param.18) | copy-start | bytes 6291460
  6.5 20.4 %copy-start.10 = (bf16[1024]{0:T(1024)(128)(2,1)S(1)}, bf16[1024]{0:T(1024)(128)(2,1)}, u32[]{:S(2)}) copy-start(bf16[1024]{0:T(1024)(128)(2,1)} %param.12) | copy-start | bytes 6148
  6.5 20.4 %copy-start.8 = (bf16[512,1024]{1,0:T(8,128)(2,1)S(1)}, bf16[512,1024]{1,0:T(8,128)(2,1)}, u32[]{:S(2)}) copy-start(bf16[512,1024]{1,0:T(8,128)(2,1)} %param.11) | copy-start | bytes 3145732
  6.5 165.8 %all-gather.3.cloned.1.call-start = ((), (), s32[]{:S(2)}) async-start(), calls=%async_computation.6 | async-start | bytes 13369344 | tf_op jit(solution)/shard_map/all_gather | solution.py:159
  29.7 6.5 %copy-start.9 = (s32[512,1]{0,1:T(1,128)S(1)}, s32[512,1]{0,1:T(1,128)}, u32[]{:S(2)}) copy-start(s32[512,1]{0,1:T(1,128)} %param.16) | copy-start | bytes 6148
  29.7 8.8 %copy-start.11 = (s32[1,32]{1,0:T(1,128)S(1)}, s32[1,32]{1,0:T(1,128)}, u32[]{:S(2)}) copy-start(s32[1,32]{1,0:T(1,128)} %param.19) | copy-start | bytes 388
  29.7 55.2 %all-to-all-start = ((bf16[528,4,1024]{2,0,1:T(8,128)(2,1)}), bf16[528,4,1024]{2,0,1:T(8,128)(2,1)}, u32[]{:S(2)}, u32[]{:S(2)}) async-start(bf16[528,4,1024]{2,0,1:T(8,128)(2,1)} %tile.6), calls=%async_computation | async-start | bytes 8650752 | tf_op jit(solution)/shard_map/all_to_all | solution.py:164
  115.6 73.6 %all-to-all-start.4 = ((s32[16,1,1]{2,1,0:T(1,128)}), s32[16,1,1]{2,1,0:T(1,128)S(1)}, u32[]{:S(2)}, u32[]{:S(2)}) async-start(s32[16,1,1]{2,1,0:T(1,128)} %copy.54), calls=%async_computation.4 | async-start | bytes 16384 | tf_op jit(solution)/shard_map/all_to_all | solution.py:189
  189.2 31.3 %all-to-all-start.3 = ((bf16[16,64,768]{2,1,0:T(8,128)(2,1)}), bf16[16,64,768]{2,1,0:T(8,128)(2,1)S(1)}, u32[]{:S(2)}, u32[]{:S(2)}) async-start(bf16[16,64,768]{2,1,0:T(8,128)(2,1)} %bitcast.71), calls=%async_computation.3 | async-start | bytes 3145728 | tf_op jit(solution)/shard_map/all_to_all | solution.py:193
  220.5 2.7 copy-start.7
  223.2 1.2 copy-start.2
  224.4 1.0 copy-start.4
  225.4 1.0 copy-start.5
  226.5 1.0 copy-start.6
  227.5 70.0 %copy-start.1 = (bf16[64,128,1,128]{3,1,2,0:T(8,128)(2,1)S(1)}, bf16[64,128,1,128]{3,1,2,0:T(8,128)(2,1)}, u32[]{:S(2)}) copy-start(bf16[64,128,1,128]{3,1,2,0:T(8,128)(2,1)} %param.18) | copy-start | bytes 6291460
  273.4 1.0 copy-start.3
  274.4 20.5 %all-to-all-start.5 = ((bf16[16,64,512]{2,1,0:T(8,128)(2,1)}), bf16[16,64,512]{2,1,0:T(8,128)(2,1)S(1)}, u32[]{:S(2)}, u32[]{:S(2)}) async-start(bf16[16,64,512]{2,1,0:T(8,128)(2,1)} %bitcast.61), calls=%async_computation.5 | async-start | bytes 2097152 | tf_op jit(solution)/shard_map/all_to_all | solution.py:227
Sparse Core Ops, SparseCore 0:
  27.0 90.0 all-gather.2

commit v10 on v8

--- a/solution.py
+++ b/solution.py
@@ -154,8 +154,18 @@
     full_width = tokens.shape[1] * n_head
     capacity = 2 * row_count // n_tok
     weights_local = jnp.concatenate([w_query, w_key, w_value], axis=2)
-    weights_head = lax.all_to_all(weights_local, "head", 1, 0, tiled=True)
-    weights_head = weights_head.reshape(n_head, -1, weights_head.shape[-1])
+    head_index = lax.axis_index("head")
+    pieces = [jnp.take(weights_local, head_index, axis=1)]
+    for shift in range(1, n_head):
+        outgoing_piece = jnp.take(weights_local, (head_index + shift) % n_head, axis=1)
+        pieces.append(
+            lax.ppermute(
+                outgoing_piece, "head", [(j, (j + shift) % n_head) for j in range(n_head)]
+            )
+        )
+    weights_head = jnp.take(
+        jnp.stack(pieces), (head_index - jnp.arange(n_head)) % n_head, axis=0
+    )
     gathered = lax.all_gather(weights_head, "tok", axis=1, tiled=True)
     gathered = gathered.reshape(-1, gathered.shape[-1])
     gain_rows = jnp.broadcast_to(gain[None, :], (16, gain.shape[0]))

time: 279 us -> 288 us (1.032)
  blocking collectives: 17.1 us -> 0 us
  local copies, waits for them, and re-layouts: 25.5 us -> 39.3 us
  starting transfers between devices: 24.4 us -> 32.7 us
  other arithmetic: 17.1 us -> 20.7 us
    all_to_all x1 -> x0, blocking collectives: 17.1 us -> none  [body(): weights_head = lax.all_to_all(weights_local, 'head', 1, 0, tiled=True)]
    unnamed x24 -> x27, local copies, waits for them, and re-layouts: 5.35 us -> 15.9 us
    ppermute x0 -> x7, starting transfers between devices: none -> 8.65 us  [body(): lax.ppermute(outgoing_piece, 'head', [(j, (j + shift) % n_head) for j in...]
  transfers between devices with their start and end apart: 5 -> 12, of which waited for: 3 -> 3; matrix products, arithmetic and copies ran while one was open for 16% -> 19% of each run, Pallas kernels for 0% -> 0%
where the time goes in v10:
time: 288 us; the launch traced here: 286 us
  waiting for transfers between devices  120 us (42%)
  Pallas kernels  45.7 us (16%)
  local copies, waits for them, and re-layouts  39.3 us (14%)
  starting transfers between devices  32.7 us (11%)
  other arithmetic  20.7 us (7%)
  matrix products  13.6 us (5%)
  between operations  13.6 us (5%)
    all_to_all x1, waiting for transfers between devices, body(): lax.all_to_all(jnp.tile(jnp.concatenate([tokens, gain_rows], axis=0), (1,...  85.9 us
    pallas_call x1, Pallas kernels, attend_rotating(): pl.pallas_call(attention_kernel, grid=(slots // block_slots,), in_specs=[...  45.7 us
    all_to_all x1, waiting for transfers between devices, body(): lax.all_to_all(outgoing.reshape(n_tok, capacity, width_all), 'tok', 0, 0,...  17.1 us
    all_to_all x1, waiting for transfers between devices, body(): lax.all_to_all(attended.reshape(n_tok, capacity, query_width), 'tok', spl...  17.1 us
    unnamed x27, local copies, waits for them, and re-layouts  15.9 us
    dot_general x1, matrix products, body(): projected = jnp.dot(normed, gathered, preferred_element_type=jnp.float32)  13.6 us
    ppermute x7, starting transfers between devices, body(): lax.ppermute(outgoing_piece, 'head', [(j, (j + shift) % n_head) for j in...  8.65 us
    all_to_all x1, starting transfers between devices, body(): lax.all_to_all(outgoing.reshape(n_tok, capacity, width_all), 'tok', 0, 0,...  7.28 us
  transfers between devices with their start and end apart: 12, of which 3 were waited for; matrix products, arithmetic and copies ran while one was open for 19% of the time, Pallas kernels for 0%

profile of v10, /device:TPU:32, one launch (start us, length us, event | category | flops | bytes accessed | tf_op | source)
XLA Modules:
  0.0 285.8 jit_solution(12074424113704499474)
XLA Ops:
  6.5 1.4 copy_dynamic-update-slice_fusion
  10.6 1.9 collective-permute-start.1
  12.5 1.3 collective-permute-start.2
  13.8 2.2 collective-permute-start.3
  17.5 2.4 collective-permute-start.5
  19.9 1.5 bitcast_dynamic-update-slice_fusion.6
  21.5 1.5 bitcast_dynamic-update-slice_fusion.5
  23.0 1.5 bitcast_dynamic-update-slice_fusion.4
  24.5 1.5 bitcast_dynamic-update-slice_fusion.3
  26.1 1.5 bitcast_dynamic-update-slice_fusion.2
  28.9 1.7 gather_fusion
  31.7 1.3 pad_maximum_fusion
  33.0 4.4 %tile.2 = bf16[528,8,1024]{2,0,1:T(8,128)(2,1)} broadcast(bf16[528,1024]{1,0:T(8,128)(2,1)S(1)} %pad_maximum_fusion), dimensions={0,2} | broadcast | bytes 9732096 | tf_op jit(solution)/shard_map/tile | solution.py:173
  37.5 6.0 %all-to-all-start = ((bf16[528,8,1024]{2,0,1:T(8,128)(2,1)}), bf16[528,8,1024]{2,0,1:T(8,128)(2,1)}, u32[]{:S(2)}, u32[]{:S(2)}) async-start(bf16[528,8,1024]{2,0,1:T(8,128)(2,1)} %tile.2), calls=%async_computation | async-start | bytes 17301504 | tf_op jit(solution)/shard_map/all_to_all | solution.py:172
  45.9 1.7 gather_fusion.2
  47.6 3.2 %gather_fusion.3 = bf16[32,128,128]{2,1,0:T(8,128)(2,1)} fusion(bf16[64,128,128]{2,1,0:T(8,128)(2,1)} %bitcast.86, s32[1024]{0:T(1024)S(1)} %pad_clamp_fusion.1), kind=kCustom, calls=%fused_computation.1.clone | custom fusion | bytes 2097280 | tf_op jit(solution)/shard_map/jit(_take)/gather | solution.py:219
  50.8 2.8 broadcast_select_fusion
  53.6 85.9 %all-to-all-done = bf16[528,8,1024]{2,0,1:T(8,128)(2,1)} async-done(((bf16[528,8,1024]{2,0,1:T(8,128)(2,1)}), bf16[528,8,1024]{2,0,1:T(8,128)(2,1)}, u32[]{:S(2)}, u32[]{:S(2)}) %all-to-all-start) | async-done | bytes 8650784 | tf_op jit(solution)/shard_map/all_to_all | solution.py:172
  139.6 7.0 %all-to-all-start.2 = ((s32[16,1,1]{2,1,0:T(1,128)}), s32[16,1,1]{2,1,0:T(1,128)S(1)}, u32[]{:S(2)}, u32[]{:S(2)}) async-start(s32[16,1,1]{2,1,0:T(1,128)} %copy.41), calls=%async_computation.2 | async-start | bytes 16384 | tf_op jit(solution)/shard_map/all_to_all | solution.py:195
  147.6 5.1 %fusion = f32[512]{0:T(512)S(1)} fusion(bf16[528,8,1024]{2,0,1:T(8,128)(2,1)} %all-to-all-done), kind=kLoop, calls=%fused_computation.7 | loop fusion | flops 12582400 | bytes 8390656 | tf_op jit(solution)/shard_map/reduce_sum | solution.py:182
  152.7 13.6 %bitcast_convert_fusion = bf16[512,768]{1,0:T(8,128)(2,1)} fusion(bf16[8,1024,768]{2,1,0:T(8,128)(2,1)} %all-gather.2.cloned.1.call-done, f32[8,1024]{1,0:T(8,128)S(1)} %bitcast.89, f32[512]{0:T(512)S(1)} %add_rsqrt_fusion, bf16[528,8,1024]{2,0,1:T(8,128)(2,1)} %all-to-all-done), kind=kOutput, calls=%fused_computation.14 | convolution fusion | flops 6459621376 | bytes 21792768 | tf_op jit(solution)/shard_map/dot_general | solution.py:187
  166.4 4.4 %scatter_custom_fusion = bf16[1024,768]{1,0:T(8,128)(2,1)} fusion(s32[512]{0:T(512)S(1)} %bitcast.92, bf16[512,768]{1,0:T(8,128)(2,1)} %bitcast_convert_fusion, bf16[]{:T(256)} %constant.114.clone.1), kind=kCustom, calls=%fused_computation.18 | custom fusion | bytes 1573376 | tf_op jit(solution)/shard_map/scatter | solution.py:197
  170.7 7.3 %all-to-all-start.1 = ((bf16[16,64,768]{2,1,0:T(8,128)(2,1)}), bf16[16,64,768]{2,1,0:T(8,128)(2,1)}, u32[]{:S(2)}, u32[]{:S(2)}) async-start(bf16[16,64,768]{2,1,0:T(8,128)(2,1)} %bitcast.85), calls=%async_computation.1 | async-start | bytes 3145728 | tf_op jit(solution)/shard_map/all_to_all | solution.py:199
  180.6 1.9 fusion.22
  182.5 1.3 pad_maximum_fusion.1
  183.8 17.1 %all-to-all-done.1 = bf16[16,64,768]{2,1,0:T(8,128)(2,1)} async-done(((bf16[16,64,768]{2,1,0:T(8,128)(2,1)}), bf16[16,64,768]{2,1,0:T(8,128)(2,1)}, u32[]{:S(2)}, u32[]{:S(2)}) %all-to-all-start.1) | async-done | bytes 1572896 | tf_op jit(solution)/shard_map/all_to_all | solution.py:199
  201.9 2.5 fusion.21
  204.5 1.2 copy-done.1
  208.9 45.7 %shard_map.91 = bf16[1024,512]{1,0:T(8,128)(2,1)S(1)} custom-call(bf16[1024,768]{1,0:T(8,128)(2,1)} %bitcast.24.q_ref.vn_ref, f32[1024,128]{1,0:T(8,128)S(1)} %copy-done.3, f32[1024,128]{1,0:T(8,128)S(1)} %copy-done.4, s32[1024,1]{1,0:T(8,128)S(1)} %copy-done.5, bf16[4096,128]{1,0:T(8,128)(2,1)S(1)} %bitcast.82, bf16[4096,128]{1,0:T(8,128)(2,1)S(1)} %bitcast.81, ...), custom_call_target="tpu_custom_call" | custom-call | tf_op jit(solution)/shard_map/pallas_call | solution.py:119
  255.6 3.7 %all-to-all-start.3 = ((bf16[16,64,512]{2,1,0:T(8,128)(2,1)}), bf16[16,64,512]{2,1,0:T(8,128)(2,1)S(1)}, u32[]{:S(2)}, u32[]{:S(2)}) async-start(bf16[16,64,512]{2,1,0:T(8,128)(2,1)} %bitcast.83), calls=%async_computation.3 | async-start | bytes 2097152 | tf_op jit(solution)/shard_map/all_to_all | solution.py:233
  259.2 17.1 %all-to-all-done.3 = bf16[16,64,512]{2,1,0:T(8,128)(2,1)S(1)} async-done(((bf16[16,64,512]{2,1,0:T(8,128)(2,1)}), bf16[16,64,512]{2,1,0:T(8,128)(2,1)S(1)}, u32[]{:S(2)}, u32[]{:S(2)}) %all-to-all-start.3) | async-done | bytes 1048608 | tf_op jit(solution)/shard_map/all_to_all | solution.py:233
  276.3 2.6 gather_fusion.1
  (78 shorter events, 17.6 us)
Async XLA Ops:
  6.5 39.4 %copy-start = (bf16[64,128,1,128]{3,1,2,0:T(8,128)(2,1)S(1)}, bf16[64,128,1,128]{3,1,2,0:T(8,128)(2,1)}, u32[]{:S(2)}) copy-start(bf16[64,128,1,128]{3,1,2,0:T(8,128)(2,1)} %param.19) | copy-start | bytes 6291460
  6.5 25.2 %copy-start.7 = (bf16[1024]{0:T(1024)(128)(2,1)S(1)}, bf16[1024]{0:T(1024)(128)(2,1)}, u32[]{:S(2)}) copy-start(bf16[1024]{0:T(1024)(128)(2,1)} %param.14) | copy-start | bytes 6148
  6.5 146.2 %all-gather.2.cloned.1.call-start = ((), (), s32[]{:S(2)}) async-start(), calls=%async_computation.4 | async-start | bytes 13369344 | tf_op jit(solution)/shard_map/all_gather | solution.py:169
  10.6 6.9 %collective-permute-start = (bf16[64,768]{1,0:T(8,128)(2,1)}, bf16[64,768]{1,0:T(8,128)(2,1)}, u32[]{:S(2)}, u32[]{:S(2)}) collective-permute-start(bf16[64,768]{1,0:T(8,128)(2,1)} %get-tuple-element.30), channel_id=1, source_target_pairs={{0,1},{1,2},{2,3},{3,4},{4,5},{5,6},{6,7},{7,0},{8,9},{9,10},{10,1... | collective-permute-start | bytes 294920 | tf_op jit(solution)/shard_map/ppermute | solution.py:162
  10.6 10.9 %collective-permute-start.1 = (bf16[64,768]{1,0:T(8,128)(2,1)S(1)}, bf16[64,768]{1,0:T(8,128)(2,1)}, u32[]{:S(2)}, u32[]{:S(2)}) collective-permute-start(bf16[64,768]{1,0:T(8,128)(2,1)S(1)} %get-tuple-element.29), channel_id=1, source_target_pairs={{0,2},{1,3},{2,4},{3,5},{4,6},{5,7},{6,0},{7,1},{8,10},{9,11},{10,... | collective-permute-start | bytes 294920 | tf_op jit(solution)/shard_map/ppermute | solution.py:162
  12.5 10.5 %collective-permute-start.2 = (bf16[64,768]{1,0:T(8,128)(2,1)S(1)}, bf16[64,768]{1,0:T(8,128)(2,1)}, u32[]{:S(2)}, u32[]{:S(2)}) collective-permute-start(bf16[64,768]{1,0:T(8,128)(2,1)S(1)} %get-tuple-element.28), channel_id=1, source_target_pairs={{0,3},{1,4},{2,5},{3,6},{4,7},{5,0},{6,1},{7,2},{8,11},{9,12},{10,... | collective-permute-start | bytes 294920 | tf_op jit(solution)/shard_map/ppermute | solution.py:162
  13.8 10.7 %collective-permute-start.3 = (bf16[64,768]{1,0:T(8,128)(2,1)S(1)}, bf16[64,768]{1,0:T(8,128)(2,1)}, u32[]{:S(2)}, u32[]{:S(2)}) collective-permute-start(bf16[64,768]{1,0:T(8,128)(2,1)S(1)} %get-tuple-element.27), channel_id=1, source_target_pairs={{0,4},{1,5},{2,6},{3,7},{4,0},{5,1},{6,2},{7,3},{8,12},{9,13},{10,... | collective-permute-start | bytes 294920 | tf_op jit(solution)/shard_map/ppermute | solution.py:162
  16.0 10.1 %collective-permute-start.4 = (bf16[64,768]{1,0:T(8,128)(2,1)S(1)}, bf16[64,768]{1,0:T(8,128)(2,1)}, u32[]{:S(2)}, u32[]{:S(2)}) collective-permute-start(bf16[64,768]{1,0:T(8,128)(2,1)S(1)} %get-tuple-element.26), channel_id=1, source_target_pairs={{0,5},{1,6},{2,7},{3,0},{4,1},{5,2},{6,3},{7,4},{8,13},{9,14},{10,... | collective-permute-start | bytes 294920 | tf_op jit(solution)/shard_map/ppermute | solution.py:162
  17.5 10.1 %collective-permute-start.5 = (bf16[64,768]{1,0:T(8,128)(2,1)S(1)}, bf16[64,768]{1,0:T(8,128)(2,1)S(1)}, u32[]{:S(2)}, u32[]{:S(2)}) collective-permute-start(bf16[64,768]{1,0:T(8,128)(2,1)S(1)} %get-tuple-element.25), channel_id=1, source_target_pairs={{0,6},{1,7},{2,0},{3,1},{4,2},{5,3},{6,4},{7,5},{8,14},{9,15},{10,... | collective-permute-start | bytes 294920 | tf_op jit(solution)/shard_map/ppermute | solution.py:162
  21.5 6.8 %collective-permute-start.6 = (bf16[64,768]{1,0:T(8,128)(2,1)S(1)}, bf16[64,768]{1,0:T(8,128)(2,1)S(1)}, u32[]{:S(2)}, u32[]{:S(2)}) collective-permute-start(bf16[64,768]{1,0:T(8,128)(2,1)S(1)} %get-tuple-element.24), channel_id=1, source_target_pairs={{0,7},{1,0},{2,1},{3,2},{4,3},{5,4},{6,5},{7,6},{8,15},{9,8},{10,9... | collective-permute-start | bytes 294920 | tf_op jit(solution)/shard_map/ppermute | solution.py:162
  37.5 6.0 %copy-start.6 = (s32[512,1]{0,1:T(1,128)S(1)}, s32[512,1]{0,1:T(1,128)}, u32[]{:S(2)}) copy-start(s32[512,1]{0,1:T(1,128)} %param.18) | copy-start | bytes 6148
  37.5 8.4 %copy-start.8 = (s32[1,32]{1,0:T(1,128)S(1)}, s32[1,32]{1,0:T(1,128)}, u32[]{:S(2)}) copy-start(s32[1,32]{1,0:T(1,128)} %param.21) | copy-start | bytes 388
  37.5 102.1 %all-to-all-start = ((bf16[528,8,1024]{2,0,1:T(8,128)(2,1)}), bf16[528,8,1024]{2,0,1:T(8,128)(2,1)}, u32[]{:S(2)}, u32[]{:S(2)}) async-start(bf16[528,8,1024]{2,0,1:T(8,128)(2,1)} %tile.2), calls=%async_computation | async-start | bytes 17301504 | tf_op jit(solution)/shard_map/all_to_all | solution.py:172
  139.6 31.2 %all-to-all-start.2 = ((s32[16,1,1]{2,1,0:T(1,128)}), s32[16,1,1]{2,1,0:T(1,128)S(1)}, u32[]{:S(2)}, u32[]{:S(2)}) async-start(s32[16,1,1]{2,1,0:T(1,128)} %copy.41), calls=%async_computation.2 | async-start | bytes 16384 | tf_op jit(solution)/shard_map/all_to_all | solution.py:195
  170.7 30.2 %all-to-all-start.1 = ((bf16[16,64,768]{2,1,0:T(8,128)(2,1)}), bf16[16,64,768]{2,1,0:T(8,128)(2,1)}, u32[]{:S(2)}, u32[]{:S(2)}) async-start(bf16[16,64,768]{2,1,0:T(8,128)(2,1)} %bitcast.85), calls=%async_computation.1 | async-start | bytes 3145728 | tf_op jit(solution)/shard_map/all_to_all | solution.py:199
  204.5 1.2 copy-start.1
  205.7 1.0 copy-start.3
  206.8 1.0 copy-start.4
  207.8 1.0 copy-start.5
  254.6 1.0 copy-start.2
  255.6 20.7 %all-to-all-start.3 = ((bf16[16,64,512]{2,1,0:T(8,128)(2,1)}), bf16[16,64,512]{2,1,0:T(8,128)(2,1)S(1)}, u32[]{:S(2)}, u32[]{:S(2)}) async-start(bf16[16,64,512]{2,1,0:T(8,128)(2,1)} %bitcast.83), calls=%async_computation.3 | async-start | bytes 2097152 | tf_op jit(solution)/shard_map/all_to_all | solution.py:233
Sparse Core Ops, SparseCore 0:
  31.8 90.4 all-gather.1

commit v11 on v8

--- a/solution.py
+++ b/solution.py
@@ -1,3 +1,4 @@
+import functools
 import math
 
 import jax
@@ -61,6 +62,7 @@
 def attention_kernel(q_ref, cos_ref, sin_ref, qr_ref, kp_ref, vp_ref, kn_ref, vn_ref, kr_ref, o_ref):
     size = kp_ref.shape[-1]
     heads = q_ref.shape[-1] // size
+    rows = q_ref.shape[0]
     scaling = 1.0 / math.sqrt(size)
     cosine = cos_ref[...]
     sine = sin_ref[...]
@@ -74,27 +76,35 @@
     before = lax.dot_general(
         q, kp_ref[...], (((1,), (1,)), ((), ())), preferred_element_type=jnp.float32
     ) * scaling
-    inside = lax.dot_general(
-        q, kn_ref[...], (((1,), (1,)), ((), ())), preferred_element_type=jnp.float32
-    ) * scaling
-    inside = jnp.where(kr_ref[...] <= q_rank, inside, -jnp.inf)
-    highest = jnp.maximum(
-        jnp.max(before, axis=1, keepdims=True), jnp.max(inside, axis=1, keepdims=True)
-    )
-    expo_before = jnp.exp(before - highest)
-    expo_inside = jnp.exp(inside - highest)
-    totals = jnp.sum(expo_before, axis=1, keepdims=True) + jnp.sum(
-        expo_inside, axis=1, keepdims=True
-    )
-    mixed = jnp.dot(
-        expo_before.astype(jnp.bfloat16), vp_ref[...], preferred_element_type=jnp.float32
-    ) + jnp.dot(
-        expo_inside.astype(jnp.bfloat16), vn_ref[...], preferred_element_type=jnp.float32
-    )
-    result = (mixed / totals).astype(o_ref.dtype)
-    rows = q_ref.shape[0]
-    for head in range(heads):
-        o_ref[:, head * size : (head + 1) * size] = result[head * rows : (head + 1) * rows]
+    high_before = jnp.max(before, axis=1, keepdims=True)
+    new_len = kn_ref.shape[0]
+    chunk = min(256, new_len)
+    per_chunk = max(chunk // rows, 1)
+    reach = pl.program_id(0) // per_chunk
+
+    def finish(width):
+        inside = lax.dot_general(
+            q, kn_ref[:width, :], (((1,), (1,)), ((), ())), preferred_element_type=jnp.float32
+        ) * scaling
+        inside = jnp.where(kr_ref[:, :width] <= q_rank, inside, -jnp.inf)
+        highest = jnp.maximum(high_before, jnp.max(inside, axis=1, keepdims=True))
+        expo_before = jnp.exp(before - highest)
+        expo_inside = jnp.exp(inside - highest)
+        totals = jnp.sum(expo_before, axis=1, keepdims=True) + jnp.sum(
+            expo_inside, axis=1, keepdims=True
+        )
+        mixed = jnp.dot(
+            expo_before.astype(jnp.bfloat16), vp_ref[...], preferred_element_type=jnp.float32
+        ) + jnp.dot(
+            expo_inside.astype(jnp.bfloat16), vn_ref[:width, :], preferred_element_type=jnp.float32
+        )
+        result = (mixed / totals).astype(o_ref.dtype)
+        for head in range(heads):
+            o_ref[:, head * size : (head + 1) * size] = result[head * rows : (head + 1) * rows]
+
+    for part in range(new_len // chunk):
+        pl.when(reach == part)(functools.partial(finish, (part + 1) * chunk))
+    pl.when(reach >= new_len // chunk)(functools.partial(finish, new_len))
 
 
 def attend_rotating(arrived, width, positions, query_rank, prefix_keys, prefix_values, new_keys,

time: 279 us -> 276 us (0.989)
  Pallas kernels: 45.7 us -> 42.6 us
    pallas_call x1, Pallas kernels: 45.7 us -> 42.6 us  [attend_rotating(): pl.pallas_call(attention_kernel, grid=(slots // block_slots,), in_specs=[...]
where the time goes in v11:
time: 276 us; the launch traced here: 274 us
  waiting for transfers between devices  120 us (43%)
  Pallas kernels  42.6 us (15%)
  local copies, waits for them, and re-layouts  25.5 us (9%)
  starting transfers between devices  24.4 us (9%)
  other arithmetic  17.1 us (6%)
  blocking collectives  17.1 us (6%)
  matrix products  13.7 us (5%)
  between operations  13.6 us (5%)
    all_to_all x1, waiting for transfers between devices, body(): lax.all_to_all(jnp.tile(jnp.concatenate([tokens, gain_rows], axis=0), (1,...  85.9 us
    pallas_call x1, Pallas kernels, attend_rotating(): pl.pallas_call(attention_kernel, grid=(slots // block_slots,), in_specs=[...  42.6 us
    all_to_all x1, blocking collectives, body(): weights_head = lax.all_to_all(weights_local, 'head', 1, 0, tiled=True)  17.1 us
    all_to_all x1, waiting for transfers between devices, body(): lax.all_to_all(attended.reshape(n_tok, capacity, query_width), 'tok', spl...  17 us
    all_to_all x1, waiting for transfers between devices, body(): lax.all_to_all(outgoing.reshape(n_tok, capacity, width_all), 'tok', 0, 0,...  17 us
    dot_general x1, matrix products, body(): projected = jnp.dot(normed, gathered, preferred_element_type=jnp.float32)  13.7 us
    all_to_all x1, starting transfers between devices, body(): lax.all_to_all(outgoing.reshape(n_tok, capacity, width_all), 'tok', 0, 0,...  7.27 us
    all_to_all x1, starting transfers between devices, body(): lax.all_to_all(counts_local, 'tok', 0, 0, tiled=True).reshape(n_tok)  7.04 us
  transfers between devices with their start and end apart: 5, of which 3 were waited for; matrix products, arithmetic and copies ran while one was open for 16% of the time, Pallas kernels for 0%

profile of v11, /device:TPU:32, one launch (start us, length us, event | category | flops | bytes accessed | tf_op | source)
XLA Modules:
  0.0 274.0 jit_solution(3662908966862527322)
XLA Ops:
  6.5 1.3 copy.34
  7.9 0.9 copy.35
  8.8 1.0 copy.36
  9.9 17.1 %all_to_all.40 = bf16[64,8,768]{2,0,1:T(8,128)(2,1)} all-to-all(bf16[64,8,768]{2,0,1:T(8,128)(2,1)S(1)} %pad_maximum_fusion.1), channel_id=1, replica_groups=mesh['tok'=16,'head'=8] {'head'}, dimensions={1} | all-to-all | bytes 1572864 | tf_op jit(solution)/shard_map/all_to_all | solution.py:167
  27.1 4.4 %tile.2 = bf16[528,8,1024]{2,0,1:T(8,128)(2,1)} broadcast(bf16[528,1024]{1,0:T(8,128)(2,1)S(1)} %pad_maximum_fusion), dimensions={0,2} | broadcast | bytes 9732096 | tf_op jit(solution)/shard_map/tile | solution.py:173
  31.6 6.5 %all-to-all-start = ((bf16[528,8,1024]{2,0,1:T(8,128)(2,1)}), bf16[528,8,1024]{2,0,1:T(8,128)(2,1)}, u32[]{:S(2)}, u32[]{:S(2)}) async-start(bf16[528,8,1024]{2,0,1:T(8,128)(2,1)} %tile.2), calls=%async_computation | async-start | bytes 17301504 | tf_op jit(solution)/shard_map/all_to_all | solution.py:172
  38.1 1.2 reduce-window.15
  39.6 0.7 copy.37
  40.4 1.7 gather_fusion.1
  42.1 3.2 %gather_fusion.2 = bf16[32,128,128]{2,1,0:T(8,128)(2,1)} fusion(bf16[64,128,128]{2,1,0:T(8,128)(2,1)} %bitcast.61, s32[1024]{0:T(1024)S(1)} %pad_clamp_fusion.1), kind=kCustom, calls=%fused_computation.1.clone | custom fusion | bytes 2097280 | tf_op jit(solution)/shard_map/jit(_take)/gather | solution.py:219
  45.4 2.8 %broadcast_select_fusion = (bf16[32,128,128]{2,1,0:T(8,128)(2,1)S(1)}, bf16[32,128,128]{2,1,0:T(8,128)(2,1)}) fusion(bf16[32,128,128]{2,1,0:T(8,128)(2,1)} %gather_fusion.2, pred[32]{0:T(512)(128)(4,1)S(1)} %get-tuple-element.8, bf16[32,128,128]{2,1,0:T(8,128)(2,1)} %gather_fusion.1), kind=kLoop, calls=%fused_computation.16 | loop fusion | flops 1048576 | bytes 4194336 | tf_op jit(solution)/shard_map/jit(_take)/select_n | solution.py:219
  48.2 85.9 %all-to-all-done = bf16[528,8,1024]{2,0,1:T(8,128)(2,1)} async-done(((bf16[528,8,1024]{2,0,1:T(8,128)(2,1)}), bf16[528,8,1024]{2,0,1:T(8,128)(2,1)}, u32[]{:S(2)}, u32[]{:S(2)}) %all-to-all-start) | async-done | bytes 8650784 | tf_op jit(solution)/shard_map/all_to_all | solution.py:172
  134.1 7.0 %all-to-all-start.3 = ((s32[16,1,1]{2,1,0:T(1,128)}), s32[16,1,1]{2,1,0:T(1,128)S(1)}, u32[]{:S(2)}, u32[]{:S(2)}) async-start(s32[16,1,1]{2,1,0:T(1,128)} %copy.37), calls=%async_computation.3 | async-start | bytes 16384 | tf_op jit(solution)/shard_map/all_to_all | solution.py:195
  141.2 0.9 slice_convert_fusion
  142.1 5.1 %fusion = f32[512]{0:T(512)S(1)} fusion(bf16[528,8,1024]{2,0,1:T(8,128)(2,1)} %all-to-all-done), kind=kLoop, calls=%fused_computation.6 | loop fusion | flops 12582400 | bytes 8390656 | tf_op jit(solution)/shard_map/reduce_sum | solution.py:182
  147.3 13.7 %bitcast_convert_fusion = bf16[512,768]{1,0:T(8,128)(2,1)} fusion(bf16[8,1024,1,768]{3,1,0,2:T(8,128)(2,1)} %all-gather.3.cloned.1.call-done, f32[8,1024]{1,0:T(8,128)S(1)} %bitcast.64, f32[512]{0:T(512)S(1)} %add_rsqrt_fusion, bf16[528,8,1024]{2,0,1:T(8,128)(2,1)} %all-to-all-done), kind=kOutput, calls=%fused_computation.14 | convolution fusion | flops 6459621376 | bytes 21792768 | tf_op jit(solution)/shard_map/dot_general | solution.py:187
  161.0 4.4 %scatter_custom_fusion = bf16[1024,768]{1,0:T(8,128)(2,1)} fusion(s32[512]{0:T(512)S(1)} %bitcast.67, bf16[512,768]{1,0:T(8,128)(2,1)} %bitcast_convert_fusion, bf16[]{:T(256)} %constant.20.clone.1), kind=kCustom, calls=%fused_computation.19 | custom fusion | bytes 1573376 | tf_op jit(solution)/shard_map/scatter | solution.py:197
  165.3 7.3 %all-to-all-start.2 = ((bf16[16,64,768]{2,1,0:T(8,128)(2,1)}), bf16[16,64,768]{2,1,0:T(8,128)(2,1)}, u32[]{:S(2)}, u32[]{:S(2)}) async-start(bf16[16,64,768]{2,1,0:T(8,128)(2,1)} %bitcast.59), calls=%async_computation.2 | async-start | bytes 3145728 | tf_op jit(solution)/shard_map/all_to_all | solution.py:199
  172.6 0.4 reduce.2
  173.6 0.3 reduce-window.19
  174.2 1.0 copy.38.qr_ref
  175.2 1.9 fusion.25
  177.1 1.3 pad_maximum_fusion.2
  178.4 17.0 %all-to-all-done.2 = bf16[16,64,768]{2,1,0:T(8,128)(2,1)} async-done(((bf16[16,64,768]{2,1,0:T(8,128)(2,1)}), bf16[16,64,768]{2,1,0:T(8,128)(2,1)}, u32[]{:S(2)}, u32[]{:S(2)}) %all-to-all-start.2) | async-done | bytes 1572896 | tf_op jit(solution)/shard_map/all_to_all | solution.py:199
  195.4 1.1 slice_bitcast_fusion
  196.5 2.5 fusion.24
  199.2 1.0 copy-done.5
  200.3 42.6 %shard_map.91 = bf16[1024,512]{1,0:T(8,128)(2,1)S(1)} custom-call(bf16[1024,768]{1,0:T(8,128)(2,1)} %bitcast.10.q_ref.vn_ref, f32[1024,128]{1,0:T(8,128)S(1)} %copy-done.3, f32[1024,128]{1,0:T(8,128)S(1)} %copy-done.4, s32[1024,1]{1,0:T(8,128)S(1)} %copy-done.5, bf16[4096,128]{1,0:T(8,128)(2,1)S(1)} %bitcast.56, bf16[4096,128]{1,0:T(8,128)(2,1)S(1)} %bitcast.55, ...), custom_call_target="tpu_custom_call" | custom-call | tf_op jit(solution)/shard_map/pallas_call | solution.py:129
  242.9 1.0 copy-done.2
  243.9 3.7 %all-to-all-start.4 = ((bf16[16,64,512]{2,1,0:T(8,128)(2,1)}), bf16[16,64,512]{2,1,0:T(8,128)(2,1)S(1)}, u32[]{:S(2)}, u32[]{:S(2)}) async-start(bf16[16,64,512]{2,1,0:T(8,128)(2,1)} %bitcast.57), calls=%async_computation.4 | async-start | bytes 2097152 | tf_op jit(solution)/shard_map/all_to_all | solution.py:233
  247.6 17.0 %all-to-all-done.4 = bf16[16,64,512]{2,1,0:T(8,128)(2,1)S(1)} async-done(((bf16[16,64,512]{2,1,0:T(8,128)(2,1)}), bf16[16,64,512]{2,1,0:T(8,128)(2,1)S(1)}, u32[]{:S(2)}, u32[]{:S(2)}) %all-to-all-start.4) | async-done | bytes 1048608 | tf_op jit(solution)/shard_map/all_to_all | solution.py:233
  264.6 2.6 gather_fusion
  (54 shorter events, 1.8 us)
Async XLA Ops:
  6.5 33.9 %copy-start = (bf16[64,128,1,128]{3,1,2,0:T(8,128)(2,1)S(1)}, bf16[64,128,1,128]{3,1,2,0:T(8,128)(2,1)}, u32[]{:S(2)}) copy-start(bf16[64,128,1,128]{3,1,2,0:T(8,128)(2,1)} %param.17) | copy-start | bytes 6291460
  6.5 140.7 %all-gather.3.cloned.1.call-start = ((), (), s32[]{:S(2)}) async-start(), calls=%async_computation.5 | async-start | bytes 13369344 | tf_op jit(solution)/shard_map/all_gather | solution.py:169
  8.8 18.2 %copy-start.8 = (bf16[1024]{0:T(1024)(128)(2,1)S(1)}, bf16[1024]{0:T(1024)(128)(2,1)}, u32[]{:S(2)}) copy-start(bf16[1024]{0:T(1024)(128)(2,1)} %param.12) | copy-start | bytes 6148
  8.8 18.2 %copy-start.6 = (bf16[512,1024]{1,0:T(8,128)(2,1)S(1)}, bf16[512,1024]{1,0:T(8,128)(2,1)}, u32[]{:S(2)}) copy-start(bf16[512,1024]{1,0:T(8,128)(2,1)} %param.11) | copy-start | bytes 3145732
  31.6 6.5 %copy-start.7 = (s32[512,1]{0,1:T(1,128)S(1)}, s32[512,1]{0,1:T(1,128)}, u32[]{:S(2)}) copy-start(s32[512,1]{0,1:T(1,128)} %param.16) | copy-start | bytes 6148
  31.6 8.8 %copy-start.9 = (s32[1,32]{1,0:T(1,128)S(1)}, s32[1,32]{1,0:T(1,128)}, u32[]{:S(2)}) copy-start(s32[1,32]{1,0:T(1,128)} %param.19) | copy-start | bytes 388
  31.6 102.5 %all-to-all-start = ((bf16[528,8,1024]{2,0,1:T(8,128)(2,1)}), bf16[528,8,1024]{2,0,1:T(8,128)(2,1)}, u32[]{:S(2)}, u32[]{:S(2)}) async-start(bf16[528,8,1024]{2,0,1:T(8,128)(2,1)} %tile.2), calls=%async_computation | async-start | bytes 17301504 | tf_op jit(solution)/shard_map/all_to_all | solution.py:172
  134.1 31.2 %all-to-all-start.3 = ((s32[16,1,1]{2,1,0:T(1,128)}), s32[16,1,1]{2,1,0:T(1,128)S(1)}, u32[]{:S(2)}, u32[]{:S(2)}) async-start(s32[16,1,1]{2,1,0:T(1,128)} %copy.37), calls=%async_computation.3 | async-start | bytes 16384 | tf_op jit(solution)/shard_map/all_to_all | solution.py:195
  165.3 30.1 %all-to-all-start.2 = ((bf16[16,64,768]{2,1,0:T(8,128)(2,1)}), bf16[16,64,768]{2,1,0:T(8,128)(2,1)}, u32[]{:S(2)}, u32[]{:S(2)}) async-start(bf16[16,64,768]{2,1,0:T(8,128)(2,1)} %bitcast.59), calls=%async_computation.2 | async-start | bytes 3145728 | tf_op jit(solution)/shard_map/all_to_all | solution.py:199
  195.4 3.8 %copy-start.1 = (bf16[32,128,128]{2,1,0:T(8,128)(2,1)S(1)}, bf16[32,128,128]{2,1,0:T(8,128)(2,1)}, u32[]{:S(2)}) copy-start(bf16[32,128,128]{2,1,0:T(8,128)(2,1)} %get-tuple-element.18) | copy-start | bytes 3145732
  195.4 3.8 %copy-start.3 = (f32[1024,128]{1,0:T(8,128)S(1)}, f32[1024,128]{1,0:T(8,128)}, u32[]{:S(2)}) copy-start(f32[1024,128]{1,0:T(8,128)} %get-tuple-element.19.cos_ref) | copy-start | bytes 1572868
  195.4 3.8 %copy-start.4 = (f32[1024,128]{1,0:T(8,128)S(1)}, f32[1024,128]{1,0:T(8,128)}, u32[]{:S(2)}) copy-start(f32[1024,128]{1,0:T(8,128)} %get-tuple-element.20.sin_ref) | copy-start | bytes 1572868
  199.2 1.0 copy-start.5
  242.9 1.0 copy-start.2
  243.9 20.7 %all-to-all-start.4 = ((bf16[16,64,512]{2,1,0:T(8,128)(2,1)}), bf16[16,64,512]{2,1,0:T(8,128)(2,1)S(1)}, u32[]{:S(2)}, u32[]{:S(2)}) async-start(bf16[16,64,512]{2,1,0:T(8,128)(2,1)} %bitcast.57), calls=%async_computation.4 | async-start | bytes 2097152 | tf_op jit(solution)/shard_map/all_to_all | solution.py:233
Sparse Core Ops, SparseCore 0:
  27.2 90.1 all-gather.2

commit v12 on v11

--- a/solution.py
+++ b/solution.py
@@ -166,8 +166,16 @@
     weights_local = jnp.concatenate([w_query, w_key, w_value], axis=2)
     weights_head = lax.all_to_all(weights_local, "head", 1, 0, tiled=True)
     weights_head = weights_head.reshape(n_head, -1, weights_head.shape[-1])
-    gathered = lax.all_gather(weights_head, "tok", axis=1, tiled=True)
-    gathered = gathered.reshape(-1, gathered.shape[-1])
+    group_of = group_ids[:, 0]
+    member = (group_of[:, None] == jnp.arange(n_tok, dtype=jnp.int32)[None, :]).astype(jnp.int32)
+    count_slab = jnp.zeros((1,) + weights_head.shape[1:], jnp.bfloat16)
+    count_slab = count_slab.at[0, 0, :n_tok].set(jnp.sum(member, axis=0).astype(jnp.bfloat16))
+    gathered_all = lax.all_gather(
+        jnp.concatenate([weights_head, count_slab], axis=0), "tok", axis=1, tiled=True
+    )
+    block_counts = gathered_all[n_head, :: weights_head.shape[1], lax.axis_index("tok")]
+    block_counts = block_counts.astype(jnp.int32)
+    gathered = gathered_all[:n_head].reshape(-1, gathered_all.shape[-1])
     gain_rows = jnp.broadcast_to(gain[None, :], (16, gain.shape[0]))
     stacked = lax.all_to_all(
         jnp.tile(jnp.concatenate([tokens, gain_rows], axis=0), (1, n_head)),
@@ -187,12 +195,8 @@
     projected = jnp.dot(normed, gathered, preferred_element_type=jnp.float32)
     projected_low = projected.astype(jnp.bfloat16)
     width_all = projected_low.shape[1]
-    group_of = group_ids[:, 0]
-    member = (group_of[:, None] == jnp.arange(n_tok, dtype=jnp.int32)[None, :]).astype(jnp.int32)
     local_rank = jnp.sum((jnp.cumsum(member, axis=0) - member) * member, axis=1)
     slot_index = group_of * capacity + local_rank
-    counts_local = jnp.sum(member, axis=0).reshape(n_tok, 1)
-    block_counts = lax.all_to_all(counts_local, "tok", 0, 0, tiled=True).reshape(n_tok)
     outgoing = (
         jnp.zeros((n_tok * capacity, width_all), jnp.bfloat16).at[slot_index].set(projected_low)
     )

time: 276 us -> 274 us (level)
  blocking collectives: 17.1 us -> 0 us
  waiting for transfers between devices: 120 us -> 132 us
    all_to_all x1 -> x0, blocking collectives: 17.1 us -> none  [body(): weights_head = lax.all_to_all(weights_local, 'head', 1, 0, tiled=True)]
    all_to_all x1, waiting for transfers between devices: 0.01 us -> 10.1 us  [body(): weights_head = lax.all_to_all(weights_local, 'head', 1, 0, tiled=True)]
  transfers between devices with their start and end apart: 5 -> 5, of which waited for: 3 -> 4; matrix products, arithmetic and copies ran while one was open for 16% -> 10% of each run, Pallas kernels for 0% -> 0%
where the time goes in v12:
time: 274 us; the launch traced here: 272 us
  waiting for transfers between devices  132 us (48%)
  Pallas kernels  42.6 us (16%)
  local copies, waits for them, and re-layouts  26.2 us (10%)
  starting transfers between devices  22.9 us (8%)
  other arithmetic  19.8 us (7%)
  matrix products  14.6 us (5%)
  between operations  13.6 us (5%)
    all_to_all x1, waiting for transfers between devices, body(): lax.all_to_all(jnp.tile(jnp.concatenate([tokens, gain_rows], axis=0), (1,...  88.2 us
    pallas_call x1, Pallas kernels, attend_rotating(): pl.pallas_call(attention_kernel, grid=(slots // block_slots,), in_specs=[...  42.6 us
    all_to_all x1, waiting for transfers between devices, body(): lax.all_to_all(outgoing.reshape(n_tok, capacity, width_all), 'tok', 0, 0,...  17.3 us
    all_to_all x1, waiting for transfers between devices, body(): lax.all_to_all(attended.reshape(n_tok, capacity, query_width), 'tok', spl...  16.9 us
    dot_general x1, matrix products, body(): projected = jnp.dot(normed, gathered, preferred_element_type=jnp.float32)  14.6 us
    all_to_all x1, waiting for transfers between devices, body(): weights_head = lax.all_to_all(weights_local, 'head', 1, 0, tiled=True)  10.1 us
    all_to_all x1, starting transfers between devices, body(): lax.all_to_all(outgoing.reshape(n_tok, capacity, width_all), 'tok', 0, 0,...  7.1 us
    all_to_all x1, starting transfers between devices, body(): lax.all_to_all(jnp.tile(jnp.concatenate([tokens, gain_rows], axis=0), (1,...  6.55 us
  transfers between devices with their start and end apart: 5, of which 4 were waited for; matrix products, arithmetic and copies ran while one was open for 10% of the time, Pallas kernels for 0%

profile of v12, /device:TPU:32, one launch (start us, length us, event | category | flops | bytes accessed | tf_op | source)
XLA Modules:
  0.0 272.2 jit_solution(13459076707799056835)
XLA Ops:
  6.5 1.1 copy.22
  7.6 0.9 copy.21
  8.6 1.2 copy.20
  9.8 1.0 pad_maximum_fusion.1
  10.7 5.5 %all-to-all-start.1 = ((bf16[64,8,768]{2,0,1:T(8,128)(2,1)}), bf16[64,8,768]{2,0,1:T(8,128)(2,1)S(1)}, u32[]{:S(2)}, u32[]{:S(2)}) async-start(bf16[64,8,768]{2,0,1:T(8,128)(2,1)} %pad_maximum_fusion.1), calls=%async_computation.1 | async-start | bytes 1572864 | tf_op jit(solution)/shard_map/all_to_all | solution.py:167
  16.3 1.2 reduce-window.15
  17.9 10.1 %all-to-all-done.1 = bf16[64,8,768]{2,0,1:T(8,128)(2,1)S(1)} async-done(((bf16[64,8,768]{2,0,1:T(8,128)(2,1)}), bf16[64,8,768]{2,0,1:T(8,128)(2,1)S(1)}, u32[]{:S(2)}, u32[]{:S(2)}) %all-to-all-start.1) | async-done | bytes 786464 | tf_op jit(solution)/shard_map/all_to_all | solution.py:167
  27.9 1.0 fusion.14
  29.0 1.3 pad_maximum_fusion
  30.3 4.5 %tile.2 = bf16[528,8,1024]{2,0,1:T(8,128)(2,1)} broadcast(bf16[528,1024]{1,0:T(8,128)(2,1)S(1)} %pad_maximum_fusion), dimensions={0,2} | broadcast | bytes 9732096 | tf_op jit(solution)/shard_map/tile | solution.py:181
  34.8 6.6 %all-to-all-start = ((bf16[528,8,1024]{2,0,1:T(8,128)(2,1)}), bf16[528,8,1024]{2,0,1:T(8,128)(2,1)}, u32[]{:S(2)}, u32[]{:S(2)}) async-start(bf16[528,8,1024]{2,0,1:T(8,128)(2,1)} %tile.2), calls=%async_computation | async-start | bytes 17301504 | tf_op jit(solution)/shard_map/all_to_all | solution.py:180
  41.5 1.7 gather_fusion.3
  43.1 3.2 %gather_fusion.2 = bf16[32,128,128]{2,1,0:T(8,128)(2,1)} fusion(bf16[64,128,128]{2,1,0:T(8,128)(2,1)} %bitcast.61, s32[1024]{0:T(1024)S(1)} %pad_clamp_fusion.1), kind=kCustom, calls=%fused_computation.clone | custom fusion | bytes 2097280 | tf_op jit(solution)/shard_map/jit(_take)/gather | solution.py:220
  46.4 2.8 %broadcast_select_fusion = (bf16[32,128,128]{2,1,0:T(8,128)(2,1)S(1)}, bf16[32,128,128]{2,1,0:T(8,128)(2,1)}) fusion(bf16[32,128,128]{2,1,0:T(8,128)(2,1)} %gather_fusion.3, pred[32]{0:T(512)(128)(4,1)S(1)} %get-tuple-element.20, bf16[32,128,128]{2,1,0:T(8,128)(2,1)} %gather_fusion.2), kind=kLoop, calls=%fused_computation.19 | loop fusion | flops 1048576 | bytes 4194336 | tf_op jit(solution)/shard_map/jit(_take)/select_n | solution.py:223
  49.3 88.2 %all-to-all-done = bf16[528,8,1024]{2,0,1:T(8,128)(2,1)} async-done(((bf16[528,8,1024]{2,0,1:T(8,128)(2,1)}), bf16[528,8,1024]{2,0,1:T(8,128)(2,1)}, u32[]{:S(2)}, u32[]{:S(2)}) %all-to-all-start) | async-done | bytes 8650784 | tf_op jit(solution)/shard_map/all_to_all | solution.py:180
  138.4 5.1 %fusion = f32[512]{0:T(512)S(1)} fusion(bf16[528,8,1024]{2,0,1:T(8,128)(2,1)} %all-to-all-done), kind=kLoop, calls=%fused_computation.7 | loop fusion | flops 12582400 | bytes 8390656 | tf_op jit(solution)/shard_map/reduce_sum | solution.py:190
  143.5 14.6 %bitcast_convert_fusion = bf16[512,768]{1,0:T(8,128)(2,1)} fusion(bf16[9,1024,768]{2,1,0:T(8,128)(2,1)} %all-gather.2.cloned.1.call-done, f32[8,1024]{1,0:T(8,128)S(1)} %bitcast.64, f32[512]{0:T(512)S(1)} %add_rsqrt_fusion, bf16[528,8,1024]{2,0,1:T(8,128)(2,1)} %all-to-all-done), kind=kOutput, calls=%fused_computation.17 | convolution fusion | flops 6459621376 | bytes 21792768 | tf_op jit(solution)/shard_map/dot_general | solution.py:195
  158.1 4.4 %scatter_custom_fusion = bf16[1024,768]{1,0:T(8,128)(2,1)} fusion(s32[512]{0:T(512)S(1)} %bitcast.67, bf16[512,768]{1,0:T(8,128)(2,1)} %bitcast_convert_fusion, bf16[]{:T(256)} %constant.70.clone.1), kind=kCustom, calls=%fused_computation.23 | custom fusion | bytes 1573376 | tf_op jit(solution)/shard_map/scatter | solution.py:201
  162.4 7.1 %all-to-all-start.2 = ((bf16[16,64,768]{2,1,0:T(8,128)(2,1)}), bf16[16,64,768]{2,1,0:T(8,128)(2,1)}, u32[]{:S(2)}, u32[]{:S(2)}) async-start(bf16[16,64,768]{2,1,0:T(8,128)(2,1)} %bitcast.59), calls=%async_computation.2 | async-start | bytes 3145728 | tf_op jit(solution)/shard_map/all_to_all | solution.py:203
  169.6 1.4 gather_fusion
  172.1 1.0 copy.23.qr_ref
  173.1 1.9 fusion.27
  175.0 1.3 pad_maximum_fusion.2
  176.4 17.3 %all-to-all-done.2 = bf16[16,64,768]{2,1,0:T(8,128)(2,1)} async-done(((bf16[16,64,768]{2,1,0:T(8,128)(2,1)}), bf16[16,64,768]{2,1,0:T(8,128)(2,1)}, u32[]{:S(2)}, u32[]{:S(2)}) %all-to-all-start.2) | async-done | bytes 1572896 | tf_op jit(solution)/shard_map/all_to_all | solution.py:203
  193.7 1.1 slice_bitcast_fusion
  194.8 2.5 fusion.26
  197.5 1.0 copy-done.5
  198.5 42.6 %shard_map.91 = bf16[1024,512]{1,0:T(8,128)(2,1)S(1)} custom-call(bf16[1024,768]{1,0:T(8,128)(2,1)} %bitcast.11.q_ref.vn_ref, f32[1024,128]{1,0:T(8,128)S(1)} %copy-done.3, f32[1024,128]{1,0:T(8,128)S(1)} %copy-done.4, s32[1024,1]{1,0:T(8,128)S(1)} %copy-done.5, bf16[4096,128]{1,0:T(8,128)(2,1)S(1)} %bitcast.56, bf16[4096,128]{1,0:T(8,128)(2,1)S(1)} %bitcast.55, ...), custom_call_target="tpu_custom_call" | custom-call | tf_op jit(solution)/shard_map/pallas_call | solution.py:129
  241.1 1.0 copy-done.2
  242.1 3.7 %all-to-all-start.3 = ((bf16[16,64,512]{2,1,0:T(8,128)(2,1)}), bf16[16,64,512]{2,1,0:T(8,128)(2,1)S(1)}, u32[]{:S(2)}, u32[]{:S(2)}) async-start(bf16[16,64,512]{2,1,0:T(8,128)(2,1)} %bitcast.57), calls=%async_computation.3 | async-start | bytes 2097152 | tf_op jit(solution)/shard_map/all_to_all | solution.py:237
  245.8 16.9 %all-to-all-done.3 = bf16[16,64,512]{2,1,0:T(8,128)(2,1)S(1)} async-done(((bf16[16,64,512]{2,1,0:T(8,128)(2,1)}), bf16[16,64,512]{2,1,0:T(8,128)(2,1)S(1)}, u32[]{:S(2)}, u32[]{:S(2)}) %all-to-all-start.3) | async-done | bytes 1048608 | tf_op jit(solution)/shard_map/all_to_all | solution.py:237
  262.7 2.6 gather_fusion.1
  (54 shorter events, 2.9 us)
Async XLA Ops:
  6.5 34.9 %copy-start = (bf16[64,128,1,128]{3,1,2,0:T(8,128)(2,1)S(1)}, bf16[64,128,1,128]{3,1,2,0:T(8,128)(2,1)}, u32[]{:S(2)}) copy-start(bf16[64,128,1,128]{3,1,2,0:T(8,128)(2,1)} %param.20) | copy-start | bytes 6291460
  8.5 7.7 %copy-start.6 = (s32[512,1]{0,1:T(1,128)S(1)}, s32[512,1]{0,1:T(1,128)}, u32[]{:S(2)}) copy-start(s32[512,1]{0,1:T(1,128)} %param.18) | copy-start | bytes 6148
  10.7 18.2 %copy-start.7 = (bf16[1024]{0:T(1024)(128)(2,1)S(1)}, bf16[1024]{0:T(1024)(128)(2,1)}, u32[]{:S(2)}) copy-start(bf16[1024]{0:T(1024)(128)(2,1)} %param.14) | copy-start | bytes 6148
  10.7 17.2 %all-to-all-start.1 = ((bf16[64,8,768]{2,0,1:T(8,128)(2,1)}), bf16[64,8,768]{2,0,1:T(8,128)(2,1)S(1)}, u32[]{:S(2)}, u32[]{:S(2)}) async-start(bf16[64,8,768]{2,0,1:T(8,128)(2,1)} %pad_maximum_fusion.1), calls=%async_computation.1 | async-start | bytes 1572864 | tf_op jit(solution)/shard_map/all_to_all | solution.py:167
  16.3 127.2 %all-gather.2.cloned.1.call-start = ((), (), s32[]{:S(2)}) async-start(), calls=%async_computation.4 | async-start | bytes 15040512 | tf_op jit(solution)/shard_map/all_gather | solution.py:173
  34.8 6.6 %copy-start.8 = (s32[1,32]{1,0:T(1,128)S(1)}, s32[1,32]{1,0:T(1,128)}, u32[]{:S(2)}) copy-start(s32[1,32]{1,0:T(1,128)} %param.21) | copy-start | bytes 388
  34.8 102.6 %all-to-all-start = ((bf16[528,8,1024]{2,0,1:T(8,128)(2,1)}), bf16[528,8,1024]{2,0,1:T(8,128)(2,1)}, u32[]{:S(2)}, u32[]{:S(2)}) async-start(bf16[528,8,1024]{2,0,1:T(8,128)(2,1)} %tile.2), calls=%async_computation | async-start | bytes 17301504 | tf_op jit(solution)/shard_map/all_to_all | solution.py:180
  162.4 31.2 %all-to-all-start.2 = ((bf16[16,64,768]{2,1,0:T(8,128)(2,1)}), bf16[16,64,768]{2,1,0:T(8,128)(2,1)}, u32[]{:S(2)}, u32[]{:S(2)}) async-start(bf16[16,64,768]{2,1,0:T(8,128)(2,1)} %bitcast.59), calls=%async_computation.2 | async-start | bytes 3145728 | tf_op jit(solution)/shard_map/all_to_all | solution.py:203
  193.7 3.8 %copy-start.1 = (bf16[32,128,128]{2,1,0:T(8,128)(2,1)S(1)}, bf16[32,128,128]{2,1,0:T(8,128)(2,1)}, u32[]{:S(2)}) copy-start(bf16[32,128,128]{2,1,0:T(8,128)(2,1)} %get-tuple-element.30) | copy-start | bytes 3145732
  193.7 3.8 %copy-start.3 = (f32[1024,128]{1,0:T(8,128)S(1)}, f32[1024,128]{1,0:T(8,128)}, u32[]{:S(2)}) copy-start(f32[1024,128]{1,0:T(8,128)} %get-tuple-element.31.cos_ref) | copy-start | bytes 1572868
  193.7 3.8 %copy-start.4 = (f32[1024,128]{1,0:T(8,128)S(1)}, f32[1024,128]{1,0:T(8,128)}, u32[]{:S(2)}) copy-start(f32[1024,128]{1,0:T(8,128)} %get-tuple-element.32.sin_ref) | copy-start | bytes 1572868
  197.5 1.0 copy-start.5
  241.1 1.0 copy-start.2
  242.1 20.6 %all-to-all-start.3 = ((bf16[16,64,512]{2,1,0:T(8,128)(2,1)}), bf16[16,64,512]{2,1,0:T(8,128)(2,1)S(1)}, u32[]{:S(2)}, u32[]{:S(2)}) async-start(bf16[16,64,512]{2,1,0:T(8,128)(2,1)} %bitcast.57), calls=%async_computation.3 | async-start | bytes 2097152 | tf_op jit(solution)/shard_map/all_to_all | solution.py:237
Sparse Core Ops, SparseCore 0:
  29.1 98.1 all-gather.1

commit v13 on v12

--- a/solution.py
+++ b/solution.py
@@ -197,9 +197,12 @@
     width_all = projected_low.shape[1]
     local_rank = jnp.sum((jnp.cumsum(member, axis=0) - member) * member, axis=1)
     slot_index = group_of * capacity + local_rank
-    outgoing = (
-        jnp.zeros((n_tok * capacity, width_all), jnp.bfloat16).at[slot_index].set(projected_low)
-    )
+    source_row = (
+        jnp.zeros((n_tok * capacity,), jnp.int32)
+        .at[slot_index]
+        .set(jnp.arange(row_count, dtype=jnp.int32))
+    )
+    outgoing = jnp.take(projected_low, source_row, axis=0)
     arrived = lax.all_to_all(
         outgoing.reshape(n_tok, capacity, width_all), "tok", 0, 0, tiled=True
     )

time: 274 us -> 280 us (1.022)
  local copies, waits for them, and re-layouts: 26.2 us -> 31.2 us
  other arithmetic: 19.8 us -> 22.6 us
    gather x0 -> x1, local copies, waits for them, and re-layouts: none -> 6.79 us  [body(): outgoing = jnp.take(projected_low, source_row, axis=0)]
  transfers between devices with their start and end apart: 5 -> 5, of which waited for: 4 -> 4; matrix products, arithmetic and copies ran while one was open for 10% -> 11% of each run, Pallas kernels for 0% -> 0%
where the time goes in v13:
time: 280 us; the launch traced here: 277 us
  waiting for transfers between devices  130 us (46%)
  Pallas kernels  42.6 us (15%)
  local copies, waits for them, and re-layouts  31.2 us (11%)
  starting transfers between devices  22.9 us (8%)
  other arithmetic  22.6 us (8%)
  matrix products  14.6 us (5%)
  between operations  13.6 us (5%)
    all_to_all x1, waiting for transfers between devices, body(): lax.all_to_all(jnp.tile(jnp.concatenate([tokens, gain_rows], axis=0), (1,...  85.6 us
    pallas_call x1, Pallas kernels, attend_rotating(): pl.pallas_call(attention_kernel, grid=(slots // block_slots,), in_specs=[...  42.6 us
    all_to_all x1, waiting for transfers between devices, body(): lax.all_to_all(outgoing.reshape(n_tok, capacity, width_all), 'tok', 0, 0,...  17.3 us
    all_to_all x1, waiting for transfers between devices, body(): lax.all_to_all(attended.reshape(n_tok, capacity, query_width), 'tok', spl...  16.9 us
    dot_general x1, matrix products, body(): projected = jnp.dot(normed, gathered, preferred_element_type=jnp.float32)  14.6 us
    all_to_all x1, waiting for transfers between devices, body(): weights_head = lax.all_to_all(weights_local, 'head', 1, 0, tiled=True)  10.1 us
    all_to_all x1, starting transfers between devices, body(): lax.all_to_all(outgoing.reshape(n_tok, capacity, width_all), 'tok', 0, 0,...  7.1 us
    gather x1, local copies, waits for them, and re-layouts, body(): outgoing = jnp.take(projected_low, source_row, axis=0)  6.79 us
  transfers between devices with their start and end apart: 5, of which 4 were waited for; matrix products, arithmetic and copies ran while one was open for 11% of the time, Pallas kernels for 0%

profile of v13, /device:TPU:32, one launch (start us, length us, event | category | flops | bytes accessed | tf_op | source)
XLA Modules:
  0.0 277.3 jit_solution(1136232854539734722)
XLA Ops:
  6.5 1.1 copy.22
  8.6 1.2 copy.20
  10.7 5.5 %all-to-all-start.1 = ((bf16[64,8,768]{2,0,1:T(8,128)(2,1)}), bf16[64,8,768]{2,0,1:T(8,128)(2,1)S(1)}, u32[]{:S(2)}, u32[]{:S(2)}) async-start(bf16[64,8,768]{2,0,1:T(8,128)(2,1)} %pad_maximum_fusion.1), calls=%async_computation.1 | async-start | bytes 1572864 | tf_op jit(solution)/shard_map/all_to_all | solution.py:167
  16.3 1.2 reduce-window.15
  17.9 10.1 %all-to-all-done.1 = bf16[64,8,768]{2,0,1:T(8,128)(2,1)S(1)} async-done(((bf16[64,8,768]{2,0,1:T(8,128)(2,1)}), bf16[64,8,768]{2,0,1:T(8,128)(2,1)S(1)}, u32[]{:S(2)}, u32[]{:S(2)}) %all-to-all-start.1) | async-done | bytes 786464 | tf_op jit(solution)/shard_map/all_to_all | solution.py:167
  27.9 1.0 fusion.14
  29.0 1.3 pad_maximum_fusion
  30.3 4.5 %tile.2 = bf16[528,8,1024]{2,0,1:T(8,128)(2,1)} broadcast(bf16[528,1024]{1,0:T(8,128)(2,1)S(1)} %pad_maximum_fusion), dimensions={0,2} | broadcast | bytes 9732096 | tf_op jit(solution)/shard_map/tile | solution.py:181
  34.8 6.6 %all-to-all-start = ((bf16[528,8,1024]{2,0,1:T(8,128)(2,1)}), bf16[528,8,1024]{2,0,1:T(8,128)(2,1)}, u32[]{:S(2)}, u32[]{:S(2)}) async-start(bf16[528,8,1024]{2,0,1:T(8,128)(2,1)} %tile.2), calls=%async_computation | async-start | bytes 17301504 | tf_op jit(solution)/shard_map/all_to_all | solution.py:180
  41.4 2.4 scatter_custom_fusion
  44.0 1.7 gather_fusion.4
  45.7 3.3 %gather_fusion.3 = bf16[32,128,128]{2,1,0:T(8,128)(2,1)} fusion(bf16[64,128,128]{2,1,0:T(8,128)(2,1)} %bitcast.61, s32[1024]{0:T(1024)S(1)} %pad_clamp_fusion.1), kind=kCustom, calls=%fused_computation.clone | custom fusion | bytes 2097280 | tf_op jit(solution)/shard_map/jit(_take)/gather | solution.py:223
  49.0 2.8 %broadcast_select_fusion.1 = (bf16[32,128,128]{2,1,0:T(8,128)(2,1)S(1)}, bf16[32,128,128]{2,1,0:T(8,128)(2,1)}) fusion(bf16[32,128,128]{2,1,0:T(8,128)(2,1)} %gather_fusion.4, pred[32]{0:T(512)(128)(4,1)S(1)} %get-tuple-element.20, bf16[32,128,128]{2,1,0:T(8,128)(2,1)} %gather_fusion.3), kind=kLoop, calls=%fused_computation.21 | loop fusion | flops 1048576 | bytes 4194336 | tf_op jit(solution)/shard_map/jit(_take)/select_n | solution.py:226
  51.9 85.6 %all-to-all-done = bf16[528,8,1024]{2,0,1:T(8,128)(2,1)} async-done(((bf16[528,8,1024]{2,0,1:T(8,128)(2,1)}), bf16[528,8,1024]{2,0,1:T(8,128)(2,1)}, u32[]{:S(2)}, u32[]{:S(2)}) %all-to-all-start) | async-done | bytes 8650784 | tf_op jit(solution)/shard_map/all_to_all | solution.py:180
  138.4 5.1 %fusion = f32[512]{0:T(512)S(1)} fusion(bf16[528,8,1024]{2,0,1:T(8,128)(2,1)} %all-to-all-done), kind=kLoop, calls=%fused_computation.8 | loop fusion | flops 12582400 | bytes 8390656 | tf_op jit(solution)/shard_map/reduce_sum | solution.py:190
  143.5 14.6 %bitcast_convert_fusion = bf16[512,768]{1,0:T(8,128)(2,1)} fusion(bf16[9,1024,768]{2,1,0:T(8,128)(2,1)} %all-gather.2.cloned.1.call-done, f32[8,1024]{1,0:T(8,128)S(1)} %bitcast.64, f32[512]{0:T(512)S(1)} %add_rsqrt_fusion, bf16[528,8,1024]{2,0,1:T(8,128)(2,1)} %all-to-all-done), kind=kOutput, calls=%fused_computation.18 | convolution fusion | flops 6459621376 | bytes 21792768 | tf_op jit(solution)/shard_map/dot_general | solution.py:195
  158.1 6.8 %gather_fusion = bf16[1024,768]{1,0:T(8,128)(2,1)} fusion(bf16[512,768]{1,0:T(8,128)(2,1)} %bitcast_convert_fusion, s32[1024]{0:T(1024)S(1)} %fusion.32), kind=kCustom, calls=%fused_computation.2 | custom fusion | bytes 3149824 | tf_op jit(solution)/shard_map/jit(_take)/gather | solution.py:205
  164.9 2.8 %broadcast_select_fusion = bf16[16,64,768]{2,1,0:T(8,128)(2,1)} fusion(bf16[16,64,768]{2,1,0:T(8,128)(2,1)} %bitcast.59, pred[16,64]{1,0:T(8,128)(4,1)S(1)} %broadcast_in_dim.30), kind=kLoop, calls=%fused_computation.19 | loop fusion | flops 786432 | bytes 3146752 | tf_op jit(solution)/shard_map/jit(_take)/select_n | solution.py:205
  167.6 7.1 %all-to-all-start.2 = ((bf16[16,64,768]{2,1,0:T(8,128)(2,1)}), bf16[16,64,768]{2,1,0:T(8,128)(2,1)}, u32[]{:S(2)}, u32[]{:S(2)}) async-start(bf16[16,64,768]{2,1,0:T(8,128)(2,1)} %broadcast_select_fusion), calls=%async_computation.2 | async-start | bytes 3145728 | tf_op jit(solution)/shard_map/all_to_all | solution.py:206
  174.8 1.4 gather_fusion.1
  177.3 1.0 copy.23.qr_ref
  178.3 1.9 fusion.25
  180.2 1.3 pad_maximum_fusion.2
  181.6 17.3 %all-to-all-done.2 = bf16[16,64,768]{2,1,0:T(8,128)(2,1)} async-done(((bf16[16,64,768]{2,1,0:T(8,128)(2,1)}), bf16[16,64,768]{2,1,0:T(8,128)(2,1)}, u32[]{:S(2)}, u32[]{:S(2)}) %all-to-all-start.2) | async-done | bytes 1572896 | tf_op jit(solution)/shard_map/all_to_all | solution.py:206
  198.9 1.1 slice_bitcast_fusion
  200.0 2.5 fusion.24
  202.7 1.0 copy-done.5
  203.7 42.6 %shard_map.91 = bf16[1024,512]{1,0:T(8,128)(2,1)S(1)} custom-call(bf16[1024,768]{1,0:T(8,128)(2,1)} %bitcast.11.q_ref.vn_ref, f32[1024,128]{1,0:T(8,128)S(1)} %copy-done.3, f32[1024,128]{1,0:T(8,128)S(1)} %copy-done.4, s32[1024,1]{1,0:T(8,128)S(1)} %copy-done.5, bf16[4096,128]{1,0:T(8,128)(2,1)S(1)} %bitcast.56, bf16[4096,128]{1,0:T(8,128)(2,1)S(1)} %bitcast.55, ...), custom_call_target="tpu_custom_call" | custom-call | tf_op jit(solution)/shard_map/pallas_call | solution.py:129
  246.3 1.0 copy-done.2
  247.3 3.7 %all-to-all-start.3 = ((bf16[16,64,512]{2,1,0:T(8,128)(2,1)}), bf16[16,64,512]{2,1,0:T(8,128)(2,1)S(1)}, u32[]{:S(2)}, u32[]{:S(2)}) async-start(bf16[16,64,512]{2,1,0:T(8,128)(2,1)} %bitcast.57), calls=%async_computation.3 | async-start | bytes 2097152 | tf_op jit(solution)/shard_map/all_to_all | solution.py:240
  251.0 16.9 %all-to-all-done.3 = bf16[16,64,512]{2,1,0:T(8,128)(2,1)S(1)} async-done(((bf16[16,64,512]{2,1,0:T(8,128)(2,1)}), bf16[16,64,512]{2,1,0:T(8,128)(2,1)S(1)}, u32[]{:S(2)}, u32[]{:S(2)}) %all-to-all-start.3) | async-done | bytes 1048608 | tf_op jit(solution)/shard_map/all_to_all | solution.py:240
  267.9 2.6 gather_fusion.2
  (60 shorter events, 4.8 us)
Async XLA Ops:
  6.5 37.5 %copy-start = (bf16[64,128,1,128]{3,1,2,0:T(8,128)(2,1)S(1)}, bf16[64,128,1,128]{3,1,2,0:T(8,128)(2,1)}, u32[]{:S(2)}) copy-start(bf16[64,128,1,128]{3,1,2,0:T(8,128)(2,1)} %param.20) | copy-start | bytes 6291460
  8.5 7.7 %copy-start.6 = (s32[512,1]{0,1:T(1,128)S(1)}, s32[512,1]{0,1:T(1,128)}, u32[]{:S(2)}) copy-start(s32[512,1]{0,1:T(1,128)} %param.18) | copy-start | bytes 6148
  10.7 18.2 %copy-start.7 = (bf16[1024]{0:T(1024)(128)(2,1)S(1)}, bf16[1024]{0:T(1024)(128)(2,1)}, u32[]{:S(2)}) copy-start(bf16[1024]{0:T(1024)(128)(2,1)} %param.14) | copy-start | bytes 6148
  10.7 17.2 %all-to-all-start.1 = ((bf16[64,8,768]{2,0,1:T(8,128)(2,1)}), bf16[64,8,768]{2,0,1:T(8,128)(2,1)S(1)}, u32[]{:S(2)}, u32[]{:S(2)}) async-start(bf16[64,8,768]{2,0,1:T(8,128)(2,1)} %pad_maximum_fusion.1), calls=%async_computation.1 | async-start | bytes 1572864 | tf_op jit(solution)/shard_map/all_to_all | solution.py:167
  16.3 127.2 %all-gather.2.cloned.1.call-start = ((), (), s32[]{:S(2)}) async-start(), calls=%async_computation.4 | async-start | bytes 15040512 | tf_op jit(solution)/shard_map/all_gather | solution.py:173
  34.8 9.2 %copy-start.8 = (s32[1,32]{1,0:T(1,128)S(1)}, s32[1,32]{1,0:T(1,128)}, u32[]{:S(2)}) copy-start(s32[1,32]{1,0:T(1,128)} %param.21) | copy-start | bytes 388
  34.8 102.6 %all-to-all-start = ((bf16[528,8,1024]{2,0,1:T(8,128)(2,1)}), bf16[528,8,1024]{2,0,1:T(8,128)(2,1)}, u32[]{:S(2)}, u32[]{:S(2)}) async-start(bf16[528,8,1024]{2,0,1:T(8,128)(2,1)} %tile.2), calls=%async_computation | async-start | bytes 17301504 | tf_op jit(solution)/shard_map/all_to_all | solution.py:180
  167.6 31.2 %all-to-all-start.2 = ((bf16[16,64,768]{2,1,0:T(8,128)(2,1)}), bf16[16,64,768]{2,1,0:T(8,128)(2,1)}, u32[]{:S(2)}, u32[]{:S(2)}) async-start(bf16[16,64,768]{2,1,0:T(8,128)(2,1)} %broadcast_select_fusion), calls=%async_computation.2 | async-start | bytes 3145728 | tf_op jit(solution)/shard_map/all_to_all | solution.py:206
  198.9 3.8 %copy-start.1 = (bf16[32,128,128]{2,1,0:T(8,128)(2,1)S(1)}, bf16[32,128,128]{2,1,0:T(8,128)(2,1)}, u32[]{:S(2)}) copy-start(bf16[32,128,128]{2,1,0:T(8,128)(2,1)} %get-tuple-element.30) | copy-start | bytes 3145732
  198.9 3.8 %copy-start.3 = (f32[1024,128]{1,0:T(8,128)S(1)}, f32[1024,128]{1,0:T(8,128)}, u32[]{:S(2)}) copy-start(f32[1024,128]{1,0:T(8,128)} %get-tuple-element.31.cos_ref) | copy-start | bytes 1572868
  198.9 3.8 %copy-start.4 = (f32[1024,128]{1,0:T(8,128)S(1)}, f32[1024,128]{1,0:T(8,128)}, u32[]{:S(2)}) copy-start(f32[1024,128]{1,0:T(8,128)} %get-tuple-element.32.sin_ref) | copy-start | bytes 1572868
  202.7 1.0 copy-start.5
  246.3 1.0 copy-start.2
  247.3 20.6 %all-to-all-start.3 = ((bf16[16,64,512]{2,1,0:T(8,128)(2,1)}), bf16[16,64,512]{2,1,0:T(8,128)(2,1)S(1)}, u32[]{:S(2)}, u32[]{:S(2)}) async-start(bf16[16,64,512]{2,1,0:T(8,128)(2,1)} %bitcast.57), calls=%async_computation.3 | async-start | bytes 2097152 | tf_op jit(solution)/shard_map/all_to_all | solution.py:240
Sparse Core Ops, SparseCore 0:
  29.1 98.1 all-gather.1
